TPU v7x, 128 devices: a whole 4x4x4 slice. The times are simulated.
128 devices in a mesh: cfg: 2 (over core), row: 4 (over z), col: 16 (over y, x).
Axes of the slice: x: 4, y: 4, z: 4, core: 2. Of those that a mesh axis runs over, the one named last changes fastest.
Arguments:
- img_tokens: bfloat16 [2, 16, 1024, 3072], P('cfg', 'col', None, 'row'), may hold values from -6 to 6
- txt_tokens: bfloat16 [2, 16, 512, 3072], P('cfg', 'col', None, 'row'), may hold values from -6 to 6
- img_mod: bfloat16 [2, 16, 2, 3072], P('cfg', 'col', None, 'row'), may hold values from -3 to 3
- txt_mod: bfloat16 [2, 16, 2, 3072], P('cfg', 'col', None, 'row'), may hold values from -3 to 3
- img_gate: bfloat16 [2, 16, 3072], P('cfg', 'col', 'row'), may hold values from -16 to 16
- txt_len: int32 [2, 16], P('cfg', 'col'), may hold values from 128 to 512, as said below
- img_qkv_weight: bfloat16 [3072, 3, 3072], P('col', None, 'row'), may hold values from -0.109375 to 0.109375
- txt_kv_weight: bfloat16 [3072, 2, 3072], P('col', None, 'row'), may hold values from -0.109375 to 0.109375
- out_weight: bfloat16 [3072, 3072], P('row', 'col'), may hold values from -0.109375 to 0.109375
- final_weight: bfloat16 [3072, 64], P('row'), may hold values from -0.109375 to 0.109375
- latent: float32 [16, 1024, 64], P('col', ('cfg', 'row')), may hold values from -6 to 6
- sigmas: float32 [5], replicated, may hold values from 0 to 2, as said below
- step_index: int32 [1], replicated, may hold values from 0 to 3
- guidance: float32 [1], replicated, may hold values from 1.5 to 5
Outputs:
- img_out: bfloat16 [2, 16, 1024, 3072], P('cfg', 'col', None, 'row')
- latent_next: float32 [16, 1024, 64], P('col', ('cfg', 'row'))
Inputs may be any that keep to these rules, and one draw needn't show every extreme that they name: `txt_len`: in each half some prompt has all 512 text slots live and some other prompt exactly 128. `sigmas`: falls strictly along the table.
All inputs are finite; a program needn't handle non-finite values.
Results may differ from a plain program's by a relative error of at most 0.015.
Values may be sent and summed in bfloat16 or wider, within the bound.
No kernel may reach another device: no remote copies, remote signals or barrier semaphores. Data moves between devices by JAX's collectives and lax.ppermute only.
A program may use at most 128 MiB of HBM per device.

v0:
```python
import math

import jax
import jax.numpy as jnp
from jax import lax
from jax.sharding import PartitionSpec as P

HD = 128


def rms_norm(values):
    return values * lax.rsqrt(jnp.mean(values * values, -1, keepdims=True) + 1e-06)


def shift_pairs(size, step):
    return [(i, (i + step) % size) for i in range(size)]


def ring_gather(piece, axis_name, size):
    assert size == 4
    from_prev = lax.ppermute(piece, axis_name, shift_pairs(size, 1))
    from_next = lax.ppermute(piece, axis_name, shift_pairs(size, -1))
    cut = piece.shape[0] // 2
    far_top = lax.ppermute(from_prev[:cut], axis_name, shift_pairs(size, 1))
    far_bottom = lax.ppermute(from_next[cut:], axis_name, shift_pairs(size, -1))
    far = jnp.concatenate([far_top, far_bottom], 0)
    return [piece, from_next, far, from_prev]


def modulate_blocks(blocks, mods, width):
    values = [b.astype(jnp.float32) for b in blocks]
    mean = sum(jnp.sum(v, -1, keepdims=True) for v in values) / width
    centred = [v - mean for v in values]
    spread = sum(jnp.sum(c * c, -1, keepdims=True) for c in centred) / width
    scale = lax.rsqrt(spread + 1e-06)
    out = []
    for c, m in zip(centred, mods):
        m = m.astype(jnp.float32)
        out.append(((c * scale) * (1.0 + m[1:2]) + m[0:1]).astype(jnp.bfloat16))
    return jnp.concatenate(out, -1)


def order_blocks(by_offset, me, size):
    stacked = jnp.stack(by_offset)
    return [
        lax.dynamic_index_in_dim(stacked, (k - me) % size, 0, keepdims=False) for k in range(size)
    ]


def add_rows(piece, ready):
    return jnp.dot(ready, piece.reshape(piece.shape[0], -1), preferred_element_type=jnp.float32)


def shards(
    img_tokens,
    txt_tokens,
    img_mod,
    txt_mod,
    img_gate,
    txt_len,
    img_qkv_weight,
    txt_kv_weight,
    out_weight,
    final_weight,
    latent,
    sigmas,
    step_index,
    guidance,
):
    n_row = 4
    images = img_tokens.shape[2]
    text_slots = txt_tokens.shape[2]
    local_width = img_qkv_weight.shape[2]
    width = local_width * n_row
    heads_here = local_width // HD
    me_row = lax.axis_index("row")
    core = lax.axis_index("cfg")

    img_blocks = order_blocks(ring_gather(img_tokens[0, 0], "row", n_row), me_row, n_row)
    txt_bundle = jnp.concatenate([txt_tokens[0, 0], img_mod[0, 0], txt_mod[0, 0]], 0)
    txt_blocks = order_blocks(ring_gather(txt_bundle, "row", n_row), me_row, n_row)
    img_ready = modulate_blocks(
        img_blocks, [b[text_slots : text_slots + 2] for b in txt_blocks], width
    )
    txt_ready = modulate_blocks(
        [b[:text_slots] for b in txt_blocks],
        [b[text_slots + 2 : text_slots + 4] for b in txt_blocks],
        width,
    )
    half = local_width // 2
    swap = [(0, 1), (1, 0)]

    def own_half(weight, axis):
        return lax.dynamic_slice_in_dim(weight, core * half, half, axis=axis)

    img_w = lax.all_gather(own_half(img_qkv_weight, 2), "col", axis=0, tiled=True)
    img_w, txt_piece = lax.optimization_barrier((img_w, own_half(txt_kv_weight, 2)))
    txt_w = lax.all_gather(txt_piece, "col", axis=0, tiled=True)
    txt_w, out_piece = lax.optimization_barrier((txt_w, own_half(out_weight, 0)))
    out_w = lax.all_gather(out_piece, "col", axis=1, tiled=True)
    halves = [
        (txt_w, img_w, out_w),
        tuple(lax.ppermute(w, "cfg", swap) for w in (txt_w, img_w, out_w)),
    ]
    positions = jnp.arange(text_slots + images, dtype=jnp.int32)
    usable = (positions < txt_len[0, 0]) | (positions >= text_slots)
    heads_half = half // HD

    def project(txt_w, img_w):
        img_proj = add_rows(img_w, img_ready).reshape(images, 3, heads_half, HD)
        txt_proj = add_rows(txt_w, txt_ready).reshape(text_slots, 2, heads_half, HD)
        queries = rms_norm(img_proj[:, 0]).astype(jnp.bfloat16)
        key_rows = jnp.concatenate(
            [rms_norm(txt_proj[:, 0]), rms_norm(img_proj[:, 1])], 0
        ).astype(jnp.bfloat16)
        value_rows = jnp.concatenate([txt_proj[:, 1], img_proj[:, 2]], 0).astype(jnp.bfloat16)
        return queries, key_rows, value_rows

    def attend(queries, key_rows, value_rows, out_w):
        scores = jnp.einsum(
            "qhe,khe->hqk", queries, key_rows, preferred_element_type=jnp.float32
        ) / math.sqrt(HD)
        weights = jnp.where(usable, jnp.exp(scores), 0.0)
        chances = (weights / jnp.sum(weights, -1, keepdims=True)).astype(jnp.bfloat16)
        mixed = jnp.einsum("hqk,khe->qhe", chances, value_rows, preferred_element_type=jnp.float32)
        outputs = mixed.reshape(queries.shape[0], half).astype(jnp.bfloat16)
        return jnp.einsum(
            "ti,iko->kto",
            outputs,
            out_w.reshape(half, n_row, local_width),
            preferred_element_type=jnp.float32,
        )

    projections = [project(*h[:2]) for h in halves]
    n_chunk = 2
    chunk = images // n_chunk
    pieces = []
    for c in range(n_chunk):
        part = 0.0
        for (queries, key_rows, value_rows), h in zip(projections, halves):
            part = part + attend(queries[c * chunk : (c + 1) * chunk], key_rows, value_rows, h[2])
        term_blocks = part.astype(jnp.bfloat16)
        got = lax.dynamic_index_in_dim(term_blocks, me_row, 0, keepdims=False).astype(jnp.float32)
        for step in range(1, n_row):
            outgoing = lax.dynamic_index_in_dim(term_blocks, (me_row + step) % n_row, 0, keepdims=False)
            got = got + lax.ppermute(outgoing, "row", shift_pairs(n_row, step)).astype(jnp.float32)
        pieces.append(got)
    projected = jnp.concatenate(pieces, 0)
    gating = img_gate[0].astype(jnp.float32)
    img_out = (img_tokens[0, 0].astype(jnp.float32) + gating * projected).astype(jnp.bfloat16)
    velocity = jnp.dot(img_out, final_weight, preferred_element_type=jnp.float32)
    strength = guidance[0]
    share = jnp.where(core == 1, strength, 1.0 - strength)
    weighted = velocity * share
    n_pair = 2 * n_row
    me_pair = core * n_row + me_row
    rows_each = weighted.shape[0] // n_pair
    velocity_blocks = weighted.reshape(n_pair, rows_each, weighted.shape[1])
    guided = lax.dynamic_index_in_dim(velocity_blocks, me_pair, 0, keepdims=False)
    for step in range(1, n_pair):
        outgoing = lax.dynamic_index_in_dim(velocity_blocks, (me_pair + step) % n_pair, 0, keepdims=False)
        guided = guided + lax.ppermute(outgoing, ("cfg", "row"), shift_pairs(n_pair, step))
    position_now = step_index[0]
    step_size = sigmas[position_now + 1] - sigmas[position_now]
    return (img_out[None, None], latent + step_size * guided[None])


def solution(mesh):
    return jax.shard_map(
        shards,
        mesh=mesh,
        in_specs=(
            P("cfg", "col", None, "row"),
            P("cfg", "col", None, "row"),
            P("cfg", "col", None, "row"),
            P("cfg", "col", None, "row"),
            P("cfg", "col", "row"),
            P("cfg", "col"),
            P("col", None, "row"),
            P("col", None, "row"),
            P("row", "col"),
            P("row", None),
            P("col", ("cfg", "row"), None),
            P(),
            P(),
            P(),
        ),
        out_specs=(P("cfg", "col", None, "row"), P("col", ("cfg", "row"), None)),
        check_vma=False,
    )
```

profile of v0, /device:TPU:1, one launch (start us, length us, event | category | flops | bytes accessed | tf_op | source)
XLA Modules:
  0.0 382.7 jit_solution(10232410427447516889)
XLA Ops:
  11.4 4.6 %collective-permute-start = (bf16[516,768]{1,0:T(8,128)(2,1)S(1)}, bf16[516,768]{1,0:T(8,128)(2,1)S(1)}, u32[]{:S(2)}, u32[]{:S(2)}) collective-permute-start(bf16[516,768]{1,0:T(8,128)(2,1)S(1)} %get-tuple-element.77), channel_id=1, source_target_pairs={{0,48},{16,0},{32,16},{48,32},{1,49},{17,1},{33,17},{49,33},{2,50}... | collective-permute-start | bytes 2377736 | tf_op jit(solution)/shard_map/ppermute | solution.py:22
  16.9 61.0 %all-gather.4.cloned.1.call-done = bf16[3072,3,384]{2,0,1:T(8,128)(2,1)} async-done(((bf16[192,3,384]{2,0,1:T(8,128)(2,1)}), bf16[3072,3,384]{2,0,1:T(8,128)(2,1)}) %all-gather.4.cloned.1.call-update) | async-done | bytes 7077904 | tf_op jit(solution)/shard_map/all_gather | solution.py:96
  85.7 3.0 collective-permute-done.3
  88.7 4.2 %collective-permute-done.2 = bf16[258,768]{1,0:T(8,128)(2,1)S(1)} collective-permute-done((bf16[258,768]{1,0:T(8,128)(2,1)}, bf16[258,768]{1,0:T(8,128)(2,1)S(1)}, u32[]{:S(2)}, u32[]{:S(2)}) %collective-permute-start.2) | collective-permute-done | bytes 396320 | tf_op jit(solution)/shard_map/ppermute | solution.py:24
  95.0 10.3 %copy.42 = bf16[3072,3,384]{0,2,1:T(8,128)(2,1)} copy(bf16[3072,3,384]{2,0,1:T(8,128)(2,1)} %all-gather.4.cloned.1.call-done) | data formatting | bytes 14155776 | tf_op jit(solution)/shard_map/optimization_barrier | solution.py:97
  105.3 3.6 collective-permute-start.10
  109.5 17.2 %collective-permute-done.5 = bf16[1024,768]{1,0:T(8,128)(2,1)} collective-permute-done((bf16[1024,768]{1,0:T(8,128)(2,1)}, bf16[1024,768]{1,0:T(8,128)(2,1)}, u32[]{:S(2)}, u32[]{:S(2)}) %collective-permute-start.5) | collective-permute-done | bytes 1572896 | tf_op jit(solution)/shard_map/ppermute | solution.py:21
  135.9 10.4 %collective-permute-done.6 = bf16[512,768]{1,0:T(8,128)(2,1)S(1)} collective-permute-done((bf16[512,768]{1,0:T(8,128)(2,1)S(1)}, bf16[512,768]{1,0:T(8,128)(2,1)S(1)}, u32[]{:S(2)}, u32[]{:S(2)}) %collective-permute-start.6) | collective-permute-done | bytes 786464 | tf_op jit(solution)/shard_map/ppermute | solution.py:24
  146.6 3.8 pad_maximum_fusion
  153.7 3.2 fusion.14
  156.9 8.3 %fusion.41 = f32[1024,3,3,128]{3,0,2,1:T(8,128)S(1)} fusion(bf16[3,3,128,3072]{3,2,1,0:T(8,128)(2,1)S(1)} %bitcast.336, bf16[1024,768]{1,0:T(8,128)(2,1)S(1)} %get-tuple-element.53, bf16[1024,768]{1,0:T(8,128)(2,1)S(1)} %get-tuple-element.52, bf16[1024,768]{1,0:T(8,128)(2,1)S(1)} %get-tuple-element.51, bf16[1024,768]{1,0:T(8,128)(2,1)S(1)} %get-tuple-element.50), kind=kOutput, calls=%fused_computation.65 | convolution fusion | flops 7272923136 | bytes 18087936 | tf_op jit(solution)/shard_map/dot_general | solution.py:51
  168.2 3.2 collective-permute-start.9
  171.5 12.6 %fusion.40 = f32[1024,3,3,128]{3,0,2,1:T(8,128)S(1)} fusion(bf16[3,3,128,3072]{3,2,1,0:T(8,128)(2,1)} %bitcast.48, bf16[1024,768]{1,0:T(8,128)(2,1)} %copy-done.10, bf16[1024,768]{1,0:T(8,128)(2,1)} %copy-done.9, bf16[1024,768]{1,0:T(8,128)(2,1)} %copy-done.8, bf16[1024,768]{1,0:T(8,128)(2,1)S(1)} %get-tuple-element.50), kind=kOutput, calls=%fused_computation.64 | convolution fusion | flops 7272923136 | bytes 18087936 | tf_op jit(solution)/shard_map/dot_general | solution.py:51
  187.7 3.0 copy.76
  190.7 6.7 %copy.41 = bf16[768,3072]{1,0:T(8,128)(2,1)} copy(bf16[768,3072]{0,1:T(8,128)(2,1)} %bitcast.327) | data formatting | bytes 9437184 | tf_op jit(solution)/shard_map/dot_general | solution.py:51
  197.4 5.7 %fusion.77 = f32[512,2,3,128]{3,0,2,1:T(8,128)S(1)} fusion(bf16[2,3,128,3072]{3,2,1,0:T(8,128)(2,1)} %bitcast.341, bf16[512,768]{1,0:T(8,128)(2,1)} %get-tuple-element.61, bf16[512,768]{1,0:T(8,128)(2,1)} %get-tuple-element.60, bf16[512,768]{1,0:T(8,128)(2,1)} %get-tuple-element.59, bf16[512,768]{1,0:T(8,128)(2,1)} %get-tuple-element.58), kind=kOutput, calls=%fused_computation.125 | convolution fusion | flops 2428502016 | bytes 9437184 | tf_op jit(solution)/shard_map/dot_general | solution.py:51
  204.5 5.0 %fusion.92 = f32[3,512,1536]{2,1,0:T(8,128)} fusion(bf16[1024,3,128]{2,0,1:T(8,128)(2,1)S(1)} %get-tuple-element.57, bf16[512,3,128]{2,0,1:T(8,128)(2,1)S(1)} %multiply_convert_fusion.5, bf16[1024,3,128]{2,0,1:T(8,128)(2,1)S(1)} %get-tuple-element.56), kind=kOutput, calls=%fused_computation.156 | convolution fusion | flops 606339072 | bytes 11010048 | tf_op jit(solution)/shard_map/qhe,khe->hqk/dot_general | solution.py:120
  209.5 5.0 %fusion.93 = f32[3,512,1536]{2,1,0:T(8,128)} fusion(bf16[1024,3,128]{2,0,1:T(8,128)(2,1)S(1)} %get-tuple-element.57, bf16[512,3,128]{2,0,1:T(8,128)(2,1)S(1)} %multiply_convert_fusion.5, bf16[1024,3,128]{2,0,1:T(8,128)(2,1)S(1)} %get-tuple-element.56), kind=kOutput, calls=%fused_computation.157 | convolution fusion | flops 606339072 | bytes 11010048 | tf_op jit(solution)/shard_map/qhe,khe->hqk/dot_general | solution.py:120
  217.2 12.7 %copy.72 = bf16[3072,2,384]{0,2,1:T(8,128)(2,1)} copy(bf16[3072,2,384]{2,1,0:T(2,128)(2,1)} %collective-permute-done.9) | data formatting | bytes 9437184 | tf_op jit(solution)/shard_map/reshape | solution.py:51
  229.9 5.7 %fusion.76 = f32[512,2,3,128]{3,0,2,1:T(8,128)S(1)} fusion(bf16[2,3,128,3072]{3,2,1,0:T(8,128)(2,1)} %bitcast.340, bf16[512,768]{1,0:T(8,128)(2,1)} %get-tuple-element.61, bf16[512,768]{1,0:T(8,128)(2,1)} %get-tuple-element.60, bf16[512,768]{1,0:T(8,128)(2,1)} %get-tuple-element.59, bf16[512,768]{1,0:T(8,128)(2,1)S(1)} %copy-done.11), kind=kOutput, calls=%fused_computation.124 | convolution fusion | flops 2428502016 | bytes 9437184 | tf_op jit(solution)/shard_map/dot_general | solution.py:51
  237.0 5.1 %fusion.90 = f32[3,512,1536]{2,1,0:T(8,128)} fusion(bf16[1024,3,128]{2,0,1:T(8,128)(2,1)S(1)} %get-tuple-element.55, bf16[512,3,128]{2,0,1:T(8,128)(2,1)S(1)} %multiply_convert_fusion.4, bf16[1024,3,128]{2,0,1:T(8,128)(2,1)S(1)} %get-tuple-element.54), kind=kOutput, calls=%fused_computation.154 | convolution fusion | flops 606339072 | bytes 11010048 | tf_op jit(solution)/shard_map/qhe,khe->hqk/dot_general | solution.py:120
  242.1 14.2 %fusion.1 = (f32[3,512]{1,0:T(4,128)S(1)}, f32[3,512]{1,0:T(4,128)S(1)}, f32[3,512]{1,0:T(4,128)S(1)}, f32[3,512]{1,0:T(4,128)S(1)}, f32[3,512,1536]{2,1,0:T(8,128)}) fusion(pred[1536]{0:T(1024)(128)(4,1)S(1)} %fusion.100, f32[3,512,1536]{2,1,0:T(8,128)S(1)} %bitcast.329, f32[3,512,1536]{2,1,0:T(8,128)} %fusion.90, f32[3,512,1536]{2,1,0:T(8,128)} %fusion.93, ...), kind=kOutput, calls=%fused_computation.9 | convolution fusion | flops 634644480 | bytes 39348224 | tf_op jit(solution)/shard_map/qhe,khe->hqk/dot_general | solution.py:120
  256.4 6.5 %fusion.81 = bf16[3,128,512]{2,1,0:T(8,128)(2,1)S(1)} fusion(f32[3,512,1536]{2,1,0:T(8,128)} %fusion.93, f32[3,512]{1,0:T(4,128)S(1)} %get-tuple-element.49, pred[1536]{0:T(1024)(128)(4,1)S(1)} %fusion.100, bf16[1024,3,128]{2,0,1:T(8,128)(2,1)} %fusion.88, bf16[512,3,128]{2,0,1:T(8,128)(2,1)} %fusion.94), kind=kOutput, calls=%fused_computation.129 | convolution fusion | flops 615972864 | bytes 11017728 | tf_op jit(solution)/shard_map/hqk,khe->qhe/dot_general | solution.py:125
  270.4 6.2 %fusion.80 = bf16[3,128,512]{2,1,0:T(8,128)(2,1)S(1)} fusion(f32[3,512,1536]{2,1,0:T(8,128)} %get-tuple-element.88, f32[3,512]{1,0:T(4,128)S(1)} %get-tuple-element.46, pred[1536]{0:T(1024)(128)(4,1)S(1)} %fusion.100, bf16[1024,3,128]{2,0,1:T(8,128)(2,1)S(1)} %copy-done.13, bf16[512,3,128]{2,0,1:T(8,128)(2,1)S(1)} %copy-done.15), kind=kOutput, calls=%fused_computation.128 | convolution fusion | flops 615972864 | bytes 11017728 | tf_op jit(solution)/shard_map/hqk,khe->qhe/dot_general | solution.py:125
  276.7 3.7 add_convert_fusion
  287.9 3.6 add_convert_fusion.1
  297.4 4.6 %collective-permute-done.14 = bf16[512,768]{1,0:T(8,128)(2,1)} collective-permute-done((bf16[512,768]{1,0:T(8,128)(2,1)S(1)}, bf16[512,768]{1,0:T(8,128)(2,1)}, u32[]{:S(2)}, u32[]{:S(2)}) %collective-permute-start.14) | collective-permute-done | bytes 786464 | tf_op jit(solution)/shard_map/ppermute | solution.py:146
  304.5 15.7 %collective-permute-done.15 = bf16[512,768]{1,0:T(8,128)(2,1)} collective-permute-done((bf16[512,768]{1,0:T(8,128)(2,1)}, bf16[512,768]{1,0:T(8,128)(2,1)}, u32[]{:S(2)}, u32[]{:S(2)}) %collective-permute-start.15) | collective-permute-done | bytes 786464 | tf_op jit(solution)/shard_map/ppermute | solution.py:146
  322.1 13.6 %collective-permute-done.11 = bf16[512,768]{1,0:T(8,128)(2,1)} collective-permute-done((bf16[512,768]{1,0:T(8,128)(2,1)}, bf16[512,768]{1,0:T(8,128)(2,1)}, u32[]{:S(2)}, u32[]{:S(2)}) %collective-permute-start.11) | collective-permute-done | bytes 786464 | tf_op jit(solution)/shard_map/ppermute | solution.py:146
  337.7 16.2 %collective-permute-done.12 = bf16[512,768]{1,0:T(8,128)(2,1)} collective-permute-done((bf16[512,768]{1,0:T(8,128)(2,1)}, bf16[512,768]{1,0:T(8,128)(2,1)}, u32[]{:S(2)}, u32[]{:S(2)}) %collective-permute-start.12) | collective-permute-done | bytes 786464 | tf_op jit(solution)/shard_map/ppermute | solution.py:146
  358.4 4.4 %collective-permute-start.23 = (f32[128,64]{0,1:T(8,128)S(1)}, f32[128,64]{0,1:T(8,128)S(1)}, u32[]{:S(2)}, u32[]{:S(2)}) collective-permute-start(f32[128,64]{0,1:T(8,128)S(1)} %bitcast.357), channel_id=1, source_target_pairs={{0,112},{16,0},{32,16},{48,32},{64,48},{80,64},{96,80},{112,96},{1... | collective-permute-start | bytes 98312 | tf_op jit(solution)/shard_map/ppermute | solution.py:162
  371.2 3.5 fusion.37
  (165 shorter events, 77.9 us)
Async XLA Ops:
  7.2 70.7 %all-gather.4.cloned.1.call-start = ((), (), s32[]{:S(2)}) async-start(), calls=%async_computation | async-start | bytes 7520256 | tf_op jit(solution)/shard_map/all_gather | solution.py:96
  8.3 76.7 %copy-start.17 = (bf16[768,192]{0,1:T(8,128)(2,1)S(1)}, bf16[768,192]{0,1:T(8,128)(2,1)}, u32[]{:S(2)}) copy-start(bf16[768,192]{0,1:T(8,128)(2,1)} %param.22) | copy-start | bytes 884740
  9.2 159.0 %all-gather.6.cloned.1.call-start = ((), (), s32[]{:S(2)}) async-start(), calls=%async_computation.1 | async-start | bytes 5013504 | tf_op jit(solution)/shard_map/all_gather | solution.py:98
  11.4 66.6 %collective-permute-start = (bf16[516,768]{1,0:T(8,128)(2,1)S(1)}, bf16[516,768]{1,0:T(8,128)(2,1)S(1)}, u32[]{:S(2)}, u32[]{:S(2)}) collective-permute-start(bf16[516,768]{1,0:T(8,128)(2,1)S(1)} %get-tuple-element.77), channel_id=1, source_target_pairs={{0,48},{16,0},{32,16},{48,32},{1,49},{17,1},{33,17},{49,33},{2,50}... | collective-permute-start | bytes 2377736 | tf_op jit(solution)/shard_map/ppermute | solution.py:22
  16.0 64.9 %collective-permute-start.1 = (bf16[516,768]{1,0:T(8,128)(2,1)S(1)}, bf16[516,768]{1,0:T(8,128)(2,1)S(1)}, u32[]{:S(2)}, u32[]{:S(2)}) collective-permute-start(bf16[516,768]{1,0:T(8,128)(2,1)S(1)} %get-tuple-element.77), channel_id=1, source_target_pairs={{0,16},{16,32},{32,48},{48,0},{1,17},{17,33},{33,49},{49,1},{2,18}... | collective-permute-start | bytes 2377736 | tf_op jit(solution)/shard_map/ppermute | solution.py:21
  77.9 137.2 %all-gather.8.cloned.1.call-start = ((), (), s32[]{:S(2)}) async-start(), calls=%async_computation.2 | async-start | bytes 2506752 | tf_op jit(solution)/shard_map/all_gather | solution.py:100
  78.0 15.0 %copy-start.6 = (bf16[516,768]{1,0:T(8,128)(2,1)}, bf16[516,768]{1,0:T(8,128)(2,1)S(1)}, u32[]{:S(2)}) copy-start(bf16[516,768]{1,0:T(8,128)(2,1)S(1)} %collective-permute-done) | copy-start | bytes 2377732
  78.1 10.6 %collective-permute-start.3 = (bf16[258,768]{1,0:T(8,128)(2,1)S(1)}, bf16[258,768]{1,0:T(8,128)(2,1)S(1)}, u32[]{:S(2)}, u32[]{:S(2)}) collective-permute-start(bf16[258,768]{1,0:T(8,128)(2,1)S(1)} %slice.217), channel_id=1, source_target_pairs={{0,48},{16,0},{32,16},{48,32},{1,49},{17,1},{33,17},{49,33},{2,50}... | collective-permute-start | bytes 1188872 | tf_op jit(solution)/shard_map/ppermute | solution.py:25
  81.7 11.2 %collective-permute-start.2 = (bf16[258,768]{1,0:T(8,128)(2,1)}, bf16[258,768]{1,0:T(8,128)(2,1)S(1)}, u32[]{:S(2)}, u32[]{:S(2)}) collective-permute-start(bf16[258,768]{1,0:T(8,128)(2,1)} %slice.216), channel_id=1, source_target_pairs={{0,16},{16,32},{32,48},{48,0},{1,17},{17,33},{33,49},{49,1},{2,18}... | collective-permute-start | bytes 1188872 | tf_op jit(solution)/shard_map/ppermute | solution.py:24
  81.7 45.0 %collective-permute-start.5 = (bf16[1024,768]{1,0:T(8,128)(2,1)}, bf16[1024,768]{1,0:T(8,128)(2,1)}, u32[]{:S(2)}, u32[]{:S(2)}) collective-permute-start(bf16[1024,768]{1,0:T(8,128)(2,1)} %bitcast.18), channel_id=1, source_target_pairs={{0,16},{16,32},{32,48},{48,0},{1,17},{17,33},{33,49},{49,1},{2,18}... | collective-permute-start | bytes 4718600 | tf_op jit(solution)/shard_map/ppermute | solution.py:21
  81.7 46.2 %collective-permute-start.4 = (bf16[1024,768]{1,0:T(8,128)(2,1)}, bf16[1024,768]{1,0:T(8,128)(2,1)}, u32[]{:S(2)}, u32[]{:S(2)}) collective-permute-start(bf16[1024,768]{1,0:T(8,128)(2,1)} %bitcast.18), channel_id=1, source_target_pairs={{0,48},{16,0},{32,16},{48,32},{1,49},{17,1},{33,17},{49,33},{2,50}... | collective-permute-start | bytes 4718600 | tf_op jit(solution)/shard_map/ppermute | solution.py:22
  105.3 66.1 %collective-permute-start.10 = (bf16[3072,3,384]{0,2,1:T(8,128)(2,1)}, bf16[3072,3,384]{0,2,1:T(8,128)(2,1)}, u32[]{:S(2)}, u32[]{:S(2)}) collective-permute-start(bf16[3072,3,384]{0,2,1:T(8,128)(2,1)} %copy.42), channel_id=1, source_target_pairs={{0,64},{64,0},{1,65},{65,1},{2,66},{66,2},{3,67},{67,3},{4,68},{68... | collective-permute-start | bytes 21233672 | tf_op jit(solution)/shard_map/ppermute | solution.py:103
  127.9 18.4 %collective-permute-start.6 = (bf16[512,768]{1,0:T(8,128)(2,1)S(1)}, bf16[512,768]{1,0:T(8,128)(2,1)S(1)}, u32[]{:S(2)}, u32[]{:S(2)}) collective-permute-start(bf16[512,768]{1,0:T(8,128)(2,1)S(1)} %slice.227), channel_id=1, source_target_pairs={{0,16},{16,32},{32,48},{48,0},{1,17},{17,33},{33,49},{49,1},{2,18}... | collective-permute-start | bytes 2359304 | tf_op jit(solution)/shard_map/ppermute | solution.py:24
  129.2 17.3 %collective-permute-start.7 = (bf16[512,768]{1,0:T(8,128)(2,1)S(1)}, bf16[512,768]{1,0:T(8,128)(2,1)S(1)}, u32[]{:S(2)}, u32[]{:S(2)}) collective-permute-start(bf16[512,768]{1,0:T(8,128)(2,1)S(1)} %slice.228), channel_id=1, source_target_pairs={{0,48},{16,0},{32,16},{48,32},{1,49},{17,1},{33,17},{49,33},{2,50}... | collective-permute-start | bytes 2359304 | tf_op jit(solution)/shard_map/ppermute | solution.py:25
  168.2 48.9 %collective-permute-start.9 = (bf16[3072,2,384]{2,1,0:T(2,128)(2,1)}, bf16[3072,2,384]{2,1,0:T(2,128)(2,1)}, u32[]{:S(2)}, u32[]{:S(2)}) collective-permute-start(bf16[3072,2,384]{2,1,0:T(2,128)(2,1)} %all-gather.6.cloned.1.call-done), channel_id=1, source_target_pairs={{0,64},{64,0},{1,65},{65,1},{2,66},{66,2},{3,67},{67,3},{4,68},{68... | collective-permute-start | bytes 14155784 | tf_op jit(solution)/shard_map/ppermute | solution.py:103
  214.5 15.3 %copy-start.11 = (bf16[512,768]{1,0:T(8,128)(2,1)S(1)}, bf16[512,768]{1,0:T(8,128)(2,1)}, u32[]{:S(2)}) copy-start(bf16[512,768]{1,0:T(8,128)(2,1)} %get-tuple-element.58) | copy-start | bytes 2359300
  215.1 61.5 %collective-permute-start.8 = (bf16[384,3072]{0,1:T(8,128)(2,1)}, bf16[384,3072]{0,1:T(8,128)(2,1)}, u32[]{:S(2)}, u32[]{:S(2)}) collective-permute-start(bf16[384,3072]{0,1:T(8,128)(2,1)} %all-gather.8.cloned.1.call-done), channel_id=1, source_target_pairs={{0,64},{64,0},{1,65},{65,1},{2,66},{66,2},{3,67},{67,3},{4,68},{68... | collective-permute-start | bytes 7077896 | tf_op jit(solution)/shard_map/ppermute | solution.py:103
  281.6 20.4 %collective-permute-start.14 = (bf16[512,768]{1,0:T(8,128)(2,1)S(1)}, bf16[512,768]{1,0:T(8,128)(2,1)}, u32[]{:S(2)}, u32[]{:S(2)}) collective-permute-start(bf16[512,768]{1,0:T(8,128)(2,1)S(1)} %get-tuple-element.73), channel_id=1, source_target_pairs={{0,16},{16,32},{32,48},{48,0},{1,17},{17,33},{33,49},{49,1},{2,18}... | collective-permute-start | bytes 2359304 | tf_op jit(solution)/shard_map/ppermute | solution.py:146
  284.8 19.7 %collective-permute-start.16 = (bf16[512,768]{1,0:T(8,128)(2,1)}, bf16[512,768]{1,0:T(8,128)(2,1)}, u32[]{:S(2)}, u32[]{:S(2)}) collective-permute-start(bf16[512,768]{1,0:T(8,128)(2,1)} %get-tuple-element.74), channel_id=1, source_target_pairs={{0,48},{16,0},{32,16},{48,32},{1,49},{17,1},{33,17},{49,33},{2,50}... | collective-permute-start | bytes 2359304 | tf_op jit(solution)/shard_map/ppermute | solution.py:146
  286.2 33.9 %collective-permute-start.15 = (bf16[512,768]{1,0:T(8,128)(2,1)}, bf16[512,768]{1,0:T(8,128)(2,1)}, u32[]{:S(2)}, u32[]{:S(2)}) collective-permute-start(bf16[512,768]{1,0:T(8,128)(2,1)} %get-tuple-element.75), channel_id=1, source_target_pairs={{0,32},{16,48},{32,0},{48,16},{1,33},{17,49},{33,1},{49,17},{2,34}... | collective-permute-start | bytes 2359304 | tf_op jit(solution)/shard_map/ppermute | solution.py:146
  294.7 41.0 %collective-permute-start.11 = (bf16[512,768]{1,0:T(8,128)(2,1)}, bf16[512,768]{1,0:T(8,128)(2,1)}, u32[]{:S(2)}, u32[]{:S(2)}) collective-permute-start(bf16[512,768]{1,0:T(8,128)(2,1)} %get-tuple-element.70), channel_id=1, source_target_pairs={{0,16},{16,32},{32,48},{48,0},{1,17},{17,33},{33,49},{49,1},{2,18}... | collective-permute-start | bytes 2359304 | tf_op jit(solution)/shard_map/ppermute | solution.py:146
  295.1 42.5 %collective-permute-start.13 = (bf16[512,768]{1,0:T(8,128)(2,1)}, bf16[512,768]{1,0:T(8,128)(2,1)}, u32[]{:S(2)}, u32[]{:S(2)}) collective-permute-start(bf16[512,768]{1,0:T(8,128)(2,1)} %get-tuple-element.71), channel_id=1, source_target_pairs={{0,48},{16,0},{32,16},{48,32},{1,49},{17,1},{33,17},{49,33},{2,50}... | collective-permute-start | bytes 2359304 | tf_op jit(solution)/shard_map/ppermute | solution.py:146
  302.0 51.8 %collective-permute-start.12 = (bf16[512,768]{1,0:T(8,128)(2,1)}, bf16[512,768]{1,0:T(8,128)(2,1)}, u32[]{:S(2)}, u32[]{:S(2)}) collective-permute-start(bf16[512,768]{1,0:T(8,128)(2,1)} %get-tuple-element.72), channel_id=1, source_target_pairs={{0,32},{16,48},{32,0},{48,16},{1,33},{17,49},{33,1},{49,17},{2,34}... | collective-permute-start | bytes 2359304 | tf_op jit(solution)/shard_map/ppermute | solution.py:146
  322.1 36.0 %copy-start.4 = (f32[512,768]{1,0:T(8,128)}, f32[512,768]{1,0:T(8,128)S(1)}, u32[]{:S(2)}) copy-start(f32[512,768]{1,0:T(8,128)S(1)} %fusion.71) | copy-start | bytes 4718596
  322.1 33.9 %copy-start.21 = (bf16[768,64]{0,1:T(8,128)(2,1)S(1)}, bf16[768,64]{0,1:T(8,128)(2,1)}, u32[]{:S(2)}) copy-start(bf16[768,64]{0,1:T(8,128)(2,1)} %param.23) | copy-start | bytes 294916
  358.4 11.0 %collective-permute-start.23 = (f32[128,64]{0,1:T(8,128)S(1)}, f32[128,64]{0,1:T(8,128)S(1)}, u32[]{:S(2)}, u32[]{:S(2)}) collective-permute-start(f32[128,64]{0,1:T(8,128)S(1)} %bitcast.357), channel_id=1, source_target_pairs={{0,112},{16,0},{32,16},{48,32},{64,48},{80,64},{96,80},{112,96},{1... | collective-permute-start | bytes 98312 | tf_op jit(solution)/shard_map/ppermute | solution.py:162
  362.8 6.9 %collective-permute-start.17 = (f32[128,64]{0,1:T(8,128)S(1)}, f32[128,64]{0,1:T(8,128)S(1)}, u32[]{:S(2)}, u32[]{:S(2)}) collective-permute-start(f32[128,64]{0,1:T(8,128)S(1)} %bitcast.356), channel_id=1, source_target_pairs={{0,16},{16,32},{32,48},{48,64},{64,80},{80,96},{96,112},{112,0},{1... | collective-permute-start | bytes 98312 | tf_op jit(solution)/shard_map/ppermute | solution.py:162
  365.4 9.3 %collective-permute-start.22 = (f32[128,64]{0,1:T(8,128)S(1)}, f32[128,64]{0,1:T(8,128)S(1)}, u32[]{:S(2)}, u32[]{:S(2)}) collective-permute-start(f32[128,64]{0,1:T(8,128)S(1)} %bitcast.355), channel_id=1, source_target_pairs={{0,96},{16,112},{32,0},{48,16},{64,32},{80,48},{96,64},{112,80},{1... | collective-permute-start | bytes 98312 | tf_op jit(solution)/shard_map/ppermute | solution.py:162
  367.0 7.7 %collective-permute-start.21 = (f32[128,64]{0,1:T(8,128)S(1)}, f32[128,64]{0,1:T(8,128)S(1)}, u32[]{:S(2)}, u32[]{:S(2)}) collective-permute-start(f32[128,64]{0,1:T(8,128)S(1)} %bitcast.354), channel_id=1, source_target_pairs={{0,80},{16,96},{32,112},{48,0},{64,16},{80,32},{96,48},{112,64},{1... | collective-permute-start | bytes 98312 | tf_op jit(solution)/shard_map/ppermute | solution.py:162
  368.0 6.6 %collective-permute-start.20 = (f32[128,64]{0,1:T(8,128)S(1)}, f32[128,64]{0,1:T(8,128)S(1)}, u32[]{:S(2)}, u32[]{:S(2)}) collective-permute-start(f32[128,64]{0,1:T(8,128)S(1)} %bitcast.353), channel_id=1, source_target_pairs={{0,64},{16,80},{32,96},{48,112},{64,0},{80,16},{96,32},{112,48},{1... | collective-permute-start | bytes 98312 | tf_op jit(solution)/shard_map/ppermute | solution.py:162
  369.4 5.3 %collective-permute-start.19 = (f32[128,64]{0,1:T(8,128)S(1)}, f32[128,64]{0,1:T(8,128)S(1)}, u32[]{:S(2)}, u32[]{:S(2)}) collective-permute-start(f32[128,64]{0,1:T(8,128)S(1)} %bitcast.352), channel_id=1, source_target_pairs={{0,48},{16,64},{32,80},{48,96},{64,112},{80,0},{96,16},{112,32},{1... | collective-permute-start | bytes 98312 | tf_op jit(solution)/shard_map/ppermute | solution.py:162
  369.7 5.4 %collective-permute-start.18 = (f32[128,64]{0,1:T(8,128)S(1)}, f32[128,64]{0,1:T(8,128)S(1)}, u32[]{:S(2)}, u32[]{:S(2)}) collective-permute-start(f32[128,64]{0,1:T(8,128)S(1)} %bitcast.351), channel_id=1, source_target_pairs={{0,32},{16,48},{32,64},{48,80},{64,96},{80,112},{96,0},{112,16},{1... | collective-permute-start | bytes 98312 | tf_op jit(solution)/shard_map/ppermute | solution.py:162
  (25 other events, 160.5 us)
Sparse Core Ops, SparseCore 0:
  10.1 67.7 all-gather.3
  80.0 53.3 all-gather.5
  168.4 46.6 all-gather.7
where the time goes:
time: 390 us; the launch traced here: 383 us
  waiting for transfers between devices  149 us (38%)
  matrix products  93 us (24%)
  local copies, waits for them, and re-layouts  49.2 us (13%)
  starting transfers between devices  40.8 us (10%)
  other arithmetic  32.3 us (8%)
  between operations  18.2 us (5%)
    all_gather x1, waiting for transfers between devices, shards(): lax.all_gather(own_half(img_qkv_weight, 2), 'col', axis=0, tiled=True)  61 us
    ppermute x6, waiting for transfers between devices, shards(): lax.ppermute(outgoing, 'row', shift_pairs(n_row, step)).astype(jnp.float32)  52 us
    dot_general x4, matrix products, add_rows(): jnp.dot(ready, piece.reshape(piece.shape[0], -1), preferred_element_type=...  32.3 us
    dot_general x4, matrix products, attend(): jnp.einsum('qhe,khe->hqk', queries, key_rows, preferred_element_type=jnp....  29.4 us
    dot_general x4, matrix products, attend(): jnp.einsum('hqk,khe->qhe', chances, value_rows, preferred_element_type=jn...  18.3 us
    ppermute x2, waiting for transfers between devices, ring_gather(): from_prev = lax.ppermute(piece, axis_name, shift_pairs(size, 1))  17.2 us
    ppermute x2, waiting for transfers between devices, ring_gather(): far_top = lax.ppermute(from_prev[:cut], axis_name, shift_pairs(size, 1))  14.6 us
    reshape x1, local copies, waits for them, and re-layouts, add_rows(): piece.reshape(piece.shape[0], -1)  12.7 us
  transfers between devices with their start and end apart: 27, of which 13 were waited for; matrix products, arithmetic and copies ran while one was open for 42% of the time, Pallas kernels for 0%

commit v1 on v0

--- a/solution.py
+++ b/solution.py
@@ -4,6 +4,7 @@
 import jax.numpy as jnp
 from jax import lax
 from jax.sharding import PartitionSpec as P
+
 
 HD = 128
 
@@ -51,7 +52,7 @@
     return jnp.dot(ready, piece.reshape(piece.shape[0], -1), preferred_element_type=jnp.float32)
 
 
-def shards(
+def layer(
     img_tokens,
     txt_tokens,
     img_mod,
@@ -72,7 +73,6 @@
     text_slots = txt_tokens.shape[2]
     local_width = img_qkv_weight.shape[2]
     width = local_width * n_row
-    heads_here = local_width // HD
     me_row = lax.axis_index("row")
     core = lax.axis_index("cfg")
 
@@ -94,13 +94,18 @@
         return lax.dynamic_slice_in_dim(weight, core * half, half, axis=axis)
 
     img_w = lax.all_gather(own_half(img_qkv_weight, 2), "col", axis=0, tiled=True)
-    img_w, txt_piece = lax.optimization_barrier((img_w, own_half(txt_kv_weight, 2)))
-    txt_w = lax.all_gather(txt_piece, "col", axis=0, tiled=True)
-    txt_w, out_piece = lax.optimization_barrier((txt_w, own_half(out_weight, 0)))
-    out_w = lax.all_gather(out_piece, "col", axis=1, tiled=True)
+    rows_here = txt_kv_weight.shape[0]
+    txt_out_piece = jnp.concatenate(
+        [own_half(txt_kv_weight, 2).reshape(rows_here, -1), own_half(out_weight, 0).T], 1
+    )
+    img_w, txt_out_piece = lax.optimization_barrier((img_w, txt_out_piece))
+    txt_out_w = lax.all_gather(txt_out_piece, "col", axis=0, tiled=True)
+    txt_w = txt_out_w[:, : 2 * half].reshape(width, 2, half)
+    out_w = txt_out_w[:, 2 * half :].T
+    img_w_other = lax.ppermute(img_w, "cfg", swap)
     halves = [
         (txt_w, img_w, out_w),
-        tuple(lax.ppermute(w, "cfg", swap) for w in (txt_w, img_w, out_w)),
+        (lax.ppermute(txt_w, "cfg", swap), img_w_other, lax.ppermute(out_w, "cfg", swap)),
     ]
     positions = jnp.arange(text_slots + images, dtype=jnp.int32)
     usable = (positions < txt_len[0, 0]) | (positions >= text_slots)
@@ -167,7 +172,7 @@
 
 def solution(mesh):
     return jax.shard_map(
-        shards,
+        layer,
         mesh=mesh,
         in_specs=(
             P("cfg", "col", None, "row"),

time: 390 us -> 416 us (1.067)
  waiting for transfers between devices: 149 us -> 167 us
  local copies, waits for them, and re-layouts: 49.2 us -> 56.2 us
    ppermute x2, waiting for transfers between devices: 0.01 us -> 16.3 us  [ring_gather(): from_next = lax.ppermute(piece, axis_name, shift_pairs(size, -1))]
    ppermute x0 -> x1, local copies, waits for them, and re-layouts: none -> 12.9 us  [layer(): lax.ppermute(txt_w, 'cfg', swap)]
    dot_general x1 -> x0, local copies, waits for them, and re-layouts: 6.71 us -> none  [add_rows(): jnp.dot(ready, piece.reshape(piece.shape[0], -1), preferred_element_type=...]
    slice x0 -> x3, local copies, waits for them, and re-layouts: none -> 5 us  [the longest x1 4.9 us: layer(): txt_w = txt_out_w[:, :2 * half].reshape(width, 2, half)]
    all_gather x3 -> x2, waiting for transfers between devices: 61.6 us -> 66.3 us  [the longest x1 66.3 us: layer(): lax.all_gather(own_half(img_qkv_weight, 2), 'col', axis=0, tiled=True)]
    transpose x0 -> x2, local copies, waits for them, and re-layouts: none -> 4.57 us  [the longest x1 3.64 us: layer(): out_w = txt_out_w[:, 2 * half:].T]
  transfers between devices with their start and end apart: 27 -> 26, of which waited for: 13 -> 13; matrix products, arithmetic and copies ran while one was open for 42% -> 42% of each run, Pallas kernels for 0% -> 0%
where the time goes in v1:
time: 416 us; the launch traced here: 409 us
  waiting for transfers between devices  167 us (40%)
  matrix products  95.2 us (23%)
  local copies, waits for them, and re-layouts  56.2 us (14%)
  starting transfers between devices  37.6 us (9%)
  other arithmetic  34.2 us (8%)
  between operations  18.4 us (4%)
    all_gather x1, waiting for transfers between devices, layer(): lax.all_gather(own_half(img_qkv_weight, 2), 'col', axis=0, tiled=True)  66.3 us
    ppermute x6, waiting for transfers between devices, layer(): lax.ppermute(outgoing, 'row', shift_pairs(n_row, step)).astype(jnp.float32)  52.3 us
    dot_general x4, matrix products, attend(): jnp.einsum('qhe,khe->hqk', queries, key_rows, preferred_element_type=jnp....  31.7 us
    dot_general x4, matrix products, add_rows(): jnp.dot(ready, piece.reshape(piece.shape[0], -1), preferred_element_type=...  31.5 us
    dot_general x4, matrix products, attend(): jnp.einsum('hqk,khe->qhe', chances, value_rows, preferred_element_type=jn...  18.3 us
    ppermute x2, waiting for transfers between devices, ring_gather(): from_next = lax.ppermute(piece, axis_name, shift_pairs(size, -1))  16.3 us
    ppermute x2, waiting for transfers between devices, ring_gather(): from_prev = lax.ppermute(piece, axis_name, shift_pairs(size, 1))  15.5 us
    ppermute x1, local copies, waits for them, and re-layouts, layer(): lax.ppermute(txt_w, 'cfg', swap)  12.9 us
  transfers between devices with their start and end apart: 26, of which 13 were waited for; matrix products, arithmetic and copies ran while one was open for 42% of the time, Pallas kernels for 0%

profile of v1, /device:TPU:1, one launch (start us, length us, event | category | flops | bytes accessed | tf_op | source)
XLA Modules:
  0.0 408.6 jit_solution(5025345916175574427)
XLA Ops:
  12.2 66.3 %all-gather.3.cloned.1.call-done = bf16[3072,3,384]{2,0,1:T(8,128)(2,1)} async-done(((bf16[192,3,384]{2,0,1:T(8,128)(2,1)}), bf16[3072,3,384]{2,0,1:T(8,128)(2,1)}) %all-gather.3.cloned.1.call-update) | async-done | bytes 7077904 | tf_op jit(solution)/shard_map/all_gather | solution.py:96
  82.2 16.3 %collective-permute-done = bf16[516,768]{1,0:T(8,128)(2,1)S(1)} collective-permute-done((bf16[516,768]{1,0:T(8,128)(2,1)S(1)}, bf16[516,768]{1,0:T(8,128)(2,1)S(1)}, u32[]{:S(2)}, u32[]{:S(2)}) %collective-permute-start) | collective-permute-done | bytes 792608 | tf_op jit(solution)/shard_map/ppermute | solution.py:23
  98.6 3.5 collective-permute-start.3
  105.6 3.5 collective-permute-done.3
  115.0 9.9 %copy.48 = bf16[3072,3,384]{0,2,1:T(8,128)(2,1)} copy(bf16[3072,3,384]{2,0,1:T(8,128)(2,1)} %all-gather.3.cloned.1.call-done) | data formatting | bytes 14155776 | tf_op jit(solution)/shard_map/optimization_barrier | solution.py:101
  124.9 5.2 %collective-permute-start.10 = (bf16[3072,3,384]{0,2,1:T(8,128)(2,1)}, bf16[3072,3,384]{0,2,1:T(8,128)(2,1)}, u32[]{:S(2)}, u32[]{:S(2)}) collective-permute-start(bf16[3072,3,384]{0,2,1:T(8,128)(2,1)} %copy.48), channel_id=1, source_target_pairs={{0,64},{64,0},{1,65},{65,1},{2,66},{66,2},{3,67},{67,3},{4,68},{68... | collective-permute-start | bytes 21233672 | tf_op jit(solution)/shard_map/ppermute | solution.py:105
  130.7 15.5 %collective-permute-done.5 = bf16[1024,768]{1,0:T(8,128)(2,1)} collective-permute-done((bf16[1024,768]{1,0:T(8,128)(2,1)}, bf16[1024,768]{1,0:T(8,128)(2,1)}, u32[]{:S(2)}, u32[]{:S(2)}) %collective-permute-start.5) | collective-permute-done | bytes 1572896 | tf_op jit(solution)/shard_map/ppermute | solution.py:22
  155.3 9.6 %collective-permute-done.6 = bf16[512,768]{1,0:T(8,128)(2,1)S(1)} collective-permute-done((bf16[512,768]{1,0:T(8,128)(2,1)S(1)}, bf16[512,768]{1,0:T(8,128)(2,1)S(1)}, u32[]{:S(2)}, u32[]{:S(2)}) %collective-permute-start.6) | collective-permute-done | bytes 786464 | tf_op jit(solution)/shard_map/ppermute | solution.py:25
  165.3 3.5 pad_maximum_fusion
  175.3 8.3 %fusion.43 = f32[1024,3,3,128]{3,0,2,1:T(8,128)S(1)} fusion(bf16[3,3,128,3072]{3,2,1,0:T(8,128)(2,1)S(1)} %bitcast.336, bf16[1024,768]{1,0:T(8,128)(2,1)S(1)} %get-tuple-element.51, bf16[1024,768]{1,0:T(8,128)(2,1)S(1)} %get-tuple-element.50, bf16[1024,768]{1,0:T(8,128)(2,1)S(1)} %get-tuple-element.49, bf16[1024,768]{1,0:T(8,128)(2,1)S(1)} %get-tuple-element.48), kind=kOutput, calls=%fused_computation.67 | convolution fusion | flops 7272923136 | bytes 18087936 | tf_op jit(solution)/shard_map/dot_general | solution.py:52
  187.3 4.9 %slice.235 = bf16[3072,768]{1,0:T(8,128)(2,1)} slice(bf16[3072,1152]{1,0:T(8,128)(2,1)} %all-gather.5.cloned.1.call-done), slice={[0:3072], [0:768]} | slice | bytes 9437184 | tf_op jit(solution)/shard_map/slice | solution.py:103
  192.2 10.1 %reshape.317 = bf16[3072,2,384]{2,1,0:T(2,128)(2,1)} reshape(bf16[3072,768]{1,0:T(8,128)(2,1)} %slice.235) | data formatting | bytes 9437184 | tf_op jit(solution)/shard_map/reshape | solution.py:103
  202.3 4.2 %collective-permute-start.9 = (bf16[3072,2,384]{2,1,0:T(2,128)(2,1)}, bf16[3072,2,384]{2,1,0:T(2,128)(2,1)}, u32[]{:S(2)}, u32[]{:S(2)}) collective-permute-start(bf16[3072,2,384]{2,1,0:T(2,128)(2,1)} %reshape.317), channel_id=1, source_target_pairs={{0,64},{64,0},{1,65},{65,1},{2,66},{66,2},{3,67},{67,3},{4,68},{68... | collective-permute-start | bytes 14155784 | tf_op jit(solution)/shard_map/ppermute | solution.py:108
  206.5 12.4 %fusion.42 = f32[1024,3,3,128]{3,0,2,1:T(8,128)S(1)} fusion(bf16[3,3,128,3072]{3,2,1,0:T(8,128)(2,1)} %bitcast.48, bf16[1024,768]{1,0:T(8,128)(2,1)} %copy-done.13, bf16[1024,768]{1,0:T(8,128)(2,1)} %copy-done.12, bf16[1024,768]{1,0:T(8,128)(2,1)} %copy-done.11, bf16[1024,768]{1,0:T(8,128)(2,1)S(1)} %get-tuple-element.48), kind=kOutput, calls=%fused_computation.66 | convolution fusion | flops 7272923136 | bytes 18087936 | tf_op jit(solution)/shard_map/dot_general | solution.py:52
  222.8 5.0 %fusion.96 = f32[512,768]{0,1:T(8,128)S(1)} fusion(bf16[512,768]{1,0:T(8,128)(2,1)S(1)} %copy-done.17, bf16[512,768]{1,0:T(8,128)(2,1)S(1)} %copy-done.16, bf16[512,768]{1,0:T(8,128)(2,1)S(1)} %copy-done.15, bf16[512,768]{1,0:T(8,128)(2,1)S(1)} %copy-done.14, bf16[3072,1152]{1,0:T(8,128)(2,1)} %all-gather.5.cloned.1.call-done), kind=kOutput, calls=%fused_computation.158 | convolution fusion | flops 2428502016 | bytes 9437184 | tf_op jit(solution)/shard_map/dot_general | solution.py:52
  230.0 3.6 slice_bitcast_fusion.5
  234.3 5.0 %fusion.94 = f32[3,512,1536]{2,1,0:T(8,128)} fusion(bf16[1024,3,128]{2,0,1:T(8,128)(2,1)S(1)} %get-tuple-element.55, bf16[512,3,128]{2,0,1:T(8,128)(2,1)S(1)} %fusion.91, bf16[1024,3,128]{2,0,1:T(8,128)(2,1)S(1)} %copy-done.6), kind=kOutput, calls=%fused_computation.156 | convolution fusion | flops 606339072 | bytes 11010048 | tf_op jit(solution)/shard_map/qhe,khe->hqk/dot_general | solution.py:125
  239.3 5.0 %fusion.95 = f32[3,512,1536]{2,1,0:T(8,128)} fusion(bf16[1024,3,128]{2,0,1:T(8,128)(2,1)S(1)} %get-tuple-element.55, bf16[512,3,128]{2,0,1:T(8,128)(2,1)S(1)} %fusion.91, bf16[1024,3,128]{2,0,1:T(8,128)(2,1)S(1)} %copy-done.6), kind=kOutput, calls=%fused_computation.157 | convolution fusion | flops 606339072 | bytes 11010048 | tf_op jit(solution)/shard_map/qhe,khe->hqk/dot_general | solution.py:125
  244.3 12.9 %copy.53 = bf16[3072,2,384]{0,2,1:T(8,128)(2,1)} copy(bf16[3072,2,384]{2,1,0:T(2,128)(2,1)} %collective-permute-done.9) | data formatting | bytes 9437184 | tf_op jit(solution)/shard_map/ppermute | solution.py:108
  257.2 5.8 %fusion.40 = f32[512,2,3,128]{3,0,2,1:T(8,128)S(1)} fusion(bf16[2,3,128,3072]{3,2,1,0:T(8,128)(2,1)} %bitcast.339, bf16[512,768]{1,0:T(8,128)(2,1)} %get-tuple-element.59, bf16[512,768]{1,0:T(8,128)(2,1)} %get-tuple-element.58, bf16[512,768]{1,0:T(8,128)(2,1)} %get-tuple-element.57, bf16[512,768]{1,0:T(8,128)(2,1)} %get-tuple-element.56), kind=kOutput, calls=%fused_computation.64 | convolution fusion | flops 2428502016 | bytes 9437184 | tf_op jit(solution)/shard_map/dot_general | solution.py:52
  263.6 5.0 %fusion.92 = f32[3,512,1536]{2,1,0:T(8,128)} fusion(bf16[1024,3,128]{2,0,1:T(8,128)(2,1)S(1)} %copy-done.7, bf16[512,3,128]{2,0,1:T(8,128)(2,1)S(1)} %multiply_convert_fusion.4, bf16[1024,3,128]{2,0,1:T(8,128)(2,1)S(1)} %copy-done.8), kind=kOutput, calls=%fused_computation.154 | convolution fusion | flops 606339072 | bytes 11010048 | tf_op jit(solution)/shard_map/qhe,khe->hqk/dot_general | solution.py:125
  268.7 16.6 %fusion.1 = (f32[3,512]{1,0:T(4,128)S(1)}, f32[3,512]{1,0:T(4,128)S(1)}, f32[3,512]{1,0:T(4,128)S(1)}, f32[3,512]{1,0:T(4,128)S(1)}, f32[3,512,1536]{2,1,0:T(8,128)}) fusion(pred[1536]{0:T(1024)(128)(4,1)S(1)} %fusion.102, f32[3,512,1536]{2,1,0:T(8,128)} %fusion.94, f32[3,512,1536]{2,1,0:T(8,128)} %fusion.92, f32[3,512,1536]{2,1,0:T(8,128)} %fusion.95, ...), kind=kOutput, calls=%fused_computation.9 | convolution fusion | flops 634644480 | bytes 39348224 | tf_op jit(solution)/shard_map/qhe,khe->hqk/dot_general | solution.py:125
  285.3 6.5 %fusion.81 = bf16[3,128,512]{2,1,0:T(8,128)(2,1)S(1)} fusion(f32[3,512,1536]{2,1,0:T(8,128)} %fusion.95, f32[3,512]{1,0:T(4,128)S(1)} %get-tuple-element.45, pred[1536]{0:T(1024)(128)(4,1)S(1)} %fusion.102, bf16[1024,3,128]{2,0,1:T(8,128)(2,1)} %fusion.88, bf16[512,3,128]{2,0,1:T(8,128)(2,1)} %bitcast.352), kind=kOutput, calls=%fused_computation.129 | convolution fusion | flops 615972864 | bytes 11017728 | tf_op jit(solution)/shard_map/hqk,khe->qhe/dot_general | solution.py:130
  296.6 6.3 %fusion.78 = bf16[3,128,512]{2,1,0:T(8,128)(2,1)S(1)} fusion(f32[3,512,1536]{2,1,0:T(8,128)} %fusion.92, f32[3,512]{1,0:T(4,128)S(1)} %get-tuple-element.44, pred[1536]{0:T(1024)(128)(4,1)S(1)} %fusion.102, bf16[1024,3,128]{2,0,1:T(8,128)(2,1)S(1)} %copy-done.18, bf16[512,3,128]{2,0,1:T(8,128)(2,1)S(1)} %fusion.97), kind=kOutput, calls=%fused_computation.126 | convolution fusion | flops 615972864 | bytes 11017728 | tf_op jit(solution)/shard_map/hqk,khe->qhe/dot_general | solution.py:130
  302.9 3.7 add_convert_fusion
  308.0 3.4 collective-permute-start.16
  317.3 3.6 add_convert_fusion.1
  325.1 3.9 collective-permute-done.14
  329.7 15.0 %collective-permute-done.16 = bf16[512,768]{1,0:T(8,128)(2,1)} collective-permute-done((bf16[512,768]{1,0:T(8,128)(2,1)}, bf16[512,768]{1,0:T(8,128)(2,1)}, u32[]{:S(2)}, u32[]{:S(2)}) %collective-permute-start.16) | collective-permute-done | bytes 786464 | tf_op jit(solution)/shard_map/ppermute | solution.py:151
  349.0 13.6 %collective-permute-done.11 = bf16[512,768]{1,0:T(8,128)(2,1)} collective-permute-done((bf16[512,768]{1,0:T(8,128)(2,1)}, bf16[512,768]{1,0:T(8,128)(2,1)}, u32[]{:S(2)}, u32[]{:S(2)}) %collective-permute-start.11) | collective-permute-done | bytes 786464 | tf_op jit(solution)/shard_map/ppermute | solution.py:151
  362.7 15.9 %collective-permute-done.13 = bf16[512,768]{1,0:T(8,128)(2,1)} collective-permute-done((bf16[512,768]{1,0:T(8,128)(2,1)}, bf16[512,768]{1,0:T(8,128)(2,1)}, u32[]{:S(2)}, u32[]{:S(2)}) %collective-permute-start.13) | collective-permute-done | bytes 786464 | tf_op jit(solution)/shard_map/ppermute | solution.py:151
  396.9 3.9 fusion.37
  (180 shorter events, 82.2 us)
Async XLA Ops:
  7.2 71.3 %copy-start.24 = (bf16[1,1,2,768]{3,2,1,0:T(2,128)(2,1)S(1)}, bf16[1,1,2,768]{3,2,1,0:T(2,128)(2,1)}, u32[]{:S(2)}) copy-start(bf16[1,1,2,768]{3,2,1,0:T(2,128)(2,1)} %param.17) | copy-start | bytes 9220
  7.2 71.3 %copy-start.25 = (bf16[1,1,2,768]{3,2,1,0:T(2,128)(2,1)S(1)}, bf16[1,1,2,768]{3,2,1,0:T(2,128)(2,1)}, u32[]{:S(2)}) copy-start(bf16[1,1,2,768]{3,2,1,0:T(2,128)(2,1)} %param.16) | copy-start | bytes 9220
  7.2 71.3 %copy-start.20 = (bf16[1,1,512,768]{3,2,1,0:T(8,128)(2,1)S(1)}, bf16[1,1,512,768]{3,2,1,0:T(8,128)(2,1)}, u32[]{:S(2)}) copy-start(bf16[1,1,512,768]{3,2,1,0:T(8,128)(2,1)} %param.15) | copy-start | bytes 2359300
  7.2 71.3 %all-gather.3.cloned.1.call-start = ((), (), s32[]{:S(2)}) async-start(), calls=%async_computation | async-start | bytes 7520256 | tf_op jit(solution)/shard_map/all_gather | solution.py:96
  9.2 178.1 %all-gather.5.cloned.1.call-start = ((), (), s32[]{:S(2)}) async-start(), calls=%async_computation.1 | async-start | bytes 7520256 | tf_op jit(solution)/shard_map/all_gather | solution.py:102
  79.5 19.0 %collective-permute-start = (bf16[516,768]{1,0:T(8,128)(2,1)S(1)}, bf16[516,768]{1,0:T(8,128)(2,1)S(1)}, u32[]{:S(2)}, u32[]{:S(2)}) collective-permute-start(bf16[516,768]{1,0:T(8,128)(2,1)S(1)} %get-tuple-element.75), channel_id=1, source_target_pairs={{0,48},{16,0},{32,16},{48,32},{1,49},{17,1},{33,17},{49,33},{2,50}... | collective-permute-start | bytes 2377736 | tf_op jit(solution)/shard_map/ppermute | solution.py:23
  82.2 19.9 %collective-permute-start.1 = (bf16[516,768]{1,0:T(8,128)(2,1)S(1)}, bf16[516,768]{1,0:T(8,128)(2,1)S(1)}, u32[]{:S(2)}, u32[]{:S(2)}) collective-permute-start(bf16[516,768]{1,0:T(8,128)(2,1)S(1)} %get-tuple-element.75), channel_id=1, source_target_pairs={{0,16},{16,32},{32,48},{48,0},{1,17},{17,33},{33,49},{49,1},{2,18}... | collective-permute-start | bytes 2377736 | tf_op jit(solution)/shard_map/ppermute | solution.py:22
  98.6 10.5 %collective-permute-start.3 = (bf16[258,768]{1,0:T(8,128)(2,1)S(1)}, bf16[258,768]{1,0:T(8,128)(2,1)S(1)}, u32[]{:S(2)}, u32[]{:S(2)}) collective-permute-start(bf16[258,768]{1,0:T(8,128)(2,1)S(1)} %slice.226), channel_id=1, source_target_pairs={{0,48},{16,0},{32,16},{48,32},{1,49},{17,1},{33,17},{49,33},{2,50}... | collective-permute-start | bytes 1188872 | tf_op jit(solution)/shard_map/ppermute | solution.py:26
  102.1 10.2 %collective-permute-start.2 = (bf16[258,768]{1,0:T(8,128)(2,1)S(1)}, bf16[258,768]{1,0:T(8,128)(2,1)S(1)}, u32[]{:S(2)}, u32[]{:S(2)}) collective-permute-start(bf16[258,768]{1,0:T(8,128)(2,1)S(1)} %slice.225), channel_id=1, source_target_pairs={{0,16},{16,32},{32,48},{48,0},{1,17},{17,33},{33,49},{49,1},{2,18}... | collective-permute-start | bytes 1188872 | tf_op jit(solution)/shard_map/ppermute | solution.py:25
  102.2 44.0 %collective-permute-start.5 = (bf16[1024,768]{1,0:T(8,128)(2,1)}, bf16[1024,768]{1,0:T(8,128)(2,1)}, u32[]{:S(2)}, u32[]{:S(2)}) collective-permute-start(bf16[1024,768]{1,0:T(8,128)(2,1)} %bitcast.17), channel_id=1, source_target_pairs={{0,16},{16,32},{32,48},{48,0},{1,17},{17,33},{33,49},{49,1},{2,18}... | collective-permute-start | bytes 4718600 | tf_op jit(solution)/shard_map/ppermute | solution.py:22
  102.3 45.2 %collective-permute-start.4 = (bf16[1024,768]{1,0:T(8,128)(2,1)}, bf16[1024,768]{1,0:T(8,128)(2,1)}, u32[]{:S(2)}, u32[]{:S(2)}) collective-permute-start(bf16[1024,768]{1,0:T(8,128)(2,1)} %bitcast.17), channel_id=1, source_target_pairs={{0,48},{16,0},{32,16},{48,32},{1,49},{17,1},{33,17},{49,33},{2,50}... | collective-permute-start | bytes 4718600 | tf_op jit(solution)/shard_map/ppermute | solution.py:23
  124.9 81.6 %collective-permute-start.10 = (bf16[3072,3,384]{0,2,1:T(8,128)(2,1)}, bf16[3072,3,384]{0,2,1:T(8,128)(2,1)}, u32[]{:S(2)}, u32[]{:S(2)}) collective-permute-start(bf16[3072,3,384]{0,2,1:T(8,128)(2,1)} %copy.48), channel_id=1, source_target_pairs={{0,64},{64,0},{1,65},{65,1},{2,66},{66,2},{3,67},{67,3},{4,68},{68... | collective-permute-start | bytes 21233672 | tf_op jit(solution)/shard_map/ppermute | solution.py:105
  147.4 17.5 %collective-permute-start.6 = (bf16[512,768]{1,0:T(8,128)(2,1)S(1)}, bf16[512,768]{1,0:T(8,128)(2,1)S(1)}, u32[]{:S(2)}, u32[]{:S(2)}) collective-permute-start(bf16[512,768]{1,0:T(8,128)(2,1)S(1)} %slice.237), channel_id=1, source_target_pairs={{0,16},{16,32},{32,48},{48,0},{1,17},{17,33},{33,49},{49,1},{2,18}... | collective-permute-start | bytes 2359304 | tf_op jit(solution)/shard_map/ppermute | solution.py:25
  148.7 16.5 %collective-permute-start.7 = (bf16[512,768]{1,0:T(8,128)(2,1)S(1)}, bf16[512,768]{1,0:T(8,128)(2,1)S(1)}, u32[]{:S(2)}, u32[]{:S(2)}) collective-permute-start(bf16[512,768]{1,0:T(8,128)(2,1)S(1)} %slice.238), channel_id=1, source_target_pairs={{0,48},{16,0},{32,16},{48,32},{1,49},{17,1},{33,17},{49,33},{2,50}... | collective-permute-start | bytes 2359304 | tf_op jit(solution)/shard_map/ppermute | solution.py:26
  202.3 42.0 %collective-permute-start.9 = (bf16[3072,2,384]{2,1,0:T(2,128)(2,1)}, bf16[3072,2,384]{2,1,0:T(2,128)(2,1)}, u32[]{:S(2)}, u32[]{:S(2)}) collective-permute-start(bf16[3072,2,384]{2,1,0:T(2,128)(2,1)} %reshape.317), channel_id=1, source_target_pairs={{0,64},{64,0},{1,65},{65,1},{2,66},{66,2},{3,67},{67,3},{4,68},{68... | collective-permute-start | bytes 14155784 | tf_op jit(solution)/shard_map/ppermute | solution.py:108
  233.6 69.2 %collective-permute-start.8 = (bf16[384,3072]{0,1:T(8,128)(2,1)}, bf16[384,3072]{0,1:T(8,128)(2,1)}, u32[]{:S(2)}, u32[]{:S(2)}) collective-permute-start(bf16[384,3072]{0,1:T(8,128)(2,1)} %get-tuple-element.46), channel_id=1, source_target_pairs={{0,64},{64,0},{1,65},{65,1},{2,66},{66,2},{3,67},{67,3},{4,68},{68... | collective-permute-start | bytes 7077896 | tf_op jit(solution)/shard_map/ppermute | solution.py:108
  268.7 23.1 %slice-start.1 = ((s8[9437184]{0:T(1024)(128)(4,1)}), s8[4194304]{0:T(1024)(128)(4,1)S(1)}, s32[]{:S(2)}) async-start(s8[9437184]{0:T(1024)(128)(4,1)} %bitcast.332), calls=%async_computation.3 | async-start | bytes 8388608
  308.0 21.0 %collective-permute-start.14 = (bf16[512,768]{1,0:T(8,128)(2,1)S(1)}, bf16[512,768]{1,0:T(8,128)(2,1)}, u32[]{:S(2)}, u32[]{:S(2)}) collective-permute-start(bf16[512,768]{1,0:T(8,128)(2,1)S(1)} %get-tuple-element.71), channel_id=1, source_target_pairs={{0,16},{16,32},{32,48},{48,0},{1,17},{17,33},{33,49},{49,1},{2,18}... | collective-permute-start | bytes 2359304 | tf_op jit(solution)/shard_map/ppermute | solution.py:151
  308.0 36.7 %collective-permute-start.16 = (bf16[512,768]{1,0:T(8,128)(2,1)}, bf16[512,768]{1,0:T(8,128)(2,1)}, u32[]{:S(2)}, u32[]{:S(2)}) collective-permute-start(bf16[512,768]{1,0:T(8,128)(2,1)} %get-tuple-element.72), channel_id=1, source_target_pairs={{0,48},{16,0},{32,16},{48,32},{1,49},{17,1},{33,17},{49,33},{2,50}... | collective-permute-start | bytes 2359304 | tf_op jit(solution)/shard_map/ppermute | solution.py:151
  311.4 35.4 %collective-permute-start.15 = (bf16[512,768]{1,0:T(8,128)(2,1)}, bf16[512,768]{1,0:T(8,128)(2,1)}, u32[]{:S(2)}, u32[]{:S(2)}) collective-permute-start(bf16[512,768]{1,0:T(8,128)(2,1)} %get-tuple-element.73), channel_id=1, source_target_pairs={{0,32},{16,48},{32,0},{48,16},{1,33},{17,49},{33,1},{49,17},{2,34}... | collective-permute-start | bytes 2359304 | tf_op jit(solution)/shard_map/ppermute | solution.py:151
  322.4 40.2 %collective-permute-start.11 = (bf16[512,768]{1,0:T(8,128)(2,1)}, bf16[512,768]{1,0:T(8,128)(2,1)}, u32[]{:S(2)}, u32[]{:S(2)}) collective-permute-start(bf16[512,768]{1,0:T(8,128)(2,1)} %get-tuple-element.68), channel_id=1, source_target_pairs={{0,16},{16,32},{32,48},{48,0},{1,17},{17,33},{33,49},{49,1},{2,18}... | collective-permute-start | bytes 2359304 | tf_op jit(solution)/shard_map/ppermute | solution.py:151
  323.3 55.3 %collective-permute-start.13 = (bf16[512,768]{1,0:T(8,128)(2,1)}, bf16[512,768]{1,0:T(8,128)(2,1)}, u32[]{:S(2)}, u32[]{:S(2)}) collective-permute-start(bf16[512,768]{1,0:T(8,128)(2,1)} %get-tuple-element.69), channel_id=1, source_target_pairs={{0,48},{16,0},{32,16},{48,32},{1,49},{17,1},{33,17},{49,33},{2,50}... | collective-permute-start | bytes 2359304 | tf_op jit(solution)/shard_map/ppermute | solution.py:151
  329.0 51.5 %collective-permute-start.12 = (bf16[512,768]{1,0:T(8,128)(2,1)}, bf16[512,768]{1,0:T(8,128)(2,1)}, u32[]{:S(2)}, u32[]{:S(2)}) collective-permute-start(bf16[512,768]{1,0:T(8,128)(2,1)} %get-tuple-element.70), channel_id=1, source_target_pairs={{0,32},{16,48},{32,0},{48,16},{1,33},{17,49},{33,1},{49,17},{2,34}... | collective-permute-start | bytes 2359304 | tf_op jit(solution)/shard_map/ppermute | solution.py:151
  349.0 36.1 %copy-start.4 = (f32[512,768]{1,0:T(8,128)}, f32[512,768]{1,0:T(8,128)S(1)}, u32[]{:S(2)}) copy-start(f32[512,768]{1,0:T(8,128)S(1)} %fusion.73) | copy-start | bytes 4718596
  349.0 33.4 %copy-start.27 = (bf16[768,64]{0,1:T(8,128)(2,1)S(1)}, bf16[768,64]{0,1:T(8,128)(2,1)}, u32[]{:S(2)}) copy-start(bf16[768,64]{0,1:T(8,128)(2,1)} %param.23) | copy-start | bytes 294916
  385.4 9.7 %collective-permute-start.23 = (f32[128,64]{0,1:T(8,128)S(1)}, f32[128,64]{0,1:T(8,128)S(1)}, u32[]{:S(2)}, u32[]{:S(2)}) collective-permute-start(f32[128,64]{0,1:T(8,128)S(1)} %bitcast.361), channel_id=1, source_target_pairs={{0,112},{16,0},{32,16},{48,32},{64,48},{80,64},{96,80},{112,96},{1... | collective-permute-start | bytes 98312 | tf_op jit(solution)/shard_map/ppermute | solution.py:167
  388.5 6.9 %collective-permute-start.17 = (f32[128,64]{0,1:T(8,128)S(1)}, f32[128,64]{0,1:T(8,128)S(1)}, u32[]{:S(2)}, u32[]{:S(2)}) collective-permute-start(f32[128,64]{0,1:T(8,128)S(1)} %bitcast.360), channel_id=1, source_target_pairs={{0,16},{16,32},{32,48},{48,64},{64,80},{80,96},{96,112},{112,0},{1... | collective-permute-start | bytes 98312 | tf_op jit(solution)/shard_map/ppermute | solution.py:167
  391.1 9.7 %collective-permute-start.22 = (f32[128,64]{0,1:T(8,128)S(1)}, f32[128,64]{0,1:T(8,128)S(1)}, u32[]{:S(2)}, u32[]{:S(2)}) collective-permute-start(f32[128,64]{0,1:T(8,128)S(1)} %bitcast.359), channel_id=1, source_target_pairs={{0,96},{16,112},{32,0},{48,16},{64,32},{80,48},{96,64},{112,80},{1... | collective-permute-start | bytes 98312 | tf_op jit(solution)/shard_map/ppermute | solution.py:167
  392.7 8.1 %collective-permute-start.21 = (f32[128,64]{0,1:T(8,128)S(1)}, f32[128,64]{0,1:T(8,128)S(1)}, u32[]{:S(2)}, u32[]{:S(2)}) collective-permute-start(f32[128,64]{0,1:T(8,128)S(1)} %bitcast.358), channel_id=1, source_target_pairs={{0,80},{16,96},{32,112},{48,0},{64,16},{80,32},{96,48},{112,64},{1... | collective-permute-start | bytes 98312 | tf_op jit(solution)/shard_map/ppermute | solution.py:167
  393.8 7.1 %collective-permute-start.20 = (f32[128,64]{0,1:T(8,128)S(1)}, f32[128,64]{0,1:T(8,128)S(1)}, u32[]{:S(2)}, u32[]{:S(2)}) collective-permute-start(f32[128,64]{0,1:T(8,128)S(1)} %bitcast.357), channel_id=1, source_target_pairs={{0,64},{16,80},{32,96},{48,112},{64,0},{80,16},{96,32},{112,48},{1... | collective-permute-start | bytes 98312 | tf_op jit(solution)/shard_map/ppermute | solution.py:167
  395.1 5.8 %collective-permute-start.19 = (f32[128,64]{0,1:T(8,128)S(1)}, f32[128,64]{0,1:T(8,128)S(1)}, u32[]{:S(2)}, u32[]{:S(2)}) collective-permute-start(f32[128,64]{0,1:T(8,128)S(1)} %bitcast.356), channel_id=1, source_target_pairs={{0,48},{16,64},{32,80},{48,96},{64,112},{80,0},{96,16},{112,32},{1... | collective-permute-start | bytes 98312 | tf_op jit(solution)/shard_map/ppermute | solution.py:167
  395.4 5.5 %collective-permute-start.18 = (f32[128,64]{0,1:T(8,128)S(1)}, f32[128,64]{0,1:T(8,128)S(1)}, u32[]{:S(2)}, u32[]{:S(2)}) collective-permute-start(f32[128,64]{0,1:T(8,128)S(1)} %bitcast.355), channel_id=1, source_target_pairs={{0,32},{16,48},{32,64},{48,80},{64,96},{80,112},{96,0},{112,16},{1... | collective-permute-start | bytes 98312 | tf_op jit(solution)/shard_map/ppermute | solution.py:167
  (30 other events, 222.2 us)
Sparse Core Ops, SparseCore 0:
  10.7 67.7 all-gather.2
  80.6 64.4 all-gather.4

commit v2 on v1

--- a/solution.py
+++ b/solution.py
@@ -49,7 +49,7 @@
 
 
 def add_rows(piece, ready):
-    return jnp.dot(ready, piece.reshape(piece.shape[0], -1), preferred_element_type=jnp.float32)
+    return jnp.einsum("ti,sin->tsn", ready, piece, preferred_element_type=jnp.float32)
 
 
 def layer(
@@ -93,15 +93,15 @@
     def own_half(weight, axis):
         return lax.dynamic_slice_in_dim(weight, core * half, half, axis=axis)
 
-    img_w = lax.all_gather(own_half(img_qkv_weight, 2), "col", axis=0, tiled=True)
-    rows_here = txt_kv_weight.shape[0]
+    img_piece = jnp.transpose(own_half(img_qkv_weight, 2), (1, 0, 2))
+    img_w = lax.all_gather(img_piece, "col", axis=1, tiled=True)
     txt_out_piece = jnp.concatenate(
-        [own_half(txt_kv_weight, 2).reshape(rows_here, -1), own_half(out_weight, 0).T], 1
+        [jnp.transpose(own_half(txt_kv_weight, 2), (1, 0, 2)), own_half(out_weight, 0).T[None]], 0
     )
     img_w, txt_out_piece = lax.optimization_barrier((img_w, txt_out_piece))
-    txt_out_w = lax.all_gather(txt_out_piece, "col", axis=0, tiled=True)
-    txt_w = txt_out_w[:, : 2 * half].reshape(width, 2, half)
-    out_w = txt_out_w[:, 2 * half :].T
+    txt_out_w = lax.all_gather(txt_out_piece, "col", axis=1, tiled=True)
+    txt_w = txt_out_w[:2]
+    out_w = txt_out_w[2]
     img_w_other = lax.ppermute(img_w, "cfg", swap)
     halves = [
         (txt_w, img_w, out_w),
@@ -130,9 +130,9 @@
         mixed = jnp.einsum("hqk,khe->qhe", chances, value_rows, preferred_element_type=jnp.float32)
         outputs = mixed.reshape(queries.shape[0], half).astype(jnp.bfloat16)
         return jnp.einsum(
-            "ti,iko->kto",
+            "ti,koi->kto",
             outputs,
-            out_w.reshape(half, n_row, local_width),
+            out_w.reshape(n_row, local_width, half),
             preferred_element_type=jnp.float32,
         )
 
@@ -147,7 +147,9 @@
         term_blocks = part.astype(jnp.bfloat16)
         got = lax.dynamic_index_in_dim(term_blocks, me_row, 0, keepdims=False).astype(jnp.float32)
         for step in range(1, n_row):
-            outgoing = lax.dynamic_index_in_dim(term_blocks, (me_row + step) % n_row, 0, keepdims=False)
+            outgoing = lax.dynamic_index_in_dim(
+                term_blocks, (me_row + step) % n_row, 0, keepdims=False
+            )
             got = got + lax.ppermute(outgoing, "row", shift_pairs(n_row, step)).astype(jnp.float32)
         pieces.append(got)
     projected = jnp.concatenate(pieces, 0)

time: 416 us -> 422 us (1.014)
  other arithmetic: 34.2 us -> 39.2 us
  starting transfers between devices: 37.6 us -> 32.6 us
  local copies, waits for them, and re-layouts: 56.2 us -> 61.1 us
    unnamed x76 -> x96, local copies, waits for them, and re-layouts: 3.39 us -> 22.5 us
    ppermute x2, waiting for transfers between devices: 15.5 us -> 29.7 us  [ring_gather(): from_prev = lax.ppermute(piece, axis_name, shift_pairs(size, 1))]
    ppermute x1 -> x0, local copies, waits for them, and re-layouts: 12.9 us -> none  [layer(): lax.ppermute(txt_w, 'cfg', swap)]
    reshape x1 -> x0, local copies, waits for them, and re-layouts: 10.1 us -> none  [layer(): txt_w = txt_out_w[:, :2 * half].reshape(width, 2, half)]
    ppermute x2, waiting for transfers between devices: 12.8 us -> 3.24 us  [ring_gather(): far_top = lax.ppermute(from_prev[:cut], axis_name, shift_pairs(size, 1))]
  transfers between devices with their start and end apart: 26 -> 26, of which waited for: 13 -> 11; matrix products, arithmetic and copies ran while one was open for 42% -> 40% of each run, Pallas kernels for 0% -> 0%
where the time goes in v2:
time: 422 us; the launch traced here: 416 us
  waiting for transfers between devices  169 us (40%)
  matrix products  95.1 us (23%)
  local copies, waits for them, and re-layouts  61.1 us (14%)
  other arithmetic  39.2 us (9%)
  starting transfers between devices  32.6 us (8%)
  between operations  18.7 us (4%)
    all_gather x1, waiting for transfers between devices, layer(): img_w = lax.all_gather(img_piece, 'col', axis=1, tiled=True)  66.3 us
    ppermute x6, waiting for transfers between devices, layer(): lax.ppermute(outgoing, 'row', shift_pairs(n_row, step)).astype(jnp.float32)  49.8 us
    dot_general x4, matrix products, attend(): jnp.einsum('qhe,khe->hqk', queries, key_rows, preferred_element_type=jnp....  33.2 us
    dot_general x4, matrix products, add_rows(): jnp.einsum('ti,sin->tsn', ready, piece, preferred_element_type=jnp.float32)  32.1 us
    ppermute x2, waiting for transfers between devices, ring_gather(): from_prev = lax.ppermute(piece, axis_name, shift_pairs(size, 1))  29.7 us
    unnamed x96, local copies, waits for them, and re-layouts  22.5 us
    ppermute x2, waiting for transfers between devices, ring_gather(): from_next = lax.ppermute(piece, axis_name, shift_pairs(size, -1))  16.3 us
    dot_general x4, matrix products, attend(): jnp.einsum('hqk,khe->qhe', chances, value_rows, preferred_element_type=jn...  16.1 us
  transfers between devices with their start and end apart: 26, of which 11 were waited for; matrix products, arithmetic and copies ran while one was open for 40% of the time, Pallas kernels for 0%

profile of v2, /device:TPU:1, one launch (start us, length us, event | category | flops | bytes accessed | tf_op | source)
XLA Modules:
  0.0 415.6 jit_solution(6785536592242910544)
XLA Ops:
  12.2 66.3 %all-gather.3.cloned.1.call-done = bf16[3,3072,384]{2,1,0:T(8,128)(2,1)} async-done(((bf16[3,192,384]{2,1,0:T(8,128)(2,1)}), bf16[3,3072,384]{2,1,0:T(8,128)(2,1)}) %all-gather.3.cloned.1.call-update) | async-done | bytes 7077904 | tf_op jit(solution)/shard_map/all_gather | solution.py:97
  82.2 16.3 %collective-permute-done = bf16[516,768]{1,0:T(8,128)(2,1)S(1)} collective-permute-done((bf16[516,768]{1,0:T(8,128)(2,1)S(1)}, bf16[516,768]{1,0:T(8,128)(2,1)S(1)}, u32[]{:S(2)}, u32[]{:S(2)}) %collective-permute-start) | collective-permute-done | bytes 792608 | tf_op jit(solution)/shard_map/ppermute | solution.py:23
  98.6 3.5 collective-permute-start.3
  105.6 3.5 collective-permute-done.3
  109.1 3.2 collective-permute-done.2
  116.5 29.7 %collective-permute-done.5 = bf16[1024,768]{1,0:T(8,128)(2,1)} collective-permute-done((bf16[1024,768]{1,0:T(8,128)(2,1)}, bf16[1024,768]{1,0:T(8,128)(2,1)}, u32[]{:S(2)}, u32[]{:S(2)}) %collective-permute-start.5) | collective-permute-done | bytes 1572896 | tf_op jit(solution)/shard_map/ppermute | solution.py:22
  153.0 10.3 %copy.40 = bf16[3,3072,384]{1,2,0:T(8,128)(2,1)} copy(bf16[3,3072,384]{2,1,0:T(8,128)(2,1)} %all-gather.3.cloned.1.call-done) | data formatting | bytes 14155776 | tf_op jit(solution)/shard_map/optimization_barrier | solution.py:101
  163.3 3.6 collective-permute-start.10
  167.0 2.9 fusion.48
  171.4 3.4 pad_maximum_fusion
  178.0 4.8 %fusion.14 = (bf16[1024,768]{1,0:T(8,128)(2,1)}, bf16[1024,768]{1,0:T(8,128)(2,1)}, bf16[1024,768]{1,0:T(8,128)(2,1)}, bf16[1024,768]{1,0:T(8,128)(2,1)}) fusion(f32[768]{0:T(1024)S(1)} %get-tuple-element.85, f32[768]{0:T(1024)S(1)} %get-tuple-element.86, f32[1024]{0:T(1024)S(1)} %add_rsqrt_fusion.6, f32[1024]{0:T(1024)S(1)} %add_multiply_fusion, ...), kind=kLoop, calls=%fused_computation.35 | loop fusion | flops 18874368 | bytes 12615696 | tf_op jit(solution)/shard_map/convert_element_type | solution.py:40
  182.9 11.5 %fusion.41 = f32[1024,3,384]{0,2,1:T(8,128)} fusion(bf16[3,3072,384]{2,1,0:T(8,128)(2,1)S(1)} %bitcast.330, bf16[1024,768]{1,0:T(8,128)(2,1)} %get-tuple-element.47, bf16[1024,768]{1,0:T(8,128)(2,1)} %get-tuple-element.46, bf16[1024,768]{1,0:T(8,128)(2,1)} %get-tuple-element.45, bf16[1024,768]{1,0:T(8,128)(2,1)} %get-tuple-element.44), kind=kOutput, calls=%fused_computation.65 | convolution fusion | flops 7272923136 | bytes 18087936 | tf_op jit(solution)/shard_map/ti,sin->tsn/dot_general | solution.py:52
  194.4 3.4 fusion.154
  206.6 10.6 %fusion.40 = f32[1024,3,384]{0,2,1:T(8,128)S(1)} fusion(bf16[3,3072,384]{1,2,0:T(8,128)(2,1)} %collective-permute-done.10, bf16[1024,768]{1,0:T(8,128)(2,1)S(1)} %copy-done.15, bf16[1024,768]{1,0:T(8,128)(2,1)S(1)} %copy-done.14, bf16[1024,768]{1,0:T(8,128)(2,1)S(1)} %copy-done.13, bf16[1024,768]{1,0:T(8,128)(2,1)S(1)} %copy-done.12), kind=kOutput, calls=%fused_computation.64 | convolution fusion | flops 7272923136 | bytes 18087936 | tf_op jit(solution)/shard_map/ti,sin->tsn/dot_general | solution.py:52
  223.4 4.9 %slice.235 = bf16[2,3072,384]{2,1,0:T(8,128)(2,1)} slice(bf16[3,3072,384]{2,1,0:T(8,128)(2,1)} %all-gather.5.cloned.1.call-done), slice={[0:2], [0:3072], [0:384]} | slice | bytes 9437184
  228.3 6.7 %copy.57 = bf16[2,3072,384]{1,2,0:T(8,128)(2,1)} copy(bf16[2,3072,384]{2,1,0:T(8,128)(2,1)} %slice.235) | data formatting | bytes 9437184
  241.6 5.0 %fusion.85 = f32[512,2,384]{0,2,1:T(8,128)S(1)} fusion(bf16[512,768]{1,0:T(8,128)(2,1)S(1)} %copy-done.24, bf16[512,768]{1,0:T(8,128)(2,1)S(1)} %copy-done.22, bf16[512,768]{1,0:T(8,128)(2,1)S(1)} %copy-done.20, bf16[512,768]{1,0:T(8,128)(2,1)S(1)} %copy-done.18, bf16[3,3072,384]{2,1,0:T(8,128)(2,1)} %all-gather.5.cloned.1.call-done), kind=kOutput, calls=%fused_computation.129 | convolution fusion | flops 2428502016 | bytes 9437184 | tf_op jit(solution)/shard_map/ti,sin->tsn/dot_general | solution.py:52
  248.1 3.5 slice_bitcast_fusion
  253.6 5.0 %fusion.104 = f32[3,512,1536]{2,1,0:T(8,128)} fusion(bf16[1024,3,128]{2,0,1:T(8,128)(2,1)S(1)} %copy-done.3, bf16[512,3,128]{2,0,1:T(8,128)(2,1)S(1)} %fusion.101, bf16[1024,3,128]{2,0,1:T(8,128)(2,1)S(1)} %copy-done.6), kind=kOutput, calls=%fused_computation.162 | convolution fusion | flops 606339072 | bytes 11010048 | tf_op jit(solution)/shard_map/qhe,khe->hqk/dot_general | solution.py:125
  258.6 5.0 %fusion.105 = f32[3,512,1536]{2,1,0:T(8,128)} fusion(bf16[1024,3,128]{2,0,1:T(8,128)(2,1)S(1)} %copy-done.3, bf16[512,3,128]{2,0,1:T(8,128)(2,1)S(1)} %fusion.101, bf16[1024,3,128]{2,0,1:T(8,128)(2,1)S(1)} %copy-done.6), kind=kOutput, calls=%fused_computation.163 | convolution fusion | flops 606339072 | bytes 11010048 | tf_op jit(solution)/shard_map/qhe,khe->hqk/dot_general | solution.py:125
  263.7 5.0 %fusion.84 = f32[512,2,384]{0,2,1:T(8,128)S(1)} fusion(bf16[2,3072,384]{1,2,0:T(8,128)(2,1)} %collective-permute-done.9, bf16[512,768]{1,0:T(8,128)(2,1)S(1)} %copy-done.25, bf16[512,768]{1,0:T(8,128)(2,1)S(1)} %copy-done.23, bf16[512,768]{1,0:T(8,128)(2,1)S(1)} %copy-done.21, bf16[512,768]{1,0:T(8,128)(2,1)S(1)} %copy-done.19), kind=kOutput, calls=%fused_computation.128 | convolution fusion | flops 2428502016 | bytes 9437184 | tf_op jit(solution)/shard_map/ti,sin->tsn/dot_general | solution.py:52
  272.7 6.4 %fusion.102 = f32[3,512,1536]{2,1,0:T(8,128)} fusion(bf16[1024,3,128]{2,0,1:T(8,128)(2,1)} %fusion.75, bf16[512,3,128]{2,0,1:T(8,128)(2,1)S(1)} %fusion.99, bf16[1024,3,128]{2,0,1:T(8,128)(2,1)} %fusion.77), kind=kOutput, calls=%fused_computation.160 | convolution fusion | flops 606339072 | bytes 11010048 | tf_op jit(solution)/shard_map/qhe,khe->hqk/dot_general | solution.py:125
  279.2 16.8 %fusion.1 = (f32[3,512]{1,0:T(4,128)S(1)}, f32[3,512]{1,0:T(4,128)S(1)}, f32[3,512]{1,0:T(4,128)S(1)}, f32[3,512]{1,0:T(4,128)S(1)}, f32[3,512,1536]{2,1,0:T(8,128)}) fusion(pred[1536]{0:T(1024)(128)(4,1)S(1)} %fusion.112, f32[3,512,1536]{2,1,0:T(8,128)} %fusion.104, f32[3,512,1536]{2,1,0:T(8,128)} %fusion.102, f32[3,512,1536]{2,1,0:T(8,128)} %fusion.105, ...), kind=kOutput, calls=%fused_computation.9 | convolution fusion | flops 634644480 | bytes 39348224 | tf_op jit(solution)/shard_map/qhe,khe->hqk/dot_general | solution.py:125
  296.0 5.3 %fusion.89 = bf16[3,128,512]{2,1,0:T(8,128)(2,1)S(1)} fusion(f32[3,512,1536]{2,1,0:T(8,128)} %fusion.105, f32[3,512]{1,0:T(4,128)S(1)} %get-tuple-element.41, pred[1536]{0:T(1024)(128)(4,1)S(1)} %fusion.112, bf16[1024,3,128]{0,2,1:T(8,128)(2,1)S(1)} %copy-done.26, bf16[512,3,128]{0,2,1:T(8,128)(2,1)S(1)} %fusion.106), kind=kOutput, calls=%fused_computation.133 | convolution fusion | flops 615972864 | bytes 11017728 | tf_op jit(solution)/shard_map/hqk,khe->qhe/dot_general | solution.py:130
  309.8 3.6 add_convert_fusion
  314.9 3.4 collective-permute-start.16
  319.5 5.5 %fusion.88 = bf16[3,128,512]{2,1,0:T(8,128)(2,1)S(1)} fusion(f32[3,512,1536]{2,1,0:T(8,128)} %get-tuple-element.82, f32[3,512]{1,0:T(4,128)S(1)} %get-tuple-element.38, pred[1536]{0:T(1024)(128)(4,1)S(1)} %fusion.112, bf16[1024,3,128]{0,2,1:T(8,128)(2,1)S(1)} %copy-done.27, bf16[512,3,128]{0,2,1:T(8,128)(2,1)S(1)} %fusion.107), kind=kOutput, calls=%fused_computation.132 | convolution fusion | flops 615972864 | bytes 11017728 | tf_op jit(solution)/shard_map/hqk,khe->qhe/dot_general | solution.py:130
  326.9 3.6 add_convert_fusion.1
  336.8 15.1 %collective-permute-done.16 = bf16[512,768]{1,0:T(8,128)(2,1)} collective-permute-done((bf16[512,768]{1,0:T(8,128)(2,1)}, bf16[512,768]{1,0:T(8,128)(2,1)}, u32[]{:S(2)}, u32[]{:S(2)}) %collective-permute-start.16) | collective-permute-done | bytes 786464 | tf_op jit(solution)/shard_map/ppermute | solution.py:153
  356.1 13.4 %collective-permute-done.11 = bf16[512,768]{1,0:T(8,128)(2,1)} collective-permute-done((bf16[512,768]{1,0:T(8,128)(2,1)}, bf16[512,768]{1,0:T(8,128)(2,1)}, u32[]{:S(2)}, u32[]{:S(2)}) %collective-permute-start.11) | collective-permute-done | bytes 786464 | tf_op jit(solution)/shard_map/ppermute | solution.py:153
  369.5 16.1 %collective-permute-done.13 = bf16[512,768]{1,0:T(8,128)(2,1)} collective-permute-done((bf16[512,768]{1,0:T(8,128)(2,1)}, bf16[512,768]{1,0:T(8,128)(2,1)}, u32[]{:S(2)}, u32[]{:S(2)}) %collective-permute-start.13) | collective-permute-done | bytes 786464 | tf_op jit(solution)/shard_map/ppermute | solution.py:153
  403.7 3.9 fusion.37
  (204 shorter events, 95.3 us)
Async XLA Ops:
  7.2 71.3 %copy-start.31 = (bf16[1,1,2,768]{3,2,1,0:T(2,128)(2,1)S(1)}, bf16[1,1,2,768]{3,2,1,0:T(2,128)(2,1)}, u32[]{:S(2)}) copy-start(bf16[1,1,2,768]{3,2,1,0:T(2,128)(2,1)} %param.17) | copy-start | bytes 9220
  7.2 71.3 %copy-start.32 = (bf16[1,1,2,768]{3,2,1,0:T(2,128)(2,1)S(1)}, bf16[1,1,2,768]{3,2,1,0:T(2,128)(2,1)}, u32[]{:S(2)}) copy-start(bf16[1,1,2,768]{3,2,1,0:T(2,128)(2,1)} %param.16) | copy-start | bytes 9220
  7.2 71.3 %copy-start.28 = (bf16[1,1,512,768]{3,2,1,0:T(8,128)(2,1)S(1)}, bf16[1,1,512,768]{3,2,1,0:T(8,128)(2,1)}, u32[]{:S(2)}) copy-start(bf16[1,1,512,768]{3,2,1,0:T(8,128)(2,1)} %param.15) | copy-start | bytes 2359300
  7.2 71.3 %all-gather.3.cloned.1.call-start = ((), (), s32[]{:S(2)}) async-start(), calls=%async_computation | async-start | bytes 7520256 | tf_op jit(solution)/shard_map/all_gather | solution.py:97
  9.2 214.2 %all-gather.5.cloned.1.call-start = ((), (), s32[]{:S(2)}) async-start(), calls=%async_computation.1 | async-start | bytes 7520256 | tf_op jit(solution)/shard_map/all_gather | solution.py:102
  79.5 19.0 %collective-permute-start = (bf16[516,768]{1,0:T(8,128)(2,1)S(1)}, bf16[516,768]{1,0:T(8,128)(2,1)S(1)}, u32[]{:S(2)}, u32[]{:S(2)}) collective-permute-start(bf16[516,768]{1,0:T(8,128)(2,1)S(1)} %get-tuple-element.71), channel_id=1, source_target_pairs={{0,48},{16,0},{32,16},{48,32},{1,49},{17,1},{33,17},{49,33},{2,50}... | collective-permute-start | bytes 2377736 | tf_op jit(solution)/shard_map/ppermute | solution.py:23
  82.2 19.9 %collective-permute-start.1 = (bf16[516,768]{1,0:T(8,128)(2,1)S(1)}, bf16[516,768]{1,0:T(8,128)(2,1)S(1)}, u32[]{:S(2)}, u32[]{:S(2)}) collective-permute-start(bf16[516,768]{1,0:T(8,128)(2,1)S(1)} %get-tuple-element.71), channel_id=1, source_target_pairs={{0,16},{16,32},{32,48},{48,0},{1,17},{17,33},{33,49},{49,1},{2,18}... | collective-permute-start | bytes 2377736 | tf_op jit(solution)/shard_map/ppermute | solution.py:22
  98.6 10.5 %collective-permute-start.3 = (bf16[258,768]{1,0:T(8,128)(2,1)S(1)}, bf16[258,768]{1,0:T(8,128)(2,1)S(1)}, u32[]{:S(2)}, u32[]{:S(2)}) collective-permute-start(bf16[258,768]{1,0:T(8,128)(2,1)S(1)} %slice.226), channel_id=1, source_target_pairs={{0,48},{16,0},{32,16},{48,32},{1,49},{17,1},{33,17},{49,33},{2,50}... | collective-permute-start | bytes 1188872 | tf_op jit(solution)/shard_map/ppermute | solution.py:26
  102.1 10.2 %collective-permute-start.2 = (bf16[258,768]{1,0:T(8,128)(2,1)S(1)}, bf16[258,768]{1,0:T(8,128)(2,1)S(1)}, u32[]{:S(2)}, u32[]{:S(2)}) collective-permute-start(bf16[258,768]{1,0:T(8,128)(2,1)S(1)} %slice.225), channel_id=1, source_target_pairs={{0,16},{16,32},{32,48},{48,0},{1,17},{17,33},{33,49},{49,1},{2,18}... | collective-permute-start | bytes 1188872 | tf_op jit(solution)/shard_map/ppermute | solution.py:25
  102.2 44.0 %collective-permute-start.5 = (bf16[1024,768]{1,0:T(8,128)(2,1)}, bf16[1024,768]{1,0:T(8,128)(2,1)}, u32[]{:S(2)}, u32[]{:S(2)}) collective-permute-start(bf16[1024,768]{1,0:T(8,128)(2,1)} %bitcast.20), channel_id=1, source_target_pairs={{0,16},{16,32},{32,48},{48,0},{1,17},{17,33},{33,49},{49,1},{2,18}... | collective-permute-start | bytes 4718600 | tf_op jit(solution)/shard_map/ppermute | solution.py:22
  102.3 46.0 %collective-permute-start.4 = (bf16[1024,768]{1,0:T(8,128)(2,1)}, bf16[1024,768]{1,0:T(8,128)(2,1)}, u32[]{:S(2)}, u32[]{:S(2)}) collective-permute-start(bf16[1024,768]{1,0:T(8,128)(2,1)} %bitcast.20), channel_id=1, source_target_pairs={{0,48},{16,0},{32,16},{48,32},{1,49},{17,1},{33,17},{49,33},{2,50}... | collective-permute-start | bytes 4718600 | tf_op jit(solution)/shard_map/ppermute | solution.py:23
  148.3 21.7 %collective-permute-start.6 = (bf16[512,768]{1,0:T(8,128)(2,1)}, bf16[512,768]{1,0:T(8,128)(2,1)}, u32[]{:S(2)}, u32[]{:S(2)}) collective-permute-start(bf16[512,768]{1,0:T(8,128)(2,1)} %slice.237), channel_id=1, source_target_pairs={{0,16},{16,32},{32,48},{48,0},{1,17},{17,33},{33,49},{49,1},{2,18}... | collective-permute-start | bytes 2359304 | tf_op jit(solution)/shard_map/ppermute | solution.py:25
  150.3 19.6 %collective-permute-start.7 = (bf16[512,768]{1,0:T(8,128)(2,1)}, bf16[512,768]{1,0:T(8,128)(2,1)}, u32[]{:S(2)}, u32[]{:S(2)}) collective-permute-start(bf16[512,768]{1,0:T(8,128)(2,1)} %slice.238), channel_id=1, source_target_pairs={{0,48},{16,0},{32,16},{48,32},{1,49},{17,1},{33,17},{49,33},{2,50}... | collective-permute-start | bytes 2359304 | tf_op jit(solution)/shard_map/ppermute | solution.py:26
  163.3 43.3 %collective-permute-start.10 = (bf16[3,3072,384]{1,2,0:T(8,128)(2,1)}, bf16[3,3072,384]{1,2,0:T(8,128)(2,1)}, u32[]{:S(2)}, u32[]{:S(2)}) collective-permute-start(bf16[3,3072,384]{1,2,0:T(8,128)(2,1)} %copy.40), channel_id=1, source_target_pairs={{0,64},{64,0},{1,65},{65,1},{2,66},{66,2},{3,67},{67,3},{4,68},{68... | collective-permute-start | bytes 21233672 | tf_op jit(solution)/shard_map/ppermute | solution.py:105
  235.0 28.7 %collective-permute-start.9 = (bf16[2,3072,384]{1,2,0:T(8,128)(2,1)}, bf16[2,3072,384]{1,2,0:T(8,128)(2,1)}, u32[]{:S(2)}, u32[]{:S(2)}) collective-permute-start(bf16[2,3072,384]{1,2,0:T(8,128)(2,1)} %copy.57), channel_id=1, source_target_pairs={{0,64},{64,0},{1,65},{65,1},{2,66},{66,2},{3,67},{67,3},{4,68},{68... | collective-permute-start | bytes 14155784 | tf_op jit(solution)/shard_map/ppermute | solution.py:108
  251.6 58.2 %collective-permute-start.8 = (bf16[3072,384]{1,0:T(8,128)(2,1)}, bf16[3072,384]{1,0:T(8,128)(2,1)}, u32[]{:S(2)}, u32[]{:S(2)}) collective-permute-start(bf16[3072,384]{1,0:T(8,128)(2,1)} %get-tuple-element.42), channel_id=1, source_target_pairs={{0,64},{64,0},{1,65},{65,1},{2,66},{66,2},{3,67},{67,3},{4,68},{68... | collective-permute-start | bytes 7077896 | tf_op jit(solution)/shard_map/ppermute | solution.py:108
  279.2 22.1 %slice-start = ((s8[9437184]{0:T(1024)(128)(4,1)}), s8[1048576]{0:T(1024)(128)(4,1)S(1)}, s32[]{:S(2)}) async-start(s8[9437184]{0:T(1024)(128)(4,1)} %bitcast.325), calls=%async_computation.2 | async-start | bytes 2097152
  314.9 21.1 %collective-permute-start.14 = (bf16[512,768]{1,0:T(8,128)(2,1)S(1)}, bf16[512,768]{1,0:T(8,128)(2,1)}, u32[]{:S(2)}, u32[]{:S(2)}) collective-permute-start(bf16[512,768]{1,0:T(8,128)(2,1)S(1)} %get-tuple-element.67), channel_id=1, source_target_pairs={{0,16},{16,32},{32,48},{48,0},{1,17},{17,33},{33,49},{49,1},{2,18}... | collective-permute-start | bytes 2359304 | tf_op jit(solution)/shard_map/ppermute | solution.py:153
  314.9 37.0 %collective-permute-start.16 = (bf16[512,768]{1,0:T(8,128)(2,1)}, bf16[512,768]{1,0:T(8,128)(2,1)}, u32[]{:S(2)}, u32[]{:S(2)}) collective-permute-start(bf16[512,768]{1,0:T(8,128)(2,1)} %get-tuple-element.68), channel_id=1, source_target_pairs={{0,48},{16,0},{32,16},{48,32},{1,49},{17,1},{33,17},{49,33},{2,50}... | collective-permute-start | bytes 2359304 | tf_op jit(solution)/shard_map/ppermute | solution.py:153
  318.4 35.5 %collective-permute-start.15 = (bf16[512,768]{1,0:T(8,128)(2,1)}, bf16[512,768]{1,0:T(8,128)(2,1)}, u32[]{:S(2)}, u32[]{:S(2)}) collective-permute-start(bf16[512,768]{1,0:T(8,128)(2,1)} %get-tuple-element.69), channel_id=1, source_target_pairs={{0,32},{16,48},{32,0},{48,16},{1,33},{17,49},{33,1},{49,17},{2,34}... | collective-permute-start | bytes 2359304 | tf_op jit(solution)/shard_map/ppermute | solution.py:153
  332.1 37.5 %collective-permute-start.11 = (bf16[512,768]{1,0:T(8,128)(2,1)}, bf16[512,768]{1,0:T(8,128)(2,1)}, u32[]{:S(2)}, u32[]{:S(2)}) collective-permute-start(bf16[512,768]{1,0:T(8,128)(2,1)} %get-tuple-element.64), channel_id=1, source_target_pairs={{0,16},{16,32},{32,48},{48,0},{1,17},{17,33},{33,49},{49,1},{2,18}... | collective-permute-start | bytes 2359304 | tf_op jit(solution)/shard_map/ppermute | solution.py:153
  332.9 52.7 %collective-permute-start.13 = (bf16[512,768]{1,0:T(8,128)(2,1)}, bf16[512,768]{1,0:T(8,128)(2,1)}, u32[]{:S(2)}, u32[]{:S(2)}) collective-permute-start(bf16[512,768]{1,0:T(8,128)(2,1)} %get-tuple-element.65), channel_id=1, source_target_pairs={{0,48},{16,0},{32,16},{48,32},{1,49},{17,1},{33,17},{49,33},{2,50}... | collective-permute-start | bytes 2359304 | tf_op jit(solution)/shard_map/ppermute | solution.py:153
  336.0 51.5 %collective-permute-start.12 = (bf16[512,768]{1,0:T(8,128)(2,1)}, bf16[512,768]{1,0:T(8,128)(2,1)}, u32[]{:S(2)}, u32[]{:S(2)}) collective-permute-start(bf16[512,768]{1,0:T(8,128)(2,1)} %get-tuple-element.66), channel_id=1, source_target_pairs={{0,32},{16,48},{32,0},{48,16},{1,33},{17,49},{33,1},{49,17},{2,34}... | collective-permute-start | bytes 2359304 | tf_op jit(solution)/shard_map/ppermute | solution.py:153
  356.1 36.1 %copy-start.4 = (f32[512,768]{1,0:T(8,128)}, f32[512,768]{1,0:T(8,128)S(1)}, u32[]{:S(2)}) copy-start(f32[512,768]{1,0:T(8,128)S(1)} %fusion.71) | copy-start | bytes 4718596
  356.1 33.4 %copy-start.34 = (bf16[768,64]{0,1:T(8,128)(2,1)S(1)}, bf16[768,64]{0,1:T(8,128)(2,1)}, u32[]{:S(2)}) copy-start(bf16[768,64]{0,1:T(8,128)(2,1)} %param.23) | copy-start | bytes 294916
  392.5 9.4 %collective-permute-start.23 = (f32[128,64]{0,1:T(8,128)S(1)}, f32[128,64]{0,1:T(8,128)S(1)}, u32[]{:S(2)}, u32[]{:S(2)}) collective-permute-start(f32[128,64]{0,1:T(8,128)S(1)} %bitcast.357), channel_id=1, source_target_pairs={{0,112},{16,0},{32,16},{48,32},{64,48},{80,64},{96,80},{112,96},{1... | collective-permute-start | bytes 98312 | tf_op jit(solution)/shard_map/ppermute | solution.py:169
  395.3 6.9 %collective-permute-start.17 = (f32[128,64]{0,1:T(8,128)S(1)}, f32[128,64]{0,1:T(8,128)S(1)}, u32[]{:S(2)}, u32[]{:S(2)}) collective-permute-start(f32[128,64]{0,1:T(8,128)S(1)} %bitcast.356), channel_id=1, source_target_pairs={{0,16},{16,32},{32,48},{48,64},{64,80},{80,96},{96,112},{112,0},{1... | collective-permute-start | bytes 98312 | tf_op jit(solution)/shard_map/ppermute | solution.py:169
  397.9 9.7 %collective-permute-start.22 = (f32[128,64]{0,1:T(8,128)S(1)}, f32[128,64]{0,1:T(8,128)S(1)}, u32[]{:S(2)}, u32[]{:S(2)}) collective-permute-start(f32[128,64]{0,1:T(8,128)S(1)} %bitcast.355), channel_id=1, source_target_pairs={{0,96},{16,112},{32,0},{48,16},{64,32},{80,48},{96,64},{112,80},{1... | collective-permute-start | bytes 98312 | tf_op jit(solution)/shard_map/ppermute | solution.py:169
  399.5 8.1 %collective-permute-start.21 = (f32[128,64]{0,1:T(8,128)S(1)}, f32[128,64]{0,1:T(8,128)S(1)}, u32[]{:S(2)}, u32[]{:S(2)}) collective-permute-start(f32[128,64]{0,1:T(8,128)S(1)} %bitcast.354), channel_id=1, source_target_pairs={{0,80},{16,96},{32,112},{48,0},{64,16},{80,32},{96,48},{112,64},{1... | collective-permute-start | bytes 98312 | tf_op jit(solution)/shard_map/ppermute | solution.py:169
  400.7 7.0 %collective-permute-start.20 = (f32[128,64]{0,1:T(8,128)S(1)}, f32[128,64]{0,1:T(8,128)S(1)}, u32[]{:S(2)}, u32[]{:S(2)}) collective-permute-start(f32[128,64]{0,1:T(8,128)S(1)} %bitcast.353), channel_id=1, source_target_pairs={{0,64},{16,80},{32,96},{48,112},{64,0},{80,16},{96,32},{112,48},{1... | collective-permute-start | bytes 98312 | tf_op jit(solution)/shard_map/ppermute | solution.py:169
  401.9 5.8 %collective-permute-start.19 = (f32[128,64]{0,1:T(8,128)S(1)}, f32[128,64]{0,1:T(8,128)S(1)}, u32[]{:S(2)}, u32[]{:S(2)}) collective-permute-start(f32[128,64]{0,1:T(8,128)S(1)} %bitcast.352), channel_id=1, source_target_pairs={{0,48},{16,64},{32,80},{48,96},{64,112},{80,0},{96,16},{112,32},{1... | collective-permute-start | bytes 98312 | tf_op jit(solution)/shard_map/ppermute | solution.py:169
  402.2 5.5 %collective-permute-start.18 = (f32[128,64]{0,1:T(8,128)S(1)}, f32[128,64]{0,1:T(8,128)S(1)}, u32[]{:S(2)}, u32[]{:S(2)}) collective-permute-start(f32[128,64]{0,1:T(8,128)S(1)} %bitcast.351), channel_id=1, source_target_pairs={{0,32},{16,48},{32,64},{48,80},{64,96},{80,112},{96,0},{112,16},{1... | collective-permute-start | bytes 98312 | tf_op jit(solution)/shard_map/ppermute | solution.py:169
  (37 other events, 232.3 us)
Sparse Core Ops, SparseCore 0:
  10.7 67.7 all-gather.2
  80.6 64.3 all-gather.4

commit v3 on v2

--- a/solution.py
+++ b/solution.py
@@ -26,6 +26,26 @@
     far_bottom = lax.ppermute(from_next[cut:], axis_name, shift_pairs(size, -1))
     far = jnp.concatenate([far_top, far_bottom], 0)
     return [piece, from_next, far, from_prev]
+
+
+def reduce_blocks(term_blocks, me, axis_name, size):
+    assert size == 4
+    rows = term_blocks.shape[1]
+    cut = rows // 2
+
+    def block(offset):
+        return lax.dynamic_index_in_dim(term_blocks, (me + offset) % size, 0, keepdims=False)
+
+    far = block(2)
+    up = lax.ppermute(jnp.concatenate([block(1), far[:cut]], 0), axis_name, shift_pairs(size, 1))
+    down = lax.ppermute(
+        jnp.concatenate([block(-1), far[cut:]], 0), axis_name, shift_pairs(size, -1)
+    )
+    far_top = lax.ppermute(up[rows:], axis_name, shift_pairs(size, 1))
+    far_bottom = lax.ppermute(down[rows:], axis_name, shift_pairs(size, -1))
+    got = block(0).astype(jnp.float32) + up[:rows].astype(jnp.float32)
+    got = got + down[:rows].astype(jnp.float32)
+    return got + jnp.concatenate([far_top, far_bottom], 0).astype(jnp.float32)
 
 
 def modulate_blocks(blocks, mods, width):
@@ -103,9 +123,10 @@
     txt_w = txt_out_w[:2]
     out_w = txt_out_w[2]
     img_w_other = lax.ppermute(img_w, "cfg", swap)
+    txt_out_other = lax.ppermute(txt_out_w, "cfg", swap)
     halves = [
         (txt_w, img_w, out_w),
-        (lax.ppermute(txt_w, "cfg", swap), img_w_other, lax.ppermute(out_w, "cfg", swap)),
+        (txt_out_other[:2], img_w_other, txt_out_other[2]),
     ]
     positions = jnp.arange(text_slots + images, dtype=jnp.int32)
     usable = (positions < txt_len[0, 0]) | (positions >= text_slots)
@@ -145,12 +166,7 @@
         for (queries, key_rows, value_rows), h in zip(projections, halves):
             part = part + attend(queries[c * chunk : (c + 1) * chunk], key_rows, value_rows, h[2])
         term_blocks = part.astype(jnp.bfloat16)
-        got = lax.dynamic_index_in_dim(term_blocks, me_row, 0, keepdims=False).astype(jnp.float32)
-        for step in range(1, n_row):
-            outgoing = lax.dynamic_index_in_dim(
-                term_blocks, (me_row + step) % n_row, 0, keepdims=False
-            )
-            got = got + lax.ppermute(outgoing, "row", shift_pairs(n_row, step)).astype(jnp.float32)
+        got = reduce_blocks(term_blocks, me_row, "row", n_row)
         pieces.append(got)
     projected = jnp.concatenate(pieces, 0)
     gating = img_gate[0].astype(jnp.float32)

time: 422 us -> 430 us (1.019)
  local copies, waits for them, and re-layouts: 61.1 us -> 68.6 us
  waiting for transfers between devices: 169 us -> 163 us
  starting transfers between devices: 32.6 us -> 38.1 us
    all_gather x0 -> x1, local copies, waits for them, and re-layouts: none -> 10.5 us  [layer(): txt_out_w = lax.all_gather(txt_out_piece, 'col', axis=1, tiled=True)]
    slice x0 -> x8, local copies, waits for them, and re-layouts: none -> 8.87 us  [the longest x1 3.26 us: layer(): txt_out_other[2]]
    unnamed x96 -> x98, local copies, waits for them, and re-layouts: 22.5 us -> 14.1 us
    ppermute x8 -> x9, waiting for transfers between devices: 49.8 us -> 43.4 us  [the longest x2 30.9 us: reduce_blocks(): lax.ppermute(jnp.concatenate([block(-1), far[cut:]], 0), axis_name, shift...]
    squeeze x3 -> x2, local copies, waits for them, and re-layouts: 6.49 us -> 0.33 us  [block(): lax.dynamic_index_in_dim(term_blocks, (me + offset) % size, 0, keepdims=F...]
    ppermute x8 -> x9, starting transfers between devices: 8.65 us -> 14.7 us  [the longest x2 6.89 us: reduce_blocks(): far_bottom = lax.ppermute(down[rows:], axis_name, shift_pairs(size, -1))]
    another operation x0 -> x1, local copies, waits for them, and re-layouts: none -> 4.4 us  [attend(): out_w.reshape(n_row, local_width, half)]
  transfers between devices with their start and end apart: 26 -> 27, of which waited for: 11 -> 11; matrix products, arithmetic and copies ran while one was open for 40% -> 32% of each run, Pallas kernels for 0% -> 0%
where the time goes in v3:
time: 430 us; the launch traced here: 422 us
  waiting for transfers between devices  163 us (38%)
  matrix products  91.9 us (21%)
  local copies, waits for them, and re-layouts  68.6 us (16%)
  other arithmetic  41.5 us (10%)
  starting transfers between devices  38.1 us (9%)
  between operations  18.5 us (4%)
    all_gather x1, waiting for transfers between devices, layer(): img_w = lax.all_gather(img_piece, 'col', axis=1, tiled=True)  67.2 us
    dot_general x4, matrix products, add_rows(): jnp.einsum('ti,sin->tsn', ready, piece, preferred_element_type=jnp.float32)  33.9 us
    dot_general x4, matrix products, attend(): jnp.einsum('qhe,khe->hqk', queries, key_rows, preferred_element_type=jnp....  31.7 us
    ppermute x2, waiting for transfers between devices, reduce_blocks(): lax.ppermute(jnp.concatenate([block(-1), far[cut:]], 0), axis_name, shift...  30.9 us
    ppermute x2, waiting for transfers between devices, ring_gather(): from_prev = lax.ppermute(piece, axis_name, shift_pairs(size, 1))  29.7 us
    ppermute x2, waiting for transfers between devices, ring_gather(): from_next = lax.ppermute(piece, axis_name, shift_pairs(size, -1))  16.3 us
    dot_general x4, matrix products, attend(): jnp.einsum('hqk,khe->qhe', chances, value_rows, preferred_element_type=jn...  15.9 us
    unnamed x98, local copies, waits for them, and re-layouts  14.1 us
  transfers between devices with their start and end apart: 27, of which 11 were waited for; matrix products, arithmetic and copies ran while one was open for 32% of the time, Pallas kernels for 0%

profile of v3, /device:TPU:1, one launch (start us, length us, event | category | flops | bytes accessed | tf_op | source)
XLA Modules:
  0.0 422.0 jit_solution(13157153309918550955)
XLA Ops:
  11.3 67.2 %all-gather.3.cloned.1.call-done = bf16[3,3072,384]{2,1,0:T(8,128)(2,1)} async-done(((bf16[3,192,384]{2,1,0:T(8,128)(2,1)}), bf16[3,3072,384]{2,1,0:T(8,128)(2,1)}) %all-gather.3.cloned.1.call-update) | async-done | bytes 7077904 | tf_op jit(solution)/shard_map/all_gather | solution.py:117
  82.2 16.3 %collective-permute-done = bf16[516,768]{1,0:T(8,128)(2,1)S(1)} collective-permute-done((bf16[516,768]{1,0:T(8,128)(2,1)S(1)}, bf16[516,768]{1,0:T(8,128)(2,1)S(1)}, u32[]{:S(2)}, u32[]{:S(2)}) %collective-permute-start) | collective-permute-done | bytes 792608 | tf_op jit(solution)/shard_map/ppermute | solution.py:23
  98.6 3.5 collective-permute-start.3
  105.7 3.5 collective-permute-done.3
  109.1 3.2 collective-permute-done.2
  116.5 29.7 %collective-permute-done.5 = bf16[1024,768]{1,0:T(8,128)(2,1)} collective-permute-done((bf16[1024,768]{1,0:T(8,128)(2,1)}, bf16[1024,768]{1,0:T(8,128)(2,1)}, u32[]{:S(2)}, u32[]{:S(2)}) %collective-permute-start.5) | collective-permute-done | bytes 1572896 | tf_op jit(solution)/shard_map/ppermute | solution.py:22
  153.1 10.3 %copy.41 = bf16[3,3072,384]{1,2,0:T(8,128)(2,1)} copy(bf16[3,3072,384]{2,1,0:T(8,128)(2,1)} %all-gather.3.cloned.1.call-done) | data formatting | bytes 14155776 | tf_op jit(solution)/shard_map/optimization_barrier | solution.py:121
  163.3 3.4 collective-permute-start.9
  171.3 3.5 pad_maximum_fusion
  178.0 4.8 %fusion.18 = (bf16[1024,768]{1,0:T(8,128)(2,1)}, bf16[1024,768]{1,0:T(8,128)(2,1)}, bf16[1024,768]{1,0:T(8,128)(2,1)}, bf16[1024,768]{1,0:T(8,128)(2,1)}) fusion(f32[768]{0:T(1024)S(1)} %get-tuple-element.87, f32[768]{0:T(1024)S(1)} %get-tuple-element.88, f32[1024]{0:T(1024)S(1)} %add_rsqrt_fusion.6, f32[1024]{0:T(1024)S(1)} %add_multiply_fusion, ...), kind=kLoop, calls=%fused_computation.39 | loop fusion | flops 18874368 | bytes 12615696 | tf_op jit(solution)/shard_map/convert_element_type | solution.py:60
  182.9 11.2 %fusion.45 = f32[1024,3,384]{0,2,1:T(8,128)} fusion(bf16[3,3072,384]{2,1,0:T(8,128)(2,1)S(1)} %bitcast.331, bf16[1024,768]{1,0:T(8,128)(2,1)} %get-tuple-element.45, bf16[1024,768]{1,0:T(8,128)(2,1)} %get-tuple-element.44, bf16[1024,768]{1,0:T(8,128)(2,1)} %get-tuple-element.43, bf16[1024,768]{1,0:T(8,128)(2,1)} %get-tuple-element.42), kind=kOutput, calls=%fused_computation.69 | convolution fusion | flops 7272923136 | bytes 18087936 | tf_op jit(solution)/shard_map/ti,sin->tsn/dot_general | solution.py:72
  194.0 3.4 fusion.155
  203.6 10.5 %copy.34 = bf16[3,3072,384]{1,2,0:T(8,128)(2,1)} copy(bf16[3,3072,384]{2,1,0:T(8,128)(2,1)} %all-gather.5.cloned.1.call-done) | data formatting | bytes 14155776 | tf_op jit(solution)/shard_map/all_gather | solution.py:122
  217.8 12.8 %fusion.44 = f32[1024,3,384]{0,2,1:T(8,128)S(1)} fusion(bf16[3,3072,384]{1,2,0:T(8,128)(2,1)} %collective-permute-done.9, bf16[1024,768]{1,0:T(8,128)(2,1)} %get-tuple-element.45, bf16[1024,768]{1,0:T(8,128)(2,1)} %get-tuple-element.44, bf16[1024,768]{1,0:T(8,128)(2,1)S(1)} %copy-done.14, bf16[1024,768]{1,0:T(8,128)(2,1)S(1)} %copy-done.13), kind=kOutput, calls=%fused_computation.68 | convolution fusion | flops 7272923136 | bytes 18087936 | tf_op jit(solution)/shard_map/ti,sin->tsn/dot_general | solution.py:72
  242.0 5.0 %fusion.6 = f32[512,2,384]{0,2,1:T(8,128)S(1)} fusion(bf16[3,3072,384]{1,2,0:T(8,128)(2,1)} %copy.34, bf16[512,768]{1,0:T(8,128)(2,1)S(1)} %copy-done.24, bf16[512,768]{1,0:T(8,128)(2,1)S(1)} %copy-done.22, bf16[512,768]{1,0:T(8,128)(2,1)S(1)} %copy-done.20, bf16[512,768]{1,0:T(8,128)(2,1)S(1)} %copy-done.18), kind=kOutput, calls=%fused_computation.18 | convolution fusion | flops 2428502016 | bytes 9437184 | tf_op jit(solution)/shard_map/ti,sin->tsn/dot_general | solution.py:72
  253.0 5.0 %fusion.106 = f32[3,512,1536]{2,1,0:T(8,128)} fusion(bf16[1024,3,128]{2,0,1:T(8,128)(2,1)S(1)} %copy-done.4, bf16[512,3,128]{2,0,1:T(8,128)(2,1)S(1)} %fusion.103, bf16[1024,3,128]{2,0,1:T(8,128)(2,1)S(1)} %copy-done.7), kind=kOutput, calls=%fused_computation.168 | convolution fusion | flops 606339072 | bytes 11010048 | tf_op jit(solution)/shard_map/qhe,khe->hqk/dot_general | solution.py:146
  258.1 5.0 %fusion.107 = f32[3,512,1536]{2,1,0:T(8,128)} fusion(bf16[1024,3,128]{2,0,1:T(8,128)(2,1)S(1)} %copy-done.4, bf16[512,3,128]{2,0,1:T(8,128)(2,1)S(1)} %fusion.103, bf16[1024,3,128]{2,0,1:T(8,128)(2,1)S(1)} %copy-done.7), kind=kOutput, calls=%fused_computation.169 | convolution fusion | flops 606339072 | bytes 11010048 | tf_op jit(solution)/shard_map/qhe,khe->hqk/dot_general | solution.py:146
  263.2 5.0 %fusion.4 = f32[512,2,384]{0,2,1:T(8,128)S(1)} fusion(bf16[3,3072,384]{1,2,0:T(8,128)(2,1)} %collective-permute-done.8, bf16[512,768]{1,0:T(8,128)(2,1)S(1)} %copy-done.25, bf16[512,768]{1,0:T(8,128)(2,1)S(1)} %copy-done.23, bf16[512,768]{1,0:T(8,128)(2,1)S(1)} %copy-done.21, bf16[512,768]{1,0:T(8,128)(2,1)S(1)} %copy-done.19), kind=kOutput, calls=%fused_computation.16 | convolution fusion | flops 2428502016 | bytes 9437184 | tf_op jit(solution)/shard_map/ti,sin->tsn/dot_general | solution.py:72
  269.1 3.3 slice.324
  272.4 4.4 %copy.59 = bf16[1,3072,384]{2,1,0:T(8,128)(2,1)} copy(bf16[1,3072,384]{1,2,0:T(8,128)(2,1)} %slice.324) | data formatting | bytes 4718592 | tf_op jit(solution)/shard_map/reshape;squeeze | solution.py:156
  279.6 5.0 %fusion.104 = f32[3,512,1536]{2,1,0:T(8,128)} fusion(bf16[1024,3,128]{2,0,1:T(8,128)(2,1)S(1)} %copy-done.9, bf16[512,3,128]{2,0,1:T(8,128)(2,1)S(1)} %fusion.101, bf16[1024,3,128]{2,0,1:T(8,128)(2,1)S(1)} %copy-done.10), kind=kOutput, calls=%fused_computation.166 | convolution fusion | flops 606339072 | bytes 11010048 | tf_op jit(solution)/shard_map/qhe,khe->hqk/dot_general | solution.py:146
  284.6 16.6 %fusion.1 = (f32[3,512]{1,0:T(4,128)S(1)}, f32[3,512]{1,0:T(4,128)S(1)}, f32[3,512]{1,0:T(4,128)S(1)}, f32[3,512]{1,0:T(4,128)S(1)}, f32[3,512,1536]{2,1,0:T(8,128)}) fusion(pred[1536]{0:T(1024)(128)(4,1)S(1)} %fusion.114, f32[3,512,1536]{2,1,0:T(8,128)} %fusion.106, f32[3,512,1536]{2,1,0:T(8,128)} %fusion.104, f32[3,512,1536]{2,1,0:T(8,128)} %fusion.107, ...), kind=kOutput, calls=%fused_computation.9 | convolution fusion | flops 634644480 | bytes 39348224 | tf_op jit(solution)/shard_map/qhe,khe->hqk/dot_general | solution.py:146
  301.3 5.3 %fusion.91 = bf16[3,128,512]{2,1,0:T(8,128)(2,1)S(1)} fusion(f32[3,512,1536]{2,1,0:T(8,128)} %fusion.107, f32[3,512]{1,0:T(4,128)S(1)} %get-tuple-element.41, pred[1536]{0:T(1024)(128)(4,1)S(1)} %fusion.114, bf16[1024,3,128]{0,2,1:T(8,128)(2,1)S(1)} %copy-done.27, bf16[512,3,128]{0,2,1:T(8,128)(2,1)S(1)} %copy-done.29), kind=kOutput, calls=%fused_computation.135 | convolution fusion | flops 615972864 | bytes 11017728 | tf_op jit(solution)/shard_map/hqk,khe->qhe/dot_general | solution.py:151
  311.1 5.3 %fusion.88 = bf16[3,128,512]{2,1,0:T(8,128)(2,1)S(1)} fusion(f32[3,512,1536]{2,1,0:T(8,128)} %fusion.104, f32[3,512]{1,0:T(4,128)S(1)} %get-tuple-element.40, pred[1536]{0:T(1024)(128)(4,1)S(1)} %fusion.114, bf16[1024,3,128]{0,2,1:T(8,128)(2,1)S(1)} %copy-done.26, bf16[512,3,128]{0,2,1:T(8,128)(2,1)S(1)} %fusion.109), kind=kOutput, calls=%fused_computation.132 | convolution fusion | flops 615972864 | bytes 11017728 | tf_op jit(solution)/shard_map/hqk,khe->qhe/dot_general | solution.py:151
  320.3 3.5 collective-permute-start.15
  335.9 13.2 %collective-permute-done.15 = bf16[768,768]{1,0:T(8,128)(2,1)S(1)} collective-permute-done((bf16[768,768]{1,0:T(8,128)(2,1)S(1)}, bf16[768,768]{1,0:T(8,128)(2,1)S(1)}, u32[]{:S(2)}, u32[]{:S(2)}) %collective-permute-start.15) | collective-permute-done | bytes 1179680 | tf_op jit(solution)/shard_map/ppermute | solution.py:41
  350.8 3.4 collective-permute-start.17
  356.8 17.7 %collective-permute-done.11 = bf16[768,768]{1,0:T(8,128)(2,1)} collective-permute-done((bf16[768,768]{1,0:T(8,128)(2,1)}, bf16[768,768]{1,0:T(8,128)(2,1)}, u32[]{:S(2)}, u32[]{:S(2)}) %collective-permute-start.11) | collective-permute-done | bytes 1179680 | tf_op jit(solution)/shard_map/ppermute | solution.py:41
  375.5 3.5 collective-permute-start.13
  382.9 3.5 collective-permute-done.16
  391.2 3.5 collective-permute-done.12
  410.3 3.9 fusion.41
  (221 shorter events, 108.1 us)
Async XLA Ops:
  7.2 71.3 %copy-start.33 = (bf16[1,1,2,768]{3,2,1,0:T(2,128)(2,1)S(1)}, bf16[1,1,2,768]{3,2,1,0:T(2,128)(2,1)}, u32[]{:S(2)}) copy-start(bf16[1,1,2,768]{3,2,1,0:T(2,128)(2,1)} %param.17) | copy-start | bytes 9220
  7.2 71.3 %copy-start.34 = (bf16[1,1,2,768]{3,2,1,0:T(2,128)(2,1)S(1)}, bf16[1,1,2,768]{3,2,1,0:T(2,128)(2,1)}, u32[]{:S(2)}) copy-start(bf16[1,1,2,768]{3,2,1,0:T(2,128)(2,1)} %param.16) | copy-start | bytes 9220
  7.2 71.3 %copy-start.28 = (bf16[1,1,512,768]{3,2,1,0:T(8,128)(2,1)S(1)}, bf16[1,1,512,768]{3,2,1,0:T(8,128)(2,1)}, u32[]{:S(2)}) copy-start(bf16[1,1,512,768]{3,2,1,0:T(8,128)(2,1)} %param.15) | copy-start | bytes 2359300
  7.2 71.3 %all-gather.3.cloned.1.call-start = ((), (), s32[]{:S(2)}) async-start(), calls=%async_computation | async-start | bytes 7520256 | tf_op jit(solution)/shard_map/all_gather | solution.py:117
  9.2 194.4 %all-gather.5.cloned.1.call-start = ((), (), s32[]{:S(2)}) async-start(), calls=%async_computation.1 | async-start | bytes 7520256 | tf_op jit(solution)/shard_map/all_gather | solution.py:122
  79.5 19.0 %collective-permute-start = (bf16[516,768]{1,0:T(8,128)(2,1)S(1)}, bf16[516,768]{1,0:T(8,128)(2,1)S(1)}, u32[]{:S(2)}, u32[]{:S(2)}) collective-permute-start(bf16[516,768]{1,0:T(8,128)(2,1)S(1)} %get-tuple-element.69), channel_id=1, source_target_pairs={{0,48},{16,0},{32,16},{48,32},{1,49},{17,1},{33,17},{49,33},{2,50}... | collective-permute-start | bytes 2377736 | tf_op jit(solution)/shard_map/ppermute | solution.py:23
  82.2 19.9 %collective-permute-start.1 = (bf16[516,768]{1,0:T(8,128)(2,1)S(1)}, bf16[516,768]{1,0:T(8,128)(2,1)S(1)}, u32[]{:S(2)}, u32[]{:S(2)}) collective-permute-start(bf16[516,768]{1,0:T(8,128)(2,1)S(1)} %get-tuple-element.69), channel_id=1, source_target_pairs={{0,16},{16,32},{32,48},{48,0},{1,17},{17,33},{33,49},{49,1},{2,18}... | collective-permute-start | bytes 2377736 | tf_op jit(solution)/shard_map/ppermute | solution.py:22
  98.6 10.5 %collective-permute-start.3 = (bf16[258,768]{1,0:T(8,128)(2,1)S(1)}, bf16[258,768]{1,0:T(8,128)(2,1)S(1)}, u32[]{:S(2)}, u32[]{:S(2)}) collective-permute-start(bf16[258,768]{1,0:T(8,128)(2,1)S(1)} %slice.298), channel_id=1, source_target_pairs={{0,48},{16,0},{32,16},{48,32},{1,49},{17,1},{33,17},{49,33},{2,50}... | collective-permute-start | bytes 1188872 | tf_op jit(solution)/shard_map/ppermute | solution.py:26
  102.1 10.2 %collective-permute-start.2 = (bf16[258,768]{1,0:T(8,128)(2,1)S(1)}, bf16[258,768]{1,0:T(8,128)(2,1)S(1)}, u32[]{:S(2)}, u32[]{:S(2)}) collective-permute-start(bf16[258,768]{1,0:T(8,128)(2,1)S(1)} %slice.297), channel_id=1, source_target_pairs={{0,16},{16,32},{32,48},{48,0},{1,17},{17,33},{33,49},{49,1},{2,18}... | collective-permute-start | bytes 1188872 | tf_op jit(solution)/shard_map/ppermute | solution.py:25
  102.2 44.0 %collective-permute-start.5 = (bf16[1024,768]{1,0:T(8,128)(2,1)}, bf16[1024,768]{1,0:T(8,128)(2,1)}, u32[]{:S(2)}, u32[]{:S(2)}) collective-permute-start(bf16[1024,768]{1,0:T(8,128)(2,1)} %bitcast.20), channel_id=1, source_target_pairs={{0,16},{16,32},{32,48},{48,0},{1,17},{17,33},{33,49},{49,1},{2,18}... | collective-permute-start | bytes 4718600 | tf_op jit(solution)/shard_map/ppermute | solution.py:22
  102.3 46.0 %collective-permute-start.4 = (bf16[1024,768]{1,0:T(8,128)(2,1)}, bf16[1024,768]{1,0:T(8,128)(2,1)}, u32[]{:S(2)}, u32[]{:S(2)}) collective-permute-start(bf16[1024,768]{1,0:T(8,128)(2,1)} %bitcast.20), channel_id=1, source_target_pairs={{0,48},{16,0},{32,16},{48,32},{1,49},{17,1},{33,17},{49,33},{2,50}... | collective-permute-start | bytes 4718600 | tf_op jit(solution)/shard_map/ppermute | solution.py:23
  148.3 21.5 %collective-permute-start.6 = (bf16[512,768]{1,0:T(8,128)(2,1)}, bf16[512,768]{1,0:T(8,128)(2,1)}, u32[]{:S(2)}, u32[]{:S(2)}) collective-permute-start(bf16[512,768]{1,0:T(8,128)(2,1)} %slice.309), channel_id=1, source_target_pairs={{0,16},{16,32},{32,48},{48,0},{1,17},{17,33},{33,49},{49,1},{2,18}... | collective-permute-start | bytes 2359304 | tf_op jit(solution)/shard_map/ppermute | solution.py:25
  150.3 19.4 %collective-permute-start.7 = (bf16[512,768]{1,0:T(8,128)(2,1)}, bf16[512,768]{1,0:T(8,128)(2,1)}, u32[]{:S(2)}, u32[]{:S(2)}) collective-permute-start(bf16[512,768]{1,0:T(8,128)(2,1)} %slice.310), channel_id=1, source_target_pairs={{0,48},{16,0},{32,16},{48,32},{1,49},{17,1},{33,17},{49,33},{2,50}... | collective-permute-start | bytes 2359304 | tf_op jit(solution)/shard_map/ppermute | solution.py:26
  163.3 54.5 %collective-permute-start.9 = (bf16[3,3072,384]{1,2,0:T(8,128)(2,1)}, bf16[3,3072,384]{1,2,0:T(8,128)(2,1)}, u32[]{:S(2)}, u32[]{:S(2)}) collective-permute-start(bf16[3,3072,384]{1,2,0:T(8,128)(2,1)} %copy.41), channel_id=1, source_target_pairs={{0,64},{64,0},{1,65},{65,1},{2,66},{66,2},{3,67},{67,3},{4,68},{68... | collective-permute-start | bytes 21233672 | tf_op jit(solution)/shard_map/ppermute | solution.py:125
  214.1 49.0 %collective-permute-start.8 = (bf16[3,3072,384]{1,2,0:T(8,128)(2,1)}, bf16[3,3072,384]{1,2,0:T(8,128)(2,1)}, u32[]{:S(2)}, u32[]{:S(2)}) collective-permute-start(bf16[3,3072,384]{1,2,0:T(8,128)(2,1)} %copy.34), channel_id=1, source_target_pairs={{0,64},{64,0},{1,65},{65,1},{2,66},{66,2},{3,67},{67,3},{4,68},{68... | collective-permute-start | bytes 21233672 | tf_op jit(solution)/shard_map/ppermute | solution.py:126
  284.6 22.0 %slice-start.1 = ((s8[9437184]{0:T(1024)(128)(4,1)}), s8[4194304]{0:T(1024)(128)(4,1)S(1)}, s32[]{:S(2)}) async-start(s8[9437184]{0:T(1024)(128)(4,1)} %bitcast.328), calls=%async_computation.3 | async-start | bytes 8388608
  320.3 28.8 %collective-permute-start.15 = (bf16[768,768]{1,0:T(8,128)(2,1)S(1)}, bf16[768,768]{1,0:T(8,128)(2,1)S(1)}, u32[]{:S(2)}, u32[]{:S(2)}) collective-permute-start(bf16[768,768]{1,0:T(8,128)(2,1)S(1)} %pad_maximum_fusion.9), channel_id=1, source_target_pairs={{0,48},{16,0},{32,16},{48,32},{1,49},{17,1},{33,17},{49,33},{2,50}... | collective-permute-start | bytes 3538952 | tf_op jit(solution)/shard_map/ppermute | solution.py:41
  323.8 30.4 %collective-permute-start.14 = (bf16[768,768]{1,0:T(8,128)(2,1)S(1)}, bf16[768,768]{1,0:T(8,128)(2,1)S(1)}, u32[]{:S(2)}, u32[]{:S(2)}) collective-permute-start(bf16[768,768]{1,0:T(8,128)(2,1)S(1)} %pad_maximum_fusion.8), channel_id=1, source_target_pairs={{0,16},{16,32},{32,48},{48,0},{1,17},{17,33},{33,49},{49,1},{2,18}... | collective-permute-start | bytes 3538952 | tf_op jit(solution)/shard_map/ppermute | solution.py:40
  332.0 42.4 %collective-permute-start.11 = (bf16[768,768]{1,0:T(8,128)(2,1)}, bf16[768,768]{1,0:T(8,128)(2,1)}, u32[]{:S(2)}, u32[]{:S(2)}) collective-permute-start(bf16[768,768]{1,0:T(8,128)(2,1)} %pad_maximum_fusion.7), channel_id=1, source_target_pairs={{0,48},{16,0},{32,16},{48,32},{1,49},{17,1},{33,17},{49,33},{2,50}... | collective-permute-start | bytes 3538952 | tf_op jit(solution)/shard_map/ppermute | solution.py:41
  334.7 45.4 %copy-start.32 = (bf16[1,1,768]{2,1,0:T(2,128)(2,1)S(1)}, bf16[1,1,768]{2,1,0:T(2,128)(2,1)}, u32[]{:S(2)}) copy-start(bf16[1,1,768]{2,1,0:T(2,128)(2,1)} %param.18) | copy-start | bytes 4612
  335.9 43.1 %collective-permute-start.10 = (bf16[768,768]{1,0:T(8,128)(2,1)}, bf16[768,768]{1,0:T(8,128)(2,1)}, u32[]{:S(2)}, u32[]{:S(2)}) collective-permute-start(bf16[768,768]{1,0:T(8,128)(2,1)} %pad_maximum_fusion.6), channel_id=1, source_target_pairs={{0,16},{16,32},{32,48},{48,0},{1,17},{17,33},{33,49},{49,1},{2,18}... | collective-permute-start | bytes 3538952 | tf_op jit(solution)/shard_map/ppermute | solution.py:40
  350.8 32.0 %collective-permute-start.17 = (bf16[256,768]{1,0:T(8,128)(2,1)}, bf16[256,768]{1,0:T(8,128)(2,1)S(1)}, u32[]{:S(2)}, u32[]{:S(2)}) collective-permute-start(bf16[256,768]{1,0:T(8,128)(2,1)} %slice.345), channel_id=1, source_target_pairs={{0,48},{16,0},{32,16},{48,32},{1,49},{17,1},{33,17},{49,33},{2,50}... | collective-permute-start | bytes 1179656 | tf_op jit(solution)/shard_map/ppermute | solution.py:45
  356.1 30.3 %collective-permute-start.16 = (bf16[256,768]{1,0:T(8,128)(2,1)}, bf16[256,768]{1,0:T(8,128)(2,1)}, u32[]{:S(2)}, u32[]{:S(2)}) collective-permute-start(bf16[256,768]{1,0:T(8,128)(2,1)} %slice.344), channel_id=1, source_target_pairs={{0,16},{16,32},{32,48},{48,0},{1,17},{17,33},{33,49},{49,1},{2,18}... | collective-permute-start | bytes 1179656 | tf_op jit(solution)/shard_map/ppermute | solution.py:44
  375.5 15.7 %collective-permute-start.13 = (bf16[256,768]{1,0:T(8,128)(2,1)S(1)}, bf16[256,768]{1,0:T(8,128)(2,1)S(1)}, u32[]{:S(2)}, u32[]{:S(2)}) collective-permute-start(bf16[256,768]{1,0:T(8,128)(2,1)S(1)} %slice.337), channel_id=1, source_target_pairs={{0,48},{16,0},{32,16},{48,32},{1,49},{17,1},{33,17},{49,33},{2,50}... | collective-permute-start | bytes 1179656 | tf_op jit(solution)/shard_map/ppermute | solution.py:45
  380.0 14.7 %collective-permute-start.12 = (bf16[256,768]{1,0:T(8,128)(2,1)S(1)}, bf16[256,768]{1,0:T(8,128)(2,1)S(1)}, u32[]{:S(2)}, u32[]{:S(2)}) collective-permute-start(bf16[256,768]{1,0:T(8,128)(2,1)S(1)} %slice.336), channel_id=1, source_target_pairs={{0,16},{16,32},{32,48},{48,0},{1,17},{17,33},{33,49},{49,1},{2,18}... | collective-permute-start | bytes 1179656 | tf_op jit(solution)/shard_map/ppermute | solution.py:44
  399.4 7.4 %collective-permute-start.24 = (f32[128,64]{0,1:T(8,128)S(1)}, f32[128,64]{0,1:T(8,128)S(1)}, u32[]{:S(2)}, u32[]{:S(2)}) collective-permute-start(f32[128,64]{0,1:T(8,128)S(1)} %bitcast.358), channel_id=1, source_target_pairs={{0,112},{16,0},{32,16},{48,32},{64,48},{80,64},{96,80},{112,96},{1... | collective-permute-start | bytes 98312 | tf_op jit(solution)/shard_map/ppermute | solution.py:185
  400.2 8.2 %collective-permute-start.18 = (f32[128,64]{0,1:T(8,128)S(1)}, f32[128,64]{0,1:T(8,128)S(1)}, u32[]{:S(2)}, u32[]{:S(2)}) collective-permute-start(f32[128,64]{0,1:T(8,128)S(1)} %bitcast.357), channel_id=1, source_target_pairs={{0,16},{16,32},{32,48},{48,64},{64,80},{80,96},{96,112},{112,0},{1... | collective-permute-start | bytes 98312 | tf_op jit(solution)/shard_map/ppermute | solution.py:185
  403.5 10.7 %collective-permute-start.23 = (f32[128,64]{0,1:T(8,128)S(1)}, f32[128,64]{0,1:T(8,128)S(1)}, u32[]{:S(2)}, u32[]{:S(2)}) collective-permute-start(f32[128,64]{0,1:T(8,128)S(1)} %bitcast.356), channel_id=1, source_target_pairs={{0,96},{16,112},{32,0},{48,16},{64,32},{80,48},{96,64},{112,80},{1... | collective-permute-start | bytes 98312 | tf_op jit(solution)/shard_map/ppermute | solution.py:185
  404.4 9.9 %collective-permute-start.22 = (f32[128,64]{0,1:T(8,128)S(1)}, f32[128,64]{0,1:T(8,128)S(1)}, u32[]{:S(2)}, u32[]{:S(2)}) collective-permute-start(f32[128,64]{0,1:T(8,128)S(1)} %bitcast.355), channel_id=1, source_target_pairs={{0,80},{16,96},{32,112},{48,0},{64,16},{80,32},{96,48},{112,64},{1... | collective-permute-start | bytes 98312 | tf_op jit(solution)/shard_map/ppermute | solution.py:185
  406.8 7.5 %collective-permute-start.21 = (f32[128,64]{0,1:T(8,128)S(1)}, f32[128,64]{0,1:T(8,128)S(1)}, u32[]{:S(2)}, u32[]{:S(2)}) collective-permute-start(f32[128,64]{0,1:T(8,128)S(1)} %bitcast.354), channel_id=1, source_target_pairs={{0,64},{16,80},{32,96},{48,112},{64,0},{80,16},{96,32},{112,48},{1... | collective-permute-start | bytes 98312 | tf_op jit(solution)/shard_map/ppermute | solution.py:185
  406.8 7.5 %collective-permute-start.20 = (f32[128,64]{0,1:T(8,128)S(1)}, f32[128,64]{0,1:T(8,128)S(1)}, u32[]{:S(2)}, u32[]{:S(2)}) collective-permute-start(f32[128,64]{0,1:T(8,128)S(1)} %bitcast.353), channel_id=1, source_target_pairs={{0,48},{16,64},{32,80},{48,96},{64,112},{80,0},{96,16},{112,32},{1... | collective-permute-start | bytes 98312 | tf_op jit(solution)/shard_map/ppermute | solution.py:185
  408.4 5.9 %collective-permute-start.19 = (f32[128,64]{0,1:T(8,128)S(1)}, f32[128,64]{0,1:T(8,128)S(1)}, u32[]{:S(2)}, u32[]{:S(2)}) collective-permute-start(f32[128,64]{0,1:T(8,128)S(1)} %bitcast.352), channel_id=1, source_target_pairs={{0,32},{16,48},{32,64},{48,80},{64,96},{80,112},{96,0},{112,16},{1... | collective-permute-start | bytes 98312 | tf_op jit(solution)/shard_map/ppermute | solution.py:185
  (40 other events, 237.7 us)
Sparse Core Ops, SparseCore 0:
  10.7 67.7 all-gather.2
  80.6 64.3 all-gather.4

commit v4 on v3

--- a/solution.py
+++ b/solution.py
@@ -37,7 +37,9 @@
         return lax.dynamic_index_in_dim(term_blocks, (me + offset) % size, 0, keepdims=False)
 
     far = block(2)
-    up = lax.ppermute(jnp.concatenate([block(1), far[:cut]], 0), axis_name, shift_pairs(size, 1))
+    up = lax.ppermute(
+        jnp.concatenate([block(1), far[:cut]], 0), axis_name, shift_pairs(size, 1)
+    )
     down = lax.ppermute(
         jnp.concatenate([block(-1), far[cut:]], 0), axis_name, shift_pairs(size, -1)
     )
@@ -123,10 +125,9 @@
     txt_w = txt_out_w[:2]
     out_w = txt_out_w[2]
     img_w_other = lax.ppermute(img_w, "cfg", swap)
-    txt_out_other = lax.ppermute(txt_out_w, "cfg", swap)
     halves = [
         (txt_w, img_w, out_w),
-        (txt_out_other[:2], img_w_other, txt_out_other[2]),
+        (lax.ppermute(txt_w, "cfg", swap), img_w_other, lax.ppermute(out_w, "cfg", swap)),
     ]
     positions = jnp.arange(text_slots + images, dtype=jnp.int32)
     usable = (positions < txt_len[0, 0]) | (positions >= text_slots)
@@ -158,7 +159,7 @@
         )
 
     projections = [project(*h[:2]) for h in halves]
-    n_chunk = 2
+    n_chunk = 4
     chunk = images // n_chunk
     pieces = []
     for c in range(n_chunk):

time: 430 us -> 430 us (level)
  waiting for transfers between devices: 163 us -> 112 us
  matrix products: 91.9 us -> 132 us
  starting transfers between devices: 38.1 us -> 52 us
  local copies, waits for them, and re-layouts: 68.6 us -> 63.9 us
    dot_general x4 -> x8, matrix products: 15.9 us -> 44.4 us  [attend(): jnp.einsum('hqk,khe->qhe', chances, value_rows, preferred_element_type=jn...]
    ppermute x2 -> x4, waiting for transfers between devices: 30.9 us -> 8.58 us  [reduce_blocks(): lax.ppermute(jnp.concatenate([block(-1), far[cut:]], 0), axis_name, shift...]
    ppermute x2, waiting for transfers between devices: 16.3 us -> 0.01 us  [ring_gather(): from_next = lax.ppermute(piece, axis_name, shift_pairs(size, -1))]
    dot_general x4 -> x8, matrix products: 7.71 us -> 22.5 us  [attend(): jnp.einsum('ti,koi->kto', outputs, out_w.reshape(n_row, local_width, half...]
    all_gather x1 -> x0, local copies, waits for them, and re-layouts: 10.5 us -> none  [layer(): txt_out_w = lax.all_gather(txt_out_piece, 'col', axis=1, tiled=True)]
    unnamed x98 -> x110, local copies, waits for them, and re-layouts: 14.1 us -> 23 us
    ppermute x2 -> x4, waiting for transfers between devices: 6.99 us -> 0.01 us  [reduce_blocks(): far_top = lax.ppermute(up[rows:], axis_name, shift_pairs(size, 1))]
    all_gather x1, waiting for transfers between devices: 67.2 us -> 60.8 us  [layer(): img_w = lax.all_gather(img_piece, 'col', axis=1, tiled=True)]
  transfers between devices with their start and end apart: 27 -> 36, of which waited for: 11 -> 9; matrix products, arithmetic and copies ran while one was open for 32% -> 51% of each run, Pallas kernels for 0% -> 0%
where the time goes in v4:
time: 430 us; the launch traced here: 423 us
  matrix products  132 us (31%)
  waiting for transfers between devices  112 us (26%)
  local copies, waits for them, and re-layouts  63.9 us (15%)
  starting transfers between devices  52 us (12%)
  other arithmetic  45.4 us (11%)
  between operations  18.5 us (4%)
    all_gather x1, waiting for transfers between devices, layer(): img_w = lax.all_gather(img_piece, 'col', axis=1, tiled=True)  60.8 us
    dot_general x8, matrix products, attend(): jnp.einsum('hqk,khe->qhe', chances, value_rows, preferred_element_type=jn...  44.4 us
    dot_general x4, matrix products, add_rows(): jnp.einsum('ti,sin->tsn', ready, piece, preferred_element_type=jnp.float32)  32.1 us
    dot_general x8, matrix products, attend(): jnp.einsum('qhe,khe->hqk', queries, key_rows, preferred_element_type=jnp....  30.8 us
    ppermute x2, waiting for transfers between devices, ring_gather(): from_prev = lax.ppermute(piece, axis_name, shift_pairs(size, 1))  29.1 us
    unnamed x110, local copies, waits for them, and re-layouts  23 us
    dot_general x8, matrix products, attend(): jnp.einsum('ti,koi->kto', outputs, out_w.reshape(n_row, local_width, half...  22.5 us
    ppermute x7, starting transfers between devices, layer(): lax.ppermute(outgoing, ('cfg', 'row'), shift_pairs(n_pair, step))  12.2 us
  transfers between devices with their start and end apart: 36, of which 9 were waited for; matrix products, arithmetic and copies ran while one was open for 51% of the time, Pallas kernels for 0%

profile of v4, /device:TPU:1, one launch (start us, length us, event | category | flops | bytes accessed | tf_op | source)
XLA Modules:
  0.0 423.3 jit_solution(2949059829314515513)
XLA Ops:
  17.1 60.8 %all-gather.3.cloned.1.call-done = bf16[3,3072,384]{2,1,0:T(8,128)(2,1)} async-done(((bf16[3,192,384]{2,1,0:T(8,128)(2,1)}), bf16[3,3072,384]{2,1,0:T(8,128)(2,1)}) %all-gather.3.cloned.1.call-update) | async-done | bytes 7077904 | tf_op jit(solution)/shard_map/all_gather | solution.py:119
  85.2 4.2 collective-permute-done.2
  94.0 29.1 %collective-permute-done.5 = bf16[1024,768]{1,0:T(8,128)(2,1)} collective-permute-done((bf16[1024,768]{1,0:T(8,128)(2,1)}, bf16[1024,768]{1,0:T(8,128)(2,1)}, u32[]{:S(2)}, u32[]{:S(2)}) %collective-permute-start.5) | collective-permute-done | bytes 1572896 | tf_op jit(solution)/shard_map/ppermute | solution.py:22
  130.0 10.3 %copy.48 = bf16[3,3072,384]{1,2,0:T(8,128)(2,1)} copy(bf16[3,3072,384]{2,1,0:T(8,128)(2,1)} %all-gather.3.cloned.1.call-done) | data formatting | bytes 14155776 | tf_op jit(solution)/shard_map/optimization_barrier | solution.py:123
  147.7 3.4 pad_maximum_fusion
  154.3 4.9 %fusion.6 = (bf16[1024,768]{1,0:T(8,128)(2,1)}, bf16[1024,768]{1,0:T(8,128)(2,1)}, bf16[1024,768]{1,0:T(8,128)(2,1)}, bf16[1024,768]{1,0:T(8,128)(2,1)}) fusion(f32[768]{0:T(1024)S(1)} %get-tuple-element.94, f32[768]{0:T(1024)S(1)} %get-tuple-element.95, f32[1024]{0:T(1024)S(1)} %add_rsqrt_fusion.6, f32[1024]{0:T(1024)S(1)} %add_multiply_fusion, ...), kind=kLoop, calls=%fused_computation.33 | loop fusion | flops 18874368 | bytes 12615696 | tf_op jit(solution)/shard_map/convert_element_type | solution.py:62
  159.2 11.3 %fusion.33 = f32[1024,3,384]{0,2,1:T(8,128)} fusion(bf16[3,3072,384]{2,1,0:T(8,128)(2,1)S(1)} %bitcast.414, bf16[1024,768]{1,0:T(8,128)(2,1)} %get-tuple-element.43, bf16[1024,768]{1,0:T(8,128)(2,1)} %get-tuple-element.42, bf16[1024,768]{1,0:T(8,128)(2,1)} %get-tuple-element.41, bf16[1024,768]{1,0:T(8,128)(2,1)} %get-tuple-element.40), kind=kOutput, calls=%fused_computation.67 | convolution fusion | flops 7272923136 | bytes 18087936 | tf_op jit(solution)/shard_map/ti,sin->tsn/dot_general | solution.py:74
  170.5 3.4 fusion.162
  182.6 10.6 %fusion.32 = f32[1024,3,384]{0,2,1:T(8,128)S(1)} fusion(bf16[3,3072,384]{1,2,0:T(8,128)(2,1)} %collective-permute-done.10, bf16[1024,768]{1,0:T(8,128)(2,1)S(1)} %copy-done.17, bf16[1024,768]{1,0:T(8,128)(2,1)S(1)} %copy-done.16, bf16[1024,768]{1,0:T(8,128)(2,1)S(1)} %copy-done.15, bf16[1024,768]{1,0:T(8,128)(2,1)S(1)} %copy-done.14), kind=kOutput, calls=%fused_computation.66 | convolution fusion | flops 7272923136 | bytes 18087936 | tf_op jit(solution)/shard_map/ti,sin->tsn/dot_general | solution.py:74
  204.4 5.0 %slice.379 = bf16[2,3072,384]{2,1,0:T(8,128)(2,1)} slice(bf16[3,3072,384]{2,1,0:T(8,128)(2,1)} %all-gather.5.cloned.1.call-done), slice={[0:2], [0:3072], [0:384]} | slice | bytes 9437184
  209.4 6.8 %copy.77 = bf16[2,3072,384]{1,2,0:T(8,128)(2,1)} copy(bf16[2,3072,384]{2,1,0:T(8,128)(2,1)} %slice.379) | data formatting | bytes 9437184
  218.1 5.0 %fusion.89 = f32[512,2,384]{0,2,1:T(8,128)S(1)} fusion(bf16[512,768]{1,0:T(8,128)(2,1)S(1)} %copy-done.25, bf16[512,768]{1,0:T(8,128)(2,1)S(1)} %copy-done.23, bf16[512,768]{1,0:T(8,128)(2,1)S(1)} %copy-done.21, bf16[512,768]{1,0:T(8,128)(2,1)S(1)} %copy-done.19, bf16[3,3072,384]{2,1,0:T(8,128)(2,1)} %all-gather.5.cloned.1.call-done), kind=kOutput, calls=%fused_computation.141 | convolution fusion | flops 2428502016 | bytes 9437184 | tf_op jit(solution)/shard_map/ti,sin->tsn/dot_general | solution.py:74
  223.1 4.0 slice_bitcast_fusion.8
  232.5 4.1 exponential_select_fusion.7
  236.6 5.5 %fusion.97 = bf16[3,128,256]{2,1,0:T(8,128)(2,1)} fusion(f32[3,256,1536]{2,1,0:T(8,128)} %exponential_select_fusion.7, bf16[1024,3,128]{0,2,1:T(8,128)(2,1)S(1)} %copy-done.28, bf16[512,3,128]{0,2,1:T(8,128)(2,1)S(1)} %fusion.118), kind=kOutput, calls=%fused_computation.153 | convolution fusion | flops 306809088 | bytes 6094848 | tf_op jit(solution)/shard_map/hqk,khe->qhe/dot_general | solution.py:152
  242.1 4.5 %exponential_select_fusion.5 = f32[3,256,1536]{2,1,0:T(8,128)} fusion(pred[1536]{0:T(1024)(128)(4,1)S(1)} %fusion.128, bf16[1024,3,128]{2,0,1:T(8,128)(2,1)} %fusion.85, bf16[1024,3,128]{2,0,1:T(8,128)(2,1)} %fusion.83, bf16[512,3,128]{2,0,1:T(8,128)(2,1)} %copy-done.38), kind=kOutput, calls=%fused_computation.13 | convolution fusion | flops 306708480 | bytes 6096384 | tf_op jit(solution)/shard_map/qhe,khe->hqk/dot_general | solution.py:147
  246.6 5.5 %fusion.95 = bf16[3,128,256]{2,1,0:T(8,128)(2,1)} fusion(f32[3,256,1536]{2,1,0:T(8,128)} %exponential_select_fusion.5, bf16[1024,3,128]{0,2,1:T(8,128)(2,1)S(1)} %copy-done.28, bf16[512,3,128]{0,2,1:T(8,128)(2,1)S(1)} %fusion.118), kind=kOutput, calls=%fused_computation.151 | convolution fusion | flops 306809088 | bytes 6094848 | tf_op jit(solution)/shard_map/hqk,khe->qhe/dot_general | solution.py:152
  252.1 4.5 %exponential_select_fusion.3 = f32[3,256,1536]{2,1,0:T(8,128)} fusion(pred[1536]{0:T(1024)(128)(4,1)S(1)} %fusion.128, bf16[1024,3,128]{2,0,1:T(8,128)(2,1)} %fusion.85, bf16[1024,3,128]{2,0,1:T(8,128)(2,1)} %fusion.83, bf16[512,3,128]{2,0,1:T(8,128)(2,1)} %copy-done.38), kind=kOutput, calls=%fused_computation.9 | convolution fusion | flops 306708480 | bytes 6096384 | tf_op jit(solution)/shard_map/qhe,khe->hqk/dot_general | solution.py:147
  256.5 5.5 %fusion.93 = bf16[3,128,256]{2,1,0:T(8,128)(2,1)} fusion(f32[3,256,1536]{2,1,0:T(8,128)} %exponential_select_fusion.3, bf16[1024,3,128]{0,2,1:T(8,128)(2,1)S(1)} %copy-done.28, bf16[512,3,128]{0,2,1:T(8,128)(2,1)S(1)} %fusion.118), kind=kOutput, calls=%fused_computation.149 | convolution fusion | flops 306809088 | bytes 6094848 | tf_op jit(solution)/shard_map/hqk,khe->qhe/dot_general | solution.py:152
  262.0 4.5 %exponential_select_fusion.1 = f32[3,256,1536]{2,1,0:T(8,128)} fusion(pred[1536]{0:T(1024)(128)(4,1)S(1)} %fusion.128, bf16[1024,3,128]{2,0,1:T(8,128)(2,1)} %fusion.85, bf16[1024,3,128]{2,0,1:T(8,128)(2,1)} %fusion.83, bf16[512,3,128]{2,0,1:T(8,128)(2,1)} %copy-done.38), kind=kOutput, calls=%fused_computation.5 | convolution fusion | flops 306708480 | bytes 6096384 | tf_op jit(solution)/shard_map/qhe,khe->hqk/dot_general | solution.py:147
  266.5 5.5 %fusion.91 = bf16[3,128,256]{2,1,0:T(8,128)(2,1)} fusion(f32[3,256,1536]{2,1,0:T(8,128)} %exponential_select_fusion.1, bf16[1024,3,128]{0,2,1:T(8,128)(2,1)S(1)} %copy-done.28, bf16[512,3,128]{0,2,1:T(8,128)(2,1)S(1)} %fusion.118), kind=kOutput, calls=%fused_computation.147 | convolution fusion | flops 306809088 | bytes 6094848 | tf_op jit(solution)/shard_map/hqk,khe->qhe/dot_general | solution.py:152
  272.0 3.6 fusion.164
  283.8 5.2 %fusion.88 = f32[512,2,384]{0,2,1:T(8,128)S(1)} fusion(bf16[2,3072,384]{1,2,0:T(8,128)(2,1)} %collective-permute-done.9, bf16[512,768]{1,0:T(8,128)(2,1)S(1)} %copy-done.26, bf16[512,768]{1,0:T(8,128)(2,1)S(1)} %copy-done.24, bf16[512,768]{1,0:T(8,128)(2,1)S(1)} %copy-done.22, bf16[512,768]{1,0:T(8,128)(2,1)S(1)} %copy-done.20), kind=kOutput, calls=%fused_computation.140 | convolution fusion | flops 2428502016 | bytes 9437184 | tf_op jit(solution)/shard_map/ti,sin->tsn/dot_general | solution.py:74
  290.4 4.0 exponential_select_fusion.6
  294.4 4.9 %fusion.96 = bf16[3,128,256]{2,1,0:T(8,128)(2,1)S(1)} fusion(f32[3,256,1536]{2,1,0:T(8,128)} %exponential_select_fusion.6, bf16[1024,3,128]{0,2,1:T(8,128)(2,1)S(1)} %copy-done.27, bf16[512,3,128]{0,2,1:T(8,128)(2,1)S(1)} %fusion.119), kind=kOutput, calls=%fused_computation.152 | convolution fusion | flops 306809088 | bytes 6094848 | tf_op jit(solution)/shard_map/hqk,khe->qhe/dot_general | solution.py:152
  316.7 5.8 %fusion.94 = bf16[3,128,256]{2,1,0:T(8,128)(2,1)} fusion(f32[3,256,1536]{2,1,0:T(8,128)} %exponential_select_fusion.4, bf16[1024,3,128]{0,2,1:T(8,128)(2,1)} %fusion.105, bf16[512,3,128]{0,2,1:T(8,128)(2,1)S(1)} %fusion.119), kind=kOutput, calls=%fused_computation.150 | convolution fusion | flops 306809088 | bytes 6094848 | tf_op jit(solution)/shard_map/hqk,khe->qhe/dot_general | solution.py:152
  330.0 5.7 %fusion.92 = bf16[3,128,256]{2,1,0:T(8,128)(2,1)} fusion(f32[3,256,1536]{2,1,0:T(8,128)} %exponential_select_fusion.2, bf16[1024,3,128]{0,2,1:T(8,128)(2,1)} %fusion.105, bf16[512,3,128]{0,2,1:T(8,128)(2,1)S(1)} %fusion.119), kind=kOutput, calls=%fused_computation.148 | convolution fusion | flops 306809088 | bytes 6094848 | tf_op jit(solution)/shard_map/hqk,khe->qhe/dot_general | solution.py:152
  340.6 6.0 %fusion.90 = bf16[3,128,256]{2,1,0:T(8,128)(2,1)} fusion(f32[3,256,1536]{2,1,0:T(8,128)} %exponential_select_fusion, bf16[1024,3,128]{0,2,1:T(8,128)(2,1)} %fusion.105, bf16[512,3,128]{0,2,1:T(8,128)(2,1)} %copy-done.37), kind=kOutput, calls=%fused_computation.146 | convolution fusion | flops 306809088 | bytes 6094848 | tf_op jit(solution)/shard_map/hqk,khe->qhe/dot_general | solution.py:152
  368.3 8.6 %collective-permute-done.24 = bf16[384,768]{1,0:T(8,128)(2,1)S(1)} collective-permute-done((bf16[384,768]{1,0:T(8,128)(2,1)S(1)}, bf16[384,768]{1,0:T(8,128)(2,1)S(1)}, u32[]{:S(2)}, u32[]{:S(2)}) %collective-permute-start.24) | collective-permute-done | bytes 589856 | tf_op jit(solution)/shard_map/ppermute | solution.py:43
  376.9 3.5 collective-permute-start.22
  382.8 3.5 collective-permute-start.26
  397.6 4.6 %collective-permute-start.28 = (f32[128,64]{0,1:T(8,128)S(1)}, f32[128,64]{0,1:T(8,128)S(1)}, u32[]{:S(2)}, u32[]{:S(2)}) collective-permute-start(f32[128,64]{0,1:T(8,128)S(1)} %bitcast.446), channel_id=1, source_target_pairs={{0,32},{16,48},{32,64},{48,80},{64,96},{80,112},{96,0},{112,16},{1... | collective-permute-start | bytes 98312 | tf_op jit(solution)/shard_map/ppermute | solution.py:186
  (272 shorter events, 151.2 us)
Async XLA Ops:
  7.2 70.7 %all-gather.3.cloned.1.call-start = ((), (), s32[]{:S(2)}) async-start(), calls=%async_computation | async-start | bytes 7520256 | tf_op jit(solution)/shard_map/all_gather | solution.py:119
  9.2 195.2 %all-gather.5.cloned.1.call-start = ((), (), s32[]{:S(2)}) async-start(), calls=%async_computation.1 | async-start | bytes 7520256 | tf_op jit(solution)/shard_map/all_gather | solution.py:124
  11.4 66.5 %collective-permute-start.1 = (bf16[516,768]{1,0:T(8,128)(2,1)S(1)}, bf16[516,768]{1,0:T(8,128)(2,1)S(1)}, u32[]{:S(2)}, u32[]{:S(2)}) collective-permute-start(bf16[516,768]{1,0:T(8,128)(2,1)S(1)} %get-tuple-element.73), channel_id=1, source_target_pairs={{0,16},{16,32},{32,48},{48,0},{1,17},{17,33},{33,49},{49,1},{2,18}... | collective-permute-start | bytes 2377736 | tf_op jit(solution)/shard_map/ppermute | solution.py:22
  13.8 65.5 %collective-permute-start = (bf16[516,768]{1,0:T(8,128)(2,1)S(1)}, bf16[516,768]{1,0:T(8,128)(2,1)S(1)}, u32[]{:S(2)}, u32[]{:S(2)}) collective-permute-start(bf16[516,768]{1,0:T(8,128)(2,1)S(1)} %get-tuple-element.73), channel_id=1, source_target_pairs={{0,48},{16,0},{32,16},{48,32},{1,49},{17,1},{33,17},{49,33},{2,50}... | collective-permute-start | bytes 2377736 | tf_op jit(solution)/shard_map/ppermute | solution.py:23
  78.0 11.4 %collective-permute-start.2 = (bf16[258,768]{1,0:T(8,128)(2,1)S(1)}, bf16[258,768]{1,0:T(8,128)(2,1)S(1)}, u32[]{:S(2)}, u32[]{:S(2)}) collective-permute-start(bf16[258,768]{1,0:T(8,128)(2,1)S(1)} %slice.369), channel_id=1, source_target_pairs={{0,16},{16,32},{32,48},{48,0},{1,17},{17,33},{33,49},{49,1},{2,18}... | collective-permute-start | bytes 1188872 | tf_op jit(solution)/shard_map/ppermute | solution.py:25
  80.3 10.0 %collective-permute-start.3 = (bf16[258,768]{1,0:T(8,128)(2,1)}, bf16[258,768]{1,0:T(8,128)(2,1)S(1)}, u32[]{:S(2)}, u32[]{:S(2)}) collective-permute-start(bf16[258,768]{1,0:T(8,128)(2,1)} %slice.370), channel_id=1, source_target_pairs={{0,48},{16,0},{32,16},{48,32},{1,49},{17,1},{33,17},{49,33},{2,50}... | collective-permute-start | bytes 1188872 | tf_op jit(solution)/shard_map/ppermute | solution.py:26
  81.8 41.4 %collective-permute-start.5 = (bf16[1024,768]{1,0:T(8,128)(2,1)}, bf16[1024,768]{1,0:T(8,128)(2,1)}, u32[]{:S(2)}, u32[]{:S(2)}) collective-permute-start(bf16[1024,768]{1,0:T(8,128)(2,1)} %bitcast.20), channel_id=1, source_target_pairs={{0,16},{16,32},{32,48},{48,0},{1,17},{17,33},{33,49},{49,1},{2,18}... | collective-permute-start | bytes 4718600 | tf_op jit(solution)/shard_map/ppermute | solution.py:22
  81.8 43.5 %collective-permute-start.4 = (bf16[1024,768]{1,0:T(8,128)(2,1)}, bf16[1024,768]{1,0:T(8,128)(2,1)}, u32[]{:S(2)}, u32[]{:S(2)}) collective-permute-start(bf16[1024,768]{1,0:T(8,128)(2,1)} %bitcast.20), channel_id=1, source_target_pairs={{0,48},{16,0},{32,16},{48,32},{1,49},{17,1},{33,17},{49,33},{2,50}... | collective-permute-start | bytes 4718600 | tf_op jit(solution)/shard_map/ppermute | solution.py:23
  125.2 20.9 %collective-permute-start.6 = (bf16[512,768]{1,0:T(8,128)(2,1)}, bf16[512,768]{1,0:T(8,128)(2,1)}, u32[]{:S(2)}, u32[]{:S(2)}) collective-permute-start(bf16[512,768]{1,0:T(8,128)(2,1)} %slice.381), channel_id=1, source_target_pairs={{0,16},{16,32},{32,48},{48,0},{1,17},{17,33},{33,49},{49,1},{2,18}... | collective-permute-start | bytes 2359304 | tf_op jit(solution)/shard_map/ppermute | solution.py:25
  127.4 18.8 %collective-permute-start.7 = (bf16[512,768]{1,0:T(8,128)(2,1)}, bf16[512,768]{1,0:T(8,128)(2,1)}, u32[]{:S(2)}, u32[]{:S(2)}) collective-permute-start(bf16[512,768]{1,0:T(8,128)(2,1)} %slice.382), channel_id=1, source_target_pairs={{0,48},{16,0},{32,16},{48,32},{1,49},{17,1},{33,17},{49,33},{2,50}... | collective-permute-start | bytes 2359304 | tf_op jit(solution)/shard_map/ppermute | solution.py:26
  140.4 42.2 %collective-permute-start.10 = (bf16[3,3072,384]{1,2,0:T(8,128)(2,1)}, bf16[3,3072,384]{1,2,0:T(8,128)(2,1)}, u32[]{:S(2)}, u32[]{:S(2)}) collective-permute-start(bf16[3,3072,384]{1,2,0:T(8,128)(2,1)} %copy.48), channel_id=1, source_target_pairs={{0,64},{64,0},{1,65},{65,1},{2,66},{66,2},{3,67},{67,3},{4,68},{68... | collective-permute-start | bytes 21233672 | tf_op jit(solution)/shard_map/ppermute | solution.py:127
  216.2 67.5 %collective-permute-start.9 = (bf16[2,3072,384]{1,2,0:T(8,128)(2,1)}, bf16[2,3072,384]{1,2,0:T(8,128)(2,1)}, u32[]{:S(2)}, u32[]{:S(2)}) collective-permute-start(bf16[2,3072,384]{1,2,0:T(8,128)(2,1)} %copy.77), channel_id=1, source_target_pairs={{0,64},{64,0},{1,65},{65,1},{2,66},{66,2},{3,67},{67,3},{4,68},{68... | collective-permute-start | bytes 14155784 | tf_op jit(solution)/shard_map/ppermute | solution.py:130
  229.4 79.1 %collective-permute-start.8 = (bf16[3072,384]{1,0:T(8,128)(2,1)}, bf16[3072,384]{1,0:T(8,128)(2,1)}, u32[]{:S(2)}, u32[]{:S(2)}) collective-permute-start(bf16[3072,384]{1,0:T(8,128)(2,1)} %get-tuple-element.38), channel_id=1, source_target_pairs={{0,64},{64,0},{1,65},{65,1},{2,66},{66,2},{3,67},{67,3},{4,68},{68... | collective-permute-start | bytes 7077896 | tf_op jit(solution)/shard_map/ppermute | solution.py:130
  312.4 38.2 %collective-permute-start.11 = (bf16[384,768]{1,0:T(8,128)(2,1)}, bf16[384,768]{1,0:T(8,128)(2,1)}, u32[]{:S(2)}, u32[]{:S(2)}) collective-permute-start(bf16[384,768]{1,0:T(8,128)(2,1)} %pad_maximum_fusion.7), channel_id=1, source_target_pairs={{0,16},{16,32},{32,48},{48,0},{1,17},{17,33},{33,49},{49,1},{2,18}... | collective-permute-start | bytes 1769480 | tf_op jit(solution)/shard_map/ppermute | solution.py:40
  314.1 39.1 %collective-permute-start.12 = (bf16[384,768]{1,0:T(8,128)(2,1)}, bf16[384,768]{1,0:T(8,128)(2,1)}, u32[]{:S(2)}, u32[]{:S(2)}) collective-permute-start(bf16[384,768]{1,0:T(8,128)(2,1)} %pad_maximum_fusion.8), channel_id=1, source_target_pairs={{0,48},{16,0},{32,16},{48,32},{1,49},{17,1},{33,17},{49,33},{2,50}... | collective-permute-start | bytes 1769480 | tf_op jit(solution)/shard_map/ppermute | solution.py:43
  326.3 27.0 %collective-permute-start.15 = (bf16[384,768]{1,0:T(8,128)(2,1)}, bf16[384,768]{1,0:T(8,128)(2,1)}, u32[]{:S(2)}, u32[]{:S(2)}) collective-permute-start(bf16[384,768]{1,0:T(8,128)(2,1)} %pad_maximum_fusion.9), channel_id=1, source_target_pairs={{0,16},{16,32},{32,48},{48,0},{1,17},{17,33},{33,49},{49,1},{2,18}... | collective-permute-start | bytes 1769480 | tf_op jit(solution)/shard_map/ppermute | solution.py:40
  327.2 32.1 %collective-permute-start.16 = (bf16[384,768]{1,0:T(8,128)(2,1)}, bf16[384,768]{1,0:T(8,128)(2,1)}, u32[]{:S(2)}, u32[]{:S(2)}) collective-permute-start(bf16[384,768]{1,0:T(8,128)(2,1)} %pad_maximum_fusion.10), channel_id=1, source_target_pairs={{0,48},{16,0},{32,16},{48,32},{1,49},{17,1},{33,17},{49,33},{2,50}... | collective-permute-start | bytes 1769480 | tf_op jit(solution)/shard_map/ppermute | solution.py:43
  340.6 18.6 %collective-permute-start.19 = (bf16[384,768]{1,0:T(8,128)(2,1)}, bf16[384,768]{1,0:T(8,128)(2,1)}, u32[]{:S(2)}, u32[]{:S(2)}) collective-permute-start(bf16[384,768]{1,0:T(8,128)(2,1)} %pad_maximum_fusion.11), channel_id=1, source_target_pairs={{0,16},{16,32},{32,48},{48,0},{1,17},{17,33},{33,49},{49,1},{2,18}... | collective-permute-start | bytes 1769480 | tf_op jit(solution)/shard_map/ppermute | solution.py:40
  350.6 14.9 %collective-permute-start.20 = (bf16[384,768]{1,0:T(8,128)(2,1)S(1)}, bf16[384,768]{1,0:T(8,128)(2,1)S(1)}, u32[]{:S(2)}, u32[]{:S(2)}) collective-permute-start(bf16[384,768]{1,0:T(8,128)(2,1)S(1)} %pad_maximum_fusion.12), channel_id=1, source_target_pairs={{0,48},{16,0},{32,16},{48,32},{1,49},{17,1},{33,17},{49,33},{2,50}... | collective-permute-start | bytes 1769480 | tf_op jit(solution)/shard_map/ppermute | solution.py:43
  353.2 14.7 %collective-permute-start.23 = (bf16[384,768]{1,0:T(8,128)(2,1)S(1)}, bf16[384,768]{1,0:T(8,128)(2,1)S(1)}, u32[]{:S(2)}, u32[]{:S(2)}) collective-permute-start(bf16[384,768]{1,0:T(8,128)(2,1)S(1)} %pad_maximum_fusion.13), channel_id=1, source_target_pairs={{0,16},{16,32},{32,48},{48,0},{1,17},{17,33},{33,49},{49,1},{2,18}... | collective-permute-start | bytes 1769480 | tf_op jit(solution)/shard_map/ppermute | solution.py:40
  353.3 23.6 %collective-permute-start.24 = (bf16[384,768]{1,0:T(8,128)(2,1)S(1)}, bf16[384,768]{1,0:T(8,128)(2,1)S(1)}, u32[]{:S(2)}, u32[]{:S(2)}) collective-permute-start(bf16[384,768]{1,0:T(8,128)(2,1)S(1)} %pad_maximum_fusion.14), channel_id=1, source_target_pairs={{0,48},{16,0},{32,16},{48,32},{1,49},{17,1},{33,17},{49,33},{2,50}... | collective-permute-start | bytes 1769480 | tf_op jit(solution)/shard_map/ppermute | solution.py:43
  359.2 17.7 %collective-permute-start.13 = (bf16[128,768]{1,0:T(8,128)(2,1)}, bf16[128,768]{1,0:T(8,128)(2,1)}, u32[]{:S(2)}, u32[]{:S(2)}) collective-permute-start(bf16[128,768]{1,0:T(8,128)(2,1)} %slice.406), channel_id=1, source_target_pairs={{0,16},{16,32},{32,48},{48,0},{1,17},{17,33},{33,49},{49,1},{2,18}... | collective-permute-start | bytes 589832 | tf_op jit(solution)/shard_map/ppermute | solution.py:46
  359.2 22.0 %collective-permute-start.14 = (bf16[128,768]{1,0:T(8,128)(2,1)}, bf16[128,768]{1,0:T(8,128)(2,1)}, u32[]{:S(2)}, u32[]{:S(2)}) collective-permute-start(bf16[128,768]{1,0:T(8,128)(2,1)} %slice.407), channel_id=1, source_target_pairs={{0,48},{16,0},{32,16},{48,32},{1,49},{17,1},{33,17},{49,33},{2,50}... | collective-permute-start | bytes 589832 | tf_op jit(solution)/shard_map/ppermute | solution.py:47
  365.5 17.4 %collective-permute-start.17 = (bf16[128,768]{1,0:T(8,128)(2,1)S(1)}, bf16[128,768]{1,0:T(8,128)(2,1)S(1)}, u32[]{:S(2)}, u32[]{:S(2)}) collective-permute-start(bf16[128,768]{1,0:T(8,128)(2,1)S(1)} %slice.414), channel_id=1, source_target_pairs={{0,16},{16,32},{32,48},{48,0},{1,17},{17,33},{33,49},{49,1},{2,18}... | collective-permute-start | bytes 589832 | tf_op jit(solution)/shard_map/ppermute | solution.py:46
  367.9 18.4 %collective-permute-start.18 = (bf16[128,768]{1,0:T(8,128)(2,1)S(1)}, bf16[128,768]{1,0:T(8,128)(2,1)S(1)}, u32[]{:S(2)}, u32[]{:S(2)}) collective-permute-start(bf16[128,768]{1,0:T(8,128)(2,1)S(1)} %slice.415), channel_id=1, source_target_pairs={{0,48},{16,0},{32,16},{48,32},{1,49},{17,1},{33,17},{49,33},{2,50}... | collective-permute-start | bytes 589832 | tf_op jit(solution)/shard_map/ppermute | solution.py:47
  376.9 10.9 %collective-permute-start.21 = (bf16[128,768]{1,0:T(8,128)(2,1)S(1)}, bf16[128,768]{1,0:T(8,128)(2,1)S(1)}, u32[]{:S(2)}, u32[]{:S(2)}) collective-permute-start(bf16[128,768]{1,0:T(8,128)(2,1)S(1)} %slice.422), channel_id=1, source_target_pairs={{0,16},{16,32},{32,48},{48,0},{1,17},{17,33},{33,49},{49,1},{2,18}... | collective-permute-start | bytes 589832 | tf_op jit(solution)/shard_map/ppermute | solution.py:46
  376.9 12.6 %collective-permute-start.22 = (bf16[128,768]{1,0:T(8,128)(2,1)S(1)}, bf16[128,768]{1,0:T(8,128)(2,1)S(1)}, u32[]{:S(2)}, u32[]{:S(2)}) collective-permute-start(bf16[128,768]{1,0:T(8,128)(2,1)S(1)} %slice.423), channel_id=1, source_target_pairs={{0,48},{16,0},{32,16},{48,32},{1,49},{17,1},{33,17},{49,33},{2,50}... | collective-permute-start | bytes 589832 | tf_op jit(solution)/shard_map/ppermute | solution.py:47
  381.2 9.6 %collective-permute-start.25 = (bf16[128,768]{1,0:T(8,128)(2,1)S(1)}, bf16[128,768]{1,0:T(8,128)(2,1)S(1)}, u32[]{:S(2)}, u32[]{:S(2)}) collective-permute-start(bf16[128,768]{1,0:T(8,128)(2,1)S(1)} %slice.430), channel_id=1, source_target_pairs={{0,16},{16,32},{32,48},{48,0},{1,17},{17,33},{33,49},{49,1},{2,18}... | collective-permute-start | bytes 589832 | tf_op jit(solution)/shard_map/ppermute | solution.py:46
  382.8 10.9 %collective-permute-start.26 = (bf16[128,768]{1,0:T(8,128)(2,1)S(1)}, bf16[128,768]{1,0:T(8,128)(2,1)S(1)}, u32[]{:S(2)}, u32[]{:S(2)}) collective-permute-start(bf16[128,768]{1,0:T(8,128)(2,1)S(1)} %slice.431), channel_id=1, source_target_pairs={{0,48},{16,0},{32,16},{48,32},{1,49},{17,1},{33,17},{49,33},{2,50}... | collective-permute-start | bytes 589832 | tf_op jit(solution)/shard_map/ppermute | solution.py:47
  397.5 12.1 %collective-permute-start.27 = (f32[128,64]{0,1:T(8,128)S(1)}, f32[128,64]{0,1:T(8,128)S(1)}, u32[]{:S(2)}, u32[]{:S(2)}) collective-permute-start(f32[128,64]{0,1:T(8,128)S(1)} %bitcast.447), channel_id=1, source_target_pairs={{0,16},{16,32},{32,48},{48,64},{64,80},{80,96},{96,112},{112,0},{1... | collective-permute-start | bytes 98312 | tf_op jit(solution)/shard_map/ppermute | solution.py:186
  397.6 12.0 %collective-permute-start.28 = (f32[128,64]{0,1:T(8,128)S(1)}, f32[128,64]{0,1:T(8,128)S(1)}, u32[]{:S(2)}, u32[]{:S(2)}) collective-permute-start(f32[128,64]{0,1:T(8,128)S(1)} %bitcast.446), channel_id=1, source_target_pairs={{0,32},{16,48},{32,64},{48,80},{64,96},{80,112},{96,0},{112,16},{1... | collective-permute-start | bytes 98312 | tf_op jit(solution)/shard_map/ppermute | solution.py:186
  404.8 10.8 %collective-permute-start.29 = (f32[128,64]{0,1:T(8,128)S(1)}, f32[128,64]{0,1:T(8,128)S(1)}, u32[]{:S(2)}, u32[]{:S(2)}) collective-permute-start(f32[128,64]{0,1:T(8,128)S(1)} %bitcast.445), channel_id=1, source_target_pairs={{0,48},{16,64},{32,80},{48,96},{64,112},{80,0},{96,16},{112,32},{1... | collective-permute-start | bytes 98312 | tf_op jit(solution)/shard_map/ppermute | solution.py:186
  (54 other events, 326.0 us)
Sparse Core Ops, SparseCore 0:
  10.1 67.7 all-gather.2
  80.0 64.3 all-gather.4

commit v5 on v3

--- a/solution.py
+++ b/solution.py
@@ -123,10 +123,9 @@
     txt_w = txt_out_w[:2]
     out_w = txt_out_w[2]
     img_w_other = lax.ppermute(img_w, "cfg", swap)
-    txt_out_other = lax.ppermute(txt_out_w, "cfg", swap)
     halves = [
         (txt_w, img_w, out_w),
-        (txt_out_other[:2], img_w_other, txt_out_other[2]),
+        (lax.ppermute(txt_w, "cfg", swap), img_w_other, lax.ppermute(out_w, "cfg", swap)),
     ]
     positions = jnp.arange(text_slots + images, dtype=jnp.int32)
     usable = (positions < txt_len[0, 0]) | (positions >= text_slots)
@@ -175,14 +174,16 @@
     strength = guidance[0]
     share = jnp.where(core == 1, strength, 1.0 - strength)
     weighted = velocity * share
+    both = weighted + lax.ppermute(weighted, "cfg", [(0, 1), (1, 0)])
     n_pair = 2 * n_row
-    me_pair = core * n_row + me_row
-    rows_each = weighted.shape[0] // n_pair
-    velocity_blocks = weighted.reshape(n_pair, rows_each, weighted.shape[1])
-    guided = lax.dynamic_index_in_dim(velocity_blocks, me_pair, 0, keepdims=False)
-    for step in range(1, n_pair):
-        outgoing = lax.dynamic_index_in_dim(velocity_blocks, (me_pair + step) % n_pair, 0, keepdims=False)
-        guided = guided + lax.ppermute(outgoing, ("cfg", "row"), shift_pairs(n_pair, step))
+    rows_each = both.shape[0] // n_pair
+    velocity_blocks = both.reshape(n_pair, rows_each, both.shape[1])
+    guided = lax.dynamic_index_in_dim(velocity_blocks, core * n_row + me_row, 0, keepdims=False)
+    for step in range(1, n_row):
+        outgoing = lax.dynamic_index_in_dim(
+            velocity_blocks, core * n_row + (me_row + step) % n_row, 0, keepdims=False
+        )
+        guided = guided + lax.ppermute(outgoing, "row", shift_pairs(n_row, step))
     position_now = step_index[0]
     step_size = sigmas[position_now + 1] - sigmas[position_now]
     return (img_out[None, None], latent + step_size * guided[None])

time: 430 us -> 418 us (0.972)
  starting transfers between devices: 38.1 us -> 32.9 us
    unnamed x98 -> x104, local copies, waits for them, and re-layouts: 14.1 us -> 26.8 us
    all_gather x1 -> x0, local copies, waits for them, and re-layouts: 10.5 us -> none  [layer(): txt_out_w = lax.all_gather(txt_out_piece, 'col', axis=1, tiled=True)]
    ppermute x8 -> x6, starting transfers between devices: 9.6 us -> 4.38 us  [the longest x1 1.56 us: layer(): both = weighted + lax.ppermute(weighted, 'cfg', [(0, 1), (1, 0)])]
    slice x2 -> x0, local copies, waits for them, and re-layouts: 5.17 us -> none  [the longest x1 3.26 us: layer(): txt_out_other[2]]
    ppermute x2, waiting for transfers between devices: 30.9 us -> 26.3 us  [reduce_blocks(): lax.ppermute(jnp.concatenate([block(-1), far[cut:]], 0), axis_name, shift...]
    another operation x1 -> x0, local copies, waits for them, and re-layouts: 4.4 us -> none  [attend(): out_w.reshape(n_row, local_width, half)]
  transfers between devices with their start and end apart: 27 -> 25, of which waited for: 11 -> 12; matrix products, arithmetic and copies ran while one was open for 32% -> 41% of each run, Pallas kernels for 0% -> 0%
where the time goes in v5:
time: 418 us; the launch traced here: 411 us
  waiting for transfers between devices  159 us (38%)
  matrix products  93.8 us (22%)
  local copies, waits for them, and re-layouts  65.4 us (16%)
  other arithmetic  40.9 us (10%)
  starting transfers between devices  32.9 us (8%)
  between operations  18.7 us (4%)
    all_gather x1, waiting for transfers between devices, layer(): img_w = lax.all_gather(img_piece, 'col', axis=1, tiled=True)  67.2 us
    dot_general x4, matrix products, add_rows(): jnp.einsum('ti,sin->tsn', ready, piece, preferred_element_type=jnp.float32)  32.1 us
    dot_general x4, matrix products, attend(): jnp.einsum('qhe,khe->hqk', queries, key_rows, preferred_element_type=jnp....  31.9 us
    ppermute x2, waiting for transfers between devices, ring_gather(): from_prev = lax.ppermute(piece, axis_name, shift_pairs(size, 1))  29.7 us
    unnamed x104, local copies, waits for them, and re-layouts  26.8 us
    ppermute x2, waiting for transfers between devices, reduce_blocks(): lax.ppermute(jnp.concatenate([block(-1), far[cut:]], 0), axis_name, shift...  26.3 us
    ppermute x2, waiting for transfers between devices, ring_gather(): from_next = lax.ppermute(piece, axis_name, shift_pairs(size, -1))  16.3 us
    dot_general x4, matrix products, attend(): jnp.einsum('hqk,khe->qhe', chances, value_rows, preferred_element_type=jn...  16.1 us
  transfers between devices with their start and end apart: 25, of which 12 were waited for; matrix products, arithmetic and copies ran while one was open for 41% of the time, Pallas kernels for 0%

profile of v5, /device:TPU:1, one launch (start us, length us, event | category | flops | bytes accessed | tf_op | source)
XLA Modules:
  0.0 411.0 jit_solution(6526995887169573753)
XLA Ops:
  11.3 67.2 %all-gather.3.cloned.1.call-done = bf16[3,3072,384]{2,1,0:T(8,128)(2,1)} async-done(((bf16[3,192,384]{2,1,0:T(8,128)(2,1)}), bf16[3,3072,384]{2,1,0:T(8,128)(2,1)}) %all-gather.3.cloned.1.call-update) | async-done | bytes 7077904 | tf_op jit(solution)/shard_map/all_gather | solution.py:117
  82.2 16.3 %collective-permute-done = bf16[516,768]{1,0:T(8,128)(2,1)S(1)} collective-permute-done((bf16[516,768]{1,0:T(8,128)(2,1)S(1)}, bf16[516,768]{1,0:T(8,128)(2,1)S(1)}, u32[]{:S(2)}, u32[]{:S(2)}) %collective-permute-start) | collective-permute-done | bytes 792608 | tf_op jit(solution)/shard_map/ppermute | solution.py:23
  98.6 3.5 collective-permute-start.3
  105.7 3.5 collective-permute-done.3
  116.5 29.7 %collective-permute-done.5 = bf16[1024,768]{1,0:T(8,128)(2,1)} collective-permute-done((bf16[1024,768]{1,0:T(8,128)(2,1)}, bf16[1024,768]{1,0:T(8,128)(2,1)}, u32[]{:S(2)}, u32[]{:S(2)}) %collective-permute-start.5) | collective-permute-done | bytes 1572896 | tf_op jit(solution)/shard_map/ppermute | solution.py:22
  153.1 10.3 %copy.40 = bf16[3,3072,384]{1,2,0:T(8,128)(2,1)} copy(bf16[3,3072,384]{2,1,0:T(8,128)(2,1)} %all-gather.3.cloned.1.call-done) | data formatting | bytes 14155776 | tf_op jit(solution)/shard_map/optimization_barrier | solution.py:121
  163.3 3.6 collective-permute-start.10
  171.4 3.4 pad_maximum_fusion
  178.0 4.8 %fusion.14 = (bf16[1024,768]{1,0:T(8,128)(2,1)}, bf16[1024,768]{1,0:T(8,128)(2,1)}, bf16[1024,768]{1,0:T(8,128)(2,1)}, bf16[1024,768]{1,0:T(8,128)(2,1)}) fusion(f32[768]{0:T(1024)S(1)} %get-tuple-element.85, f32[768]{0:T(1024)S(1)} %get-tuple-element.86, f32[1024]{0:T(1024)S(1)} %add_rsqrt_fusion.6, f32[1024]{0:T(1024)S(1)} %add_multiply_fusion, ...), kind=kLoop, calls=%fused_computation.35 | loop fusion | flops 18874368 | bytes 12615696 | tf_op jit(solution)/shard_map/convert_element_type | solution.py:60
  182.9 11.5 %fusion.41 = f32[1024,3,384]{0,2,1:T(8,128)} fusion(bf16[3,3072,384]{2,1,0:T(8,128)(2,1)S(1)} %bitcast.330, bf16[1024,768]{1,0:T(8,128)(2,1)} %get-tuple-element.47, bf16[1024,768]{1,0:T(8,128)(2,1)} %get-tuple-element.46, bf16[1024,768]{1,0:T(8,128)(2,1)} %get-tuple-element.45, bf16[1024,768]{1,0:T(8,128)(2,1)} %get-tuple-element.44), kind=kOutput, calls=%fused_computation.65 | convolution fusion | flops 7272923136 | bytes 18087936 | tf_op jit(solution)/shard_map/ti,sin->tsn/dot_general | solution.py:72
  194.4 3.4 fusion.151
  206.6 10.6 %fusion.40 = f32[1024,3,384]{0,2,1:T(8,128)S(1)} fusion(bf16[3,3072,384]{1,2,0:T(8,128)(2,1)} %collective-permute-done.10, bf16[1024,768]{1,0:T(8,128)(2,1)S(1)} %copy-done.16, bf16[1024,768]{1,0:T(8,128)(2,1)S(1)} %copy-done.15, bf16[1024,768]{1,0:T(8,128)(2,1)S(1)} %copy-done.14, bf16[1024,768]{1,0:T(8,128)(2,1)S(1)} %copy-done.13), kind=kOutput, calls=%fused_computation.64 | convolution fusion | flops 7272923136 | bytes 18087936 | tf_op jit(solution)/shard_map/ti,sin->tsn/dot_general | solution.py:72
  223.3 4.9 %slice.299 = bf16[2,3072,384]{2,1,0:T(8,128)(2,1)} slice(bf16[3,3072,384]{2,1,0:T(8,128)(2,1)} %all-gather.5.cloned.1.call-done), slice={[0:2], [0:3072], [0:384]} | slice | bytes 9437184
  228.2 6.7 %copy.57 = bf16[2,3072,384]{1,2,0:T(8,128)(2,1)} copy(bf16[2,3072,384]{2,1,0:T(8,128)(2,1)} %slice.299) | data formatting | bytes 9437184
  241.4 5.0 %fusion.85 = f32[512,2,384]{0,2,1:T(8,128)S(1)} fusion(bf16[512,768]{1,0:T(8,128)(2,1)S(1)} %copy-done.27, bf16[512,768]{1,0:T(8,128)(2,1)S(1)} %copy-done.25, bf16[512,768]{1,0:T(8,128)(2,1)S(1)} %copy-done.23, bf16[512,768]{1,0:T(8,128)(2,1)S(1)} %copy-done.21, bf16[3,3072,384]{2,1,0:T(8,128)(2,1)} %all-gather.5.cloned.1.call-done), kind=kOutput, calls=%fused_computation.129 | convolution fusion | flops 2428502016 | bytes 9437184 | tf_op jit(solution)/shard_map/ti,sin->tsn/dot_general | solution.py:72
  247.9 3.5 slice_bitcast_fusion.4
  253.3 5.0 %fusion.101 = f32[3,512,1536]{2,1,0:T(8,128)} fusion(bf16[1024,3,128]{2,0,1:T(8,128)(2,1)S(1)} %copy-done.3, bf16[512,3,128]{2,0,1:T(8,128)(2,1)S(1)} %fusion.98, bf16[1024,3,128]{2,0,1:T(8,128)(2,1)S(1)} %copy-done.7), kind=kOutput, calls=%fused_computation.165 | convolution fusion | flops 606339072 | bytes 11010048 | tf_op jit(solution)/shard_map/qhe,khe->hqk/dot_general | solution.py:145
  258.4 5.0 %fusion.102 = f32[3,512,1536]{2,1,0:T(8,128)} fusion(bf16[1024,3,128]{2,0,1:T(8,128)(2,1)S(1)} %copy-done.3, bf16[512,3,128]{2,0,1:T(8,128)(2,1)S(1)} %fusion.98, bf16[1024,3,128]{2,0,1:T(8,128)(2,1)S(1)} %copy-done.7), kind=kOutput, calls=%fused_computation.166 | convolution fusion | flops 606339072 | bytes 11010048 | tf_op jit(solution)/shard_map/qhe,khe->hqk/dot_general | solution.py:145
  263.4 5.0 %fusion.84 = f32[512,2,384]{0,2,1:T(8,128)S(1)} fusion(bf16[2,3072,384]{1,2,0:T(8,128)(2,1)} %collective-permute-done.9, bf16[512,768]{1,0:T(8,128)(2,1)S(1)} %copy-done.28, bf16[512,768]{1,0:T(8,128)(2,1)S(1)} %copy-done.26, bf16[512,768]{1,0:T(8,128)(2,1)S(1)} %copy-done.24, bf16[512,768]{1,0:T(8,128)(2,1)S(1)} %copy-done.22), kind=kOutput, calls=%fused_computation.128 | convolution fusion | flops 2428502016 | bytes 9437184 | tf_op jit(solution)/shard_map/ti,sin->tsn/dot_general | solution.py:72
  273.3 5.0 %fusion.99 = f32[3,512,1536]{2,1,0:T(8,128)} fusion(bf16[1024,3,128]{2,0,1:T(8,128)(2,1)S(1)} %copy-done.9, bf16[512,3,128]{2,0,1:T(8,128)(2,1)S(1)} %fusion.96, bf16[1024,3,128]{2,0,1:T(8,128)(2,1)S(1)} %copy-done.10), kind=kOutput, calls=%fused_computation.163 | convolution fusion | flops 606339072 | bytes 11010048 | tf_op jit(solution)/shard_map/qhe,khe->hqk/dot_general | solution.py:145
  278.4 16.8 %fusion.1 = (f32[3,512]{1,0:T(4,128)S(1)}, f32[3,512]{1,0:T(4,128)S(1)}, f32[3,512]{1,0:T(4,128)S(1)}, f32[3,512]{1,0:T(4,128)S(1)}, f32[3,512,1536]{2,1,0:T(8,128)}) fusion(pred[1536]{0:T(1024)(128)(4,1)S(1)} %fusion.109, f32[3,512,1536]{2,1,0:T(8,128)} %fusion.101, f32[3,512,1536]{2,1,0:T(8,128)} %fusion.99, f32[3,512,1536]{2,1,0:T(8,128)} %fusion.102, ...), kind=kOutput, calls=%fused_computation.9 | convolution fusion | flops 634644480 | bytes 39348224 | tf_op jit(solution)/shard_map/qhe,khe->hqk/dot_general | solution.py:145
  295.2 5.3 %fusion.89 = bf16[3,128,512]{2,1,0:T(8,128)(2,1)S(1)} fusion(f32[3,512,1536]{2,1,0:T(8,128)} %fusion.102, f32[3,512]{1,0:T(4,128)S(1)} %get-tuple-element.41, pred[1536]{0:T(1024)(128)(4,1)S(1)} %fusion.109, bf16[1024,3,128]{0,2,1:T(8,128)(2,1)S(1)} %copy-done.30, bf16[512,3,128]{0,2,1:T(8,128)(2,1)S(1)} %fusion.103), kind=kOutput, calls=%fused_computation.133 | convolution fusion | flops 615972864 | bytes 11017728 | tf_op jit(solution)/shard_map/hqk,khe->qhe/dot_general | solution.py:150
  309.0 3.6 add_convert_fusion
  314.4 3.5 collective-permute-start.16
  320.0 5.5 %fusion.88 = bf16[3,128,512]{2,1,0:T(8,128)(2,1)S(1)} fusion(f32[3,512,1536]{2,1,0:T(8,128)} %get-tuple-element.82, f32[3,512]{1,0:T(4,128)S(1)} %get-tuple-element.38, pred[1536]{0:T(1024)(128)(4,1)S(1)} %fusion.109, bf16[1024,3,128]{0,2,1:T(8,128)(2,1)S(1)} %copy-done.29, bf16[512,3,128]{0,2,1:T(8,128)(2,1)S(1)} %fusion.104), kind=kOutput, calls=%fused_computation.132 | convolution fusion | flops 615972864 | bytes 11017728 | tf_op jit(solution)/shard_map/hqk,khe->qhe/dot_general | solution.py:150
  325.5 3.6 add_convert_fusion.1
  334.3 8.6 %collective-permute-done.16 = bf16[768,768]{1,0:T(8,128)(2,1)S(1)} collective-permute-done((bf16[768,768]{1,0:T(8,128)(2,1)S(1)}, bf16[768,768]{1,0:T(8,128)(2,1)S(1)}, u32[]{:S(2)}, u32[]{:S(2)}) %collective-permute-start.16) | collective-permute-done | bytes 1179680 | tf_op jit(solution)/shard_map/ppermute | solution.py:41
  344.7 3.4 collective-permute-start.18
  350.6 17.7 %collective-permute-done.12 = bf16[768,768]{1,0:T(8,128)(2,1)} collective-permute-done((bf16[768,768]{1,0:T(8,128)(2,1)}, bf16[768,768]{1,0:T(8,128)(2,1)}, u32[]{:S(2)}, u32[]{:S(2)}) %collective-permute-start.12) | collective-permute-done | bytes 1179680 | tf_op jit(solution)/shard_map/ppermute | solution.py:41
  369.3 3.5 collective-permute-start.14
  376.7 3.3 collective-permute-done.17
  398.8 3.5 fusion.37
  (221 shorter events, 106.0 us)
Async XLA Ops:
  7.2 71.3 %copy-start.35 = (bf16[1,1,2,768]{3,2,1,0:T(2,128)(2,1)S(1)}, bf16[1,1,2,768]{3,2,1,0:T(2,128)(2,1)}, u32[]{:S(2)}) copy-start(bf16[1,1,2,768]{3,2,1,0:T(2,128)(2,1)} %param.17) | copy-start | bytes 9220
  7.2 71.3 %copy-start.36 = (bf16[1,1,2,768]{3,2,1,0:T(2,128)(2,1)S(1)}, bf16[1,1,2,768]{3,2,1,0:T(2,128)(2,1)}, u32[]{:S(2)}) copy-start(bf16[1,1,2,768]{3,2,1,0:T(2,128)(2,1)} %param.16) | copy-start | bytes 9220
  7.2 71.3 %copy-start.31 = (bf16[1,1,512,768]{3,2,1,0:T(8,128)(2,1)S(1)}, bf16[1,1,512,768]{3,2,1,0:T(8,128)(2,1)}, u32[]{:S(2)}) copy-start(bf16[1,1,512,768]{3,2,1,0:T(8,128)(2,1)} %param.15) | copy-start | bytes 2359300
  7.2 71.3 %all-gather.3.cloned.1.call-start = ((), (), s32[]{:S(2)}) async-start(), calls=%async_computation | async-start | bytes 7520256 | tf_op jit(solution)/shard_map/all_gather | solution.py:117
  9.2 214.1 %all-gather.5.cloned.1.call-start = ((), (), s32[]{:S(2)}) async-start(), calls=%async_computation.1 | async-start | bytes 7520256 | tf_op jit(solution)/shard_map/all_gather | solution.py:122
  79.5 19.0 %collective-permute-start = (bf16[516,768]{1,0:T(8,128)(2,1)S(1)}, bf16[516,768]{1,0:T(8,128)(2,1)S(1)}, u32[]{:S(2)}, u32[]{:S(2)}) collective-permute-start(bf16[516,768]{1,0:T(8,128)(2,1)S(1)} %get-tuple-element.71), channel_id=1, source_target_pairs={{0,48},{16,0},{32,16},{48,32},{1,49},{17,1},{33,17},{49,33},{2,50}... | collective-permute-start | bytes 2377736 | tf_op jit(solution)/shard_map/ppermute | solution.py:23
  82.2 19.9 %collective-permute-start.1 = (bf16[516,768]{1,0:T(8,128)(2,1)S(1)}, bf16[516,768]{1,0:T(8,128)(2,1)S(1)}, u32[]{:S(2)}, u32[]{:S(2)}) collective-permute-start(bf16[516,768]{1,0:T(8,128)(2,1)S(1)} %get-tuple-element.71), channel_id=1, source_target_pairs={{0,16},{16,32},{32,48},{48,0},{1,17},{17,33},{33,49},{49,1},{2,18}... | collective-permute-start | bytes 2377736 | tf_op jit(solution)/shard_map/ppermute | solution.py:22
  98.6 10.5 %collective-permute-start.3 = (bf16[258,768]{1,0:T(8,128)(2,1)S(1)}, bf16[258,768]{1,0:T(8,128)(2,1)S(1)}, u32[]{:S(2)}, u32[]{:S(2)}) collective-permute-start(bf16[258,768]{1,0:T(8,128)(2,1)S(1)} %slice.290), channel_id=1, source_target_pairs={{0,48},{16,0},{32,16},{48,32},{1,49},{17,1},{33,17},{49,33},{2,50}... | collective-permute-start | bytes 1188872 | tf_op jit(solution)/shard_map/ppermute | solution.py:26
  102.1 10.2 %collective-permute-start.2 = (bf16[258,768]{1,0:T(8,128)(2,1)S(1)}, bf16[258,768]{1,0:T(8,128)(2,1)S(1)}, u32[]{:S(2)}, u32[]{:S(2)}) collective-permute-start(bf16[258,768]{1,0:T(8,128)(2,1)S(1)} %slice.289), channel_id=1, source_target_pairs={{0,16},{16,32},{32,48},{48,0},{1,17},{17,33},{33,49},{49,1},{2,18}... | collective-permute-start | bytes 1188872 | tf_op jit(solution)/shard_map/ppermute | solution.py:25
  102.2 44.0 %collective-permute-start.5 = (bf16[1024,768]{1,0:T(8,128)(2,1)}, bf16[1024,768]{1,0:T(8,128)(2,1)}, u32[]{:S(2)}, u32[]{:S(2)}) collective-permute-start(bf16[1024,768]{1,0:T(8,128)(2,1)} %bitcast.20), channel_id=1, source_target_pairs={{0,16},{16,32},{32,48},{48,0},{1,17},{17,33},{33,49},{49,1},{2,18}... | collective-permute-start | bytes 4718600 | tf_op jit(solution)/shard_map/ppermute | solution.py:22
  102.3 46.0 %collective-permute-start.4 = (bf16[1024,768]{1,0:T(8,128)(2,1)}, bf16[1024,768]{1,0:T(8,128)(2,1)}, u32[]{:S(2)}, u32[]{:S(2)}) collective-permute-start(bf16[1024,768]{1,0:T(8,128)(2,1)} %bitcast.20), channel_id=1, source_target_pairs={{0,48},{16,0},{32,16},{48,32},{1,49},{17,1},{33,17},{49,33},{2,50}... | collective-permute-start | bytes 4718600 | tf_op jit(solution)/shard_map/ppermute | solution.py:23
  148.3 21.7 %collective-permute-start.6 = (bf16[512,768]{1,0:T(8,128)(2,1)}, bf16[512,768]{1,0:T(8,128)(2,1)}, u32[]{:S(2)}, u32[]{:S(2)}) collective-permute-start(bf16[512,768]{1,0:T(8,128)(2,1)} %slice.301), channel_id=1, source_target_pairs={{0,16},{16,32},{32,48},{48,0},{1,17},{17,33},{33,49},{49,1},{2,18}... | collective-permute-start | bytes 2359304 | tf_op jit(solution)/shard_map/ppermute | solution.py:25
  150.3 19.6 %collective-permute-start.7 = (bf16[512,768]{1,0:T(8,128)(2,1)}, bf16[512,768]{1,0:T(8,128)(2,1)}, u32[]{:S(2)}, u32[]{:S(2)}) collective-permute-start(bf16[512,768]{1,0:T(8,128)(2,1)} %slice.302), channel_id=1, source_target_pairs={{0,48},{16,0},{32,16},{48,32},{1,49},{17,1},{33,17},{49,33},{2,50}... | collective-permute-start | bytes 2359304 | tf_op jit(solution)/shard_map/ppermute | solution.py:26
  163.3 43.2 %collective-permute-start.10 = (bf16[3,3072,384]{1,2,0:T(8,128)(2,1)}, bf16[3,3072,384]{1,2,0:T(8,128)(2,1)}, u32[]{:S(2)}, u32[]{:S(2)}) collective-permute-start(bf16[3,3072,384]{1,2,0:T(8,128)(2,1)} %copy.40), channel_id=1, source_target_pairs={{0,64},{64,0},{1,65},{65,1},{2,66},{66,2},{3,67},{67,3},{4,68},{68... | collective-permute-start | bytes 21233672 | tf_op jit(solution)/shard_map/ppermute | solution.py:125
  234.9 28.5 %collective-permute-start.9 = (bf16[2,3072,384]{1,2,0:T(8,128)(2,1)}, bf16[2,3072,384]{1,2,0:T(8,128)(2,1)}, u32[]{:S(2)}, u32[]{:S(2)}) collective-permute-start(bf16[2,3072,384]{1,2,0:T(8,128)(2,1)} %copy.57), channel_id=1, source_target_pairs={{0,64},{64,0},{1,65},{65,1},{2,66},{66,2},{3,67},{67,3},{4,68},{68... | collective-permute-start | bytes 14155784 | tf_op jit(solution)/shard_map/ppermute | solution.py:128
  251.4 57.6 %collective-permute-start.8 = (bf16[3072,384]{1,0:T(8,128)(2,1)}, bf16[3072,384]{1,0:T(8,128)(2,1)}, u32[]{:S(2)}, u32[]{:S(2)}) collective-permute-start(bf16[3072,384]{1,0:T(8,128)(2,1)} %get-tuple-element.42), channel_id=1, source_target_pairs={{0,64},{64,0},{1,65},{65,1},{2,66},{66,2},{3,67},{67,3},{4,68},{68... | collective-permute-start | bytes 7077896 | tf_op jit(solution)/shard_map/ppermute | solution.py:128
  278.4 16.8 %copy-start.30 = (bf16[1024,3,128]{0,2,1:T(8,128)(2,1)S(1)}, bf16[1024,3,128]{0,2,1:T(8,128)(2,1)}, u32[]{:S(2)}) copy-start(bf16[1024,3,128]{0,2,1:T(8,128)(2,1)} %fusion.93) | copy-start | bytes 2359300
  278.4 22.1 %slice-start = ((s8[9437184]{0:T(1024)(128)(4,1)}), s8[1048576]{0:T(1024)(128)(4,1)S(1)}, s32[]{:S(2)}) async-start(s8[9437184]{0:T(1024)(128)(4,1)} %bitcast.325), calls=%async_computation.2 | async-start | bytes 2097152
  278.4 22.1 %slice-start.1 = ((s8[9437184]{0:T(1024)(128)(4,1)}), s8[4194304]{0:T(1024)(128)(4,1)S(1)}, s32[]{:S(2)}) async-start(s8[9437184]{0:T(1024)(128)(4,1)} %bitcast.325), calls=%async_computation.3 | async-start | bytes 8388608
  314.4 28.5 %collective-permute-start.16 = (bf16[768,768]{1,0:T(8,128)(2,1)S(1)}, bf16[768,768]{1,0:T(8,128)(2,1)S(1)}, u32[]{:S(2)}, u32[]{:S(2)}) collective-permute-start(bf16[768,768]{1,0:T(8,128)(2,1)S(1)} %pad_maximum_fusion.9), channel_id=1, source_target_pairs={{0,48},{16,0},{32,16},{48,32},{1,49},{17,1},{33,17},{49,33},{2,50}... | collective-permute-start | bytes 3538952 | tf_op jit(solution)/shard_map/ppermute | solution.py:41
  318.0 30.1 %collective-permute-start.15 = (bf16[768,768]{1,0:T(8,128)(2,1)S(1)}, bf16[768,768]{1,0:T(8,128)(2,1)S(1)}, u32[]{:S(2)}, u32[]{:S(2)}) collective-permute-start(bf16[768,768]{1,0:T(8,128)(2,1)S(1)} %pad_maximum_fusion.8), channel_id=1, source_target_pairs={{0,16},{16,32},{32,48},{48,0},{1,17},{17,33},{33,49},{49,1},{2,18}... | collective-permute-start | bytes 3538952 | tf_op jit(solution)/shard_map/ppermute | solution.py:40
  330.5 37.9 %collective-permute-start.12 = (bf16[768,768]{1,0:T(8,128)(2,1)}, bf16[768,768]{1,0:T(8,128)(2,1)}, u32[]{:S(2)}, u32[]{:S(2)}) collective-permute-start(bf16[768,768]{1,0:T(8,128)(2,1)} %pad_maximum_fusion.7), channel_id=1, source_target_pairs={{0,48},{16,0},{32,16},{48,32},{1,49},{17,1},{33,17},{49,33},{2,50}... | collective-permute-start | bytes 3538952 | tf_op jit(solution)/shard_map/ppermute | solution.py:41
  333.1 40.8 %copy-start.34 = (bf16[1,1,768]{2,1,0:T(2,128)(2,1)S(1)}, bf16[1,1,768]{2,1,0:T(2,128)(2,1)}, u32[]{:S(2)}) copy-start(bf16[1,1,768]{2,1,0:T(2,128)(2,1)} %param.18) | copy-start | bytes 4612
  334.3 38.5 %collective-permute-start.11 = (bf16[768,768]{1,0:T(8,128)(2,1)}, bf16[768,768]{1,0:T(8,128)(2,1)}, u32[]{:S(2)}, u32[]{:S(2)}) collective-permute-start(bf16[768,768]{1,0:T(8,128)(2,1)} %pad_maximum_fusion.6), channel_id=1, source_target_pairs={{0,16},{16,32},{32,48},{48,0},{1,17},{17,33},{33,49},{49,1},{2,18}... | collective-permute-start | bytes 3538952 | tf_op jit(solution)/shard_map/ppermute | solution.py:40
  344.7 32.0 %collective-permute-start.18 = (bf16[256,768]{1,0:T(8,128)(2,1)}, bf16[256,768]{1,0:T(8,128)(2,1)S(1)}, u32[]{:S(2)}, u32[]{:S(2)}) collective-permute-start(bf16[256,768]{1,0:T(8,128)(2,1)} %slice.335), channel_id=1, source_target_pairs={{0,48},{16,0},{32,16},{48,32},{1,49},{17,1},{33,17},{49,33},{2,50}... | collective-permute-start | bytes 1179656 | tf_op jit(solution)/shard_map/ppermute | solution.py:45
  349.9 30.1 %collective-permute-start.17 = (bf16[256,768]{1,0:T(8,128)(2,1)}, bf16[256,768]{1,0:T(8,128)(2,1)}, u32[]{:S(2)}, u32[]{:S(2)}) collective-permute-start(bf16[256,768]{1,0:T(8,128)(2,1)} %slice.334), channel_id=1, source_target_pairs={{0,16},{16,32},{32,48},{48,0},{1,17},{17,33},{33,49},{49,1},{2,18}... | collective-permute-start | bytes 1179656 | tf_op jit(solution)/shard_map/ppermute | solution.py:44
  369.3 15.7 %collective-permute-start.14 = (bf16[256,768]{1,0:T(8,128)(2,1)S(1)}, bf16[256,768]{1,0:T(8,128)(2,1)S(1)}, u32[]{:S(2)}, u32[]{:S(2)}) collective-permute-start(bf16[256,768]{1,0:T(8,128)(2,1)S(1)} %slice.327), channel_id=1, source_target_pairs={{0,48},{16,0},{32,16},{48,32},{1,49},{17,1},{33,17},{49,33},{2,50}... | collective-permute-start | bytes 1179656 | tf_op jit(solution)/shard_map/ppermute | solution.py:45
  373.8 14.5 %collective-permute-start.13 = (bf16[256,768]{1,0:T(8,128)(2,1)S(1)}, bf16[256,768]{1,0:T(8,128)(2,1)S(1)}, u32[]{:S(2)}, u32[]{:S(2)}) collective-permute-start(bf16[256,768]{1,0:T(8,128)(2,1)S(1)} %slice.326), channel_id=1, source_target_pairs={{0,16},{16,32},{32,48},{48,0},{1,17},{17,33},{33,49},{49,1},{2,18}... | collective-permute-start | bytes 1179656 | tf_op jit(solution)/shard_map/ppermute | solution.py:44
  392.8 4.2 %collective-permute-start.19 = (f32[1024,64]{0,1:T(8,128)S(1)}, f32[1024,64]{0,1:T(8,128)S(1)}, u32[]{:S(2)}, u32[]{:S(2)}) collective-permute-start(f32[1024,64]{0,1:T(8,128)S(1)} %fusion.90), channel_id=1, source_target_pairs={{0,64},{64,0},{1,65},{65,1},{2,66},{66,2},{3,67},{67,3},{4,68},{68... | collective-permute-start | bytes 786440 | tf_op jit(solution)/shard_map/ppermute | solution.py:177
  397.2 5.0 %collective-permute-start.22 = (f32[128,64]{0,1:T(8,128)S(1)}, f32[128,64]{0,1:T(8,128)S(1)}, u32[]{:S(2)}, u32[]{:S(2)}) collective-permute-start(f32[128,64]{0,1:T(8,128)S(1)} %bitcast.353), channel_id=1, source_target_pairs={{0,48},{16,0},{32,16},{48,32},{1,49},{17,1},{33,17},{49,33},{2,50}... | collective-permute-start | bytes 98312 | tf_op jit(solution)/shard_map/ppermute | solution.py:186
  397.3 4.9 %collective-permute-start.20 = (f32[128,64]{0,1:T(8,128)S(1)}, f32[128,64]{0,1:T(8,128)S(1)}, u32[]{:S(2)}, u32[]{:S(2)}) collective-permute-start(f32[128,64]{0,1:T(8,128)S(1)} %bitcast.352), channel_id=1, source_target_pairs={{0,16},{16,32},{32,48},{48,0},{1,17},{17,33},{33,49},{49,1},{2,18}... | collective-permute-start | bytes 98312 | tf_op jit(solution)/shard_map/ppermute | solution.py:186
  398.8 4.3 %collective-permute-start.21 = (f32[128,64]{0,1:T(8,128)S(1)}, f32[128,64]{0,1:T(8,128)S(1)}, u32[]{:S(2)}, u32[]{:S(2)}) collective-permute-start(f32[128,64]{0,1:T(8,128)S(1)} %bitcast.351), channel_id=1, source_target_pairs={{0,32},{16,48},{32,0},{48,16},{1,33},{17,49},{33,1},{49,17},{2,34}... | collective-permute-start | bytes 98312 | tf_op jit(solution)/shard_map/ppermute | solution.py:186
  (40 other events, 174.8 us)
Sparse Core Ops, SparseCore 0:
  10.7 67.7 all-gather.2
  80.6 64.3 all-gather.4
